TPU v7x, 1024 devices: a whole 4x8x16 slice. The times are simulated.
1024 devices in a mesh: seq: 16 (over z_lo, core), head: 64 (over z_hi, x, y).
Axes of the slice: x: 4, y: 8, z: 16 (z_hi: 2, z_lo: 8; z = z_hi * 8 + z_lo), core: 2. Of those that a mesh axis runs over, the one named last changes fastest.
Arguments:
- queries: float32 [4096, 4096], P('seq', 'head'), may hold values from -50 to 50
- keys: float32 [4096, 4096], P('seq', 'head'), may hold values from -16 to 16
- values: float32 [4096, 4096], P('seq', 'head'), may hold values from -6 to 6
- local_span: int32 [32], replicated, may hold values from 1 to 2
- wo_local: float32 [4096, 4096], P('head'), may hold values from -0.1875 to 0.1875
- wo_strided: float32 [4096, 4096], P('head'), may hold values from -0.1875 to 0.1875
- grad_out: bfloat16 [4096, 4096], P('seq', 'head'), may hold values from -6 to 6
Outputs:
- mixed: float32 [4096, 4096], P('seq', 'head')
- grad_queries: float32 [4096, 4096], P('seq', 'head')
- grad_keys: float32 [4096, 4096], P('seq', 'head')
- grad_values: float32 [4096, 4096], P('seq', 'head')
All inputs are finite; a program needn't handle non-finite values.
Results may differ from a plain program's by a relative error of at most 0.0003.
Values may be sent and summed in bfloat16 or wider, within the bound.
No kernel may reach another device: no remote copies, remote signals or barrier semaphores. Data moves between devices by JAX's collectives and lax.ppermute only.
A program may use at most 32 MiB of HBM per device.

v0:
```python
import jax
import jax.numpy as jnp
from jax import lax
from jax.sharding import PartitionSpec as P

HDIM = 128
BLOCK = 128
GROUP_BLK = 2
STRIDE = 128


HIGHEST = lax.Precision.HIGHEST


def swapped(x, axis, distance):
    return lax.ppermute(x, axis, [(i, i ^ 1 << distance) for i in range(lax.axis_size(axis))])


def pair_sum(partial_value):
    return partial_value + swapped(partial_value, "head", 0)


def attend_forward(query_part, key_part, value_part, allowed):
    scale_factor = HDIM ** (-0.5)
    partial_value = jnp.einsum("bqhd,bkhd->bhqk", query_part, key_part, precision=HIGHEST)
    scores = pair_sum(partial_value) * scale_factor
    row_max = jnp.max(jnp.where(allowed, scores, -jnp.inf), axis=-1, keepdims=True)
    weights = jnp.where(allowed, jnp.exp(scores - row_max), 0.0)
    probs = weights / jnp.sum(weights, axis=-1, keepdims=True)
    attended = jnp.einsum("bhqk,bkhd->bqhd", probs, value_part, precision=HIGHEST)
    return (attended, probs)


def attend_backward(query_part, key_part, value_part, probs, attended, incoming):
    scale_factor = HDIM ** (-0.5)
    dprobs_part = jnp.einsum("bqhd,bkhd->bhqk", incoming, value_part, precision=HIGHEST)
    delta_part = jnp.transpose(jnp.sum(incoming * attended, axis=-1), (0, 2, 1))[..., None]
    joined = pair_sum(jnp.concatenate([dprobs_part, delta_part], axis=-1))
    dprobs = joined[..., :-1]
    row_delta = joined[..., -1:]
    dscores = probs * (dprobs - row_delta)
    grad_query = jnp.einsum("bhqk,bkhd->bqhd", dscores, key_part, precision=HIGHEST) * scale_factor
    grad_key = jnp.einsum("bhqk,bqhd->bkhd", dscores, query_part, precision=HIGHEST) * scale_factor
    grad_value = jnp.einsum("bhqk,bqhd->bkhd", probs, incoming, precision=HIGHEST)
    return (grad_query, grad_key, grad_value)


def to_strided(stacked):
    seq_devices = lax.axis_size("seq")
    tok_rows, members, head_dim = stacked.shape
    layout = stacked.reshape(tok_rows // seq_devices, seq_devices, members, head_dim)
    moved = lax.all_to_all(layout, "seq", split_axis=1, concat_axis=0, tiled=True)
    return moved.reshape(tok_rows, members, head_dim)


def to_contiguous(stacked):
    seq_devices = lax.axis_size("seq")
    tok_rows, members, head_dim = stacked.shape
    layout = stacked.reshape(seq_devices, tok_rows // seq_devices, 1, members, head_dim)
    moved = lax.all_to_all(layout, "seq", split_axis=0, concat_axis=2, tiled=True)
    return moved.reshape(tok_rows, members, head_dim)


def local(queries, keys, values, local_span, wo_local, wo_strided, grad_out):
    tok_rows, head_dim = queries.shape
    seq_devices = lax.axis_size("seq")
    per_run = STRIDE // seq_devices
    runs_here = tok_rows // per_run
    group_len = GROUP_BLK * BLOCK
    local_layout = (tok_rows // group_len, group_len, 1, head_dim)
    own_span = local_span[lax.axis_index("head") // 2]
    stacked = jnp.stack([queries, keys, values], axis=1)
    spread = to_strided(stacked)
    local_q = queries.reshape(local_layout)
    local_k = keys.reshape(local_layout)
    local_v = values.reshape(local_layout)
    position = jnp.arange(group_len)
    block_of = position // BLOCK
    causal = position[None, :] <= position[:, None]
    reach = block_of[:, None] - block_of[None, :] < own_span
    allowed_local = (causal & reach)[None, None]
    attn_local, probs_local = attend_forward(local_q, local_k, local_v, allowed_local)

    def to_runs(matrix):
        return matrix.reshape(runs_here, per_run, 1, head_dim).transpose(1, 0, 2, 3)

    def from_runs(arranged):
        return arranged.transpose(1, 0, 2, 3).reshape(tok_rows, head_dim)

    strided_q = to_runs(spread[:, 0])
    strided_k = to_runs(spread[:, 1])
    strided_v = to_runs(spread[:, 2])
    order = jnp.arange(runs_here)
    allowed_strided = (order[None, :] <= order[:, None])[None, None]
    attn_strided, probs_strided = attend_forward(strided_q, strided_k, strided_v, allowed_strided)
    strided_home = to_contiguous(from_runs(attn_strided)[:, None, :])[:, 0]
    attn_both = jnp.concatenate([attn_local.reshape(tok_rows, head_dim), strided_home], axis=1)
    wo_both = jnp.concatenate([wo_local, wo_strided], axis=0)
    w_cols = wo_both
    mixed_cols = lax.psum_scatter(
        lax.dot_general(
            w_cols,
            attn_both,
            (((0,), (1,)), ((), ())),
            precision=HIGHEST,
            preferred_element_type=jnp.float32,
        ),
        "head",
        scatter_dimension=0,
        tiled=True,
    )
    mixed = mixed_cols.T
    w_cols = wo_both
    grad_both = lax.dot_general(
        lax.all_gather(grad_out, "head", axis=1, tiled=True).astype(jnp.float32),
        w_cols,
        (((1,), (1,)), ((), ())),
        precision=HIGHEST,
        preferred_element_type=jnp.float32,
    )
    grad_local = grad_both[:, :head_dim]
    grad_strided = to_strided(grad_both[:, head_dim:][:, None, :])[:, 0]
    dq_local, dk_local, dv_local = attend_backward(
        local_q, local_k, local_v, probs_local, attn_local, grad_local.reshape(local_layout)
    )
    dq_strided, dk_strided, dv_strided = attend_backward(
        strided_q, strided_k, strided_v, probs_strided, attn_strided, to_runs(grad_strided)
    )
    strided_grads = jnp.stack(
        [from_runs(dq_strided), from_runs(dk_strided), from_runs(dv_strided)], axis=1
    )
    grads_home = to_contiguous(strided_grads)
    grad_queries = dq_local.reshape(tok_rows, head_dim) + grads_home[:, 0]
    grad_keys = dk_local.reshape(tok_rows, head_dim) + grads_home[:, 1]
    grad_values = dv_local.reshape(tok_rows, head_dim) + grads_home[:, 2]
    return (mixed, grad_queries, grad_keys, grad_values)


def solution(mesh):
    return jax.shard_map(
        local,
        mesh=mesh,
        in_specs=(
            P("seq", "head"),
            P("seq", "head"),
            P("seq", "head"),
            P(),
            P("head", None),
            P("head", None),
            P("seq", "head"),
        ),
        out_specs=(P("seq", "head"), P("seq", "head"), P("seq", "head"), P("seq", "head")),
        check_vma=False,
    )
```

profile of v0, /device:TPU:128, one launch (start us, length us, event | category | flops | bytes accessed | tf_op | source)
XLA Modules:
  0.0 859.0 jit_solution(7805840087700622424)
XLA Ops:
  7.2 0.7 all-gather.2.cloned.1.call-update
  7.9 0.9 copy.37
  8.9 0.9 copy.38
  9.8 0.9 copy.39
  10.9 0.9 reshape.266
  11.8 14.7 %all-to-all-start = ((f32[16,1,3072]{2,1,0:T(1,128)}), f32[16,1,3072]{2,1,0:T(1,128)S(1)}, u32[]{:S(2)}, u32[]{:S(2)}) async-start(f32[16,1,3072]{2,1,0:T(1,128)} %reshape.266), calls=%async_computation | async-start | bytes 393216 | tf_op jit(solution)/shard_map/all_to_all | solution.py:52
  26.6 0.4 convolution_bitcast_fusion.1
  27.0 3.2 collective-permute-start
  30.3 1.3 constant_dynamic-update-slice_fusion.1
  31.6 1.3 constant_dynamic-update-slice_fusion
  32.9 0.6 dynamic_slice.3
  33.5 3.8 collective-permute-done
  37.3 0.8 select_reduce_fusion
  38.3 0.5 broadcast.151
  38.8 1.1 reduce.7
  40.1 0.7 slice_bitcast_fusion.2
  41.1 3.2 collective-permute-start.1
  44.3 1.3 fusion.12
  45.6 3.3 collective-permute-done.1
  49.0 142.2 %all-gather.2.cloned.1.call-done = bf16[256,4096]{0,1:T(8,128)(2,1)} async-done(((bf16[256,64]{0,1:T(8,128)(2,1)}), bf16[256,4096]{0,1:T(8,128)(2,1)}) %all-gather.2.cloned.1.call-update) | async-done | bytes 2097168 | tf_op jit(solution)/shard_map/all_gather | solution.py:115
  191.2 2.7 convolution_bitcast_fusion.5
  194.1 0.8 reshape.270
  194.9 12.3 %all-to-all-start.2 = ((f32[16,1,1024]{2,1,0:T(1,128)}), f32[16,1,1024]{2,1,0:T(1,128)S(1)}, u32[]{:S(2)}, u32[]{:S(2)}) async-start(f32[16,1,1024]{2,1,0:T(1,128)} %reshape.270), calls=%async_computation.3 | async-start | bytes 131072 | tf_op jit(solution)/shard_map/all_to_all | solution.py:52
  207.3 8.1 all-to-all-done.2
  215.3 0.8 reduce.6
  216.2 1.4 fusion.19
  217.7 0.8 reshape.268
  218.5 6.8 all-to-all-start.1
  225.3 1.4 fusion.11
  226.8 1.1 fusion.43
  227.9 5.7 all-to-all-done.1
  233.6 1.6 reduce.8
  235.5 5.0 fusion.15
  240.5 0.9 copy-done
  241.8 2.5 collective-permute-start.3
  244.6 5.3 collective-permute-done.3
  250.0 0.4 fusion.1
  250.9 0.9 reshape.272
  251.8 5.8 all-to-all-start.3
  257.6 0.4 convolution_bitcast_fusion
  258.1 2.5 collective-permute-start.2
  260.6 7.9 collective-permute-done.2
  268.6 5.9 all-to-all-done.3
  274.5 1.1 reduce.9
  276.2 1.0 fusion.2
  277.2 1.0 fusion.3
  278.2 0.9 fusion.4
  279.2 573.0 %reduce-scatter.2.cloned.1.call-done = f32[64,256]{1,0:T(8,128)} async-done(((f32[4096,256]{1,0:T(8,128)}), f32[64,256]{1,0:T(8,128)}) %reduce-scatter.2.cloned.1.call-update) | async-done | bytes 65552 | tf_op jit(solution)/shard_map/reduce_scatter | solution.py:100
  (57 shorter events, 3.5 us)
Async XLA Ops:
  7.2 19.4 %copy-start.2 = (f32[256,64]{0,1:T(8,128)S(1)}, f32[256,64]{0,1:T(8,128)}, u32[]{:S(2)}) copy-start(f32[256,64]{0,1:T(8,128)} %param.7) | copy-start | bytes 196612
  7.2 19.4 %copy-start.4 = (f32[256,64]{0,1:T(8,128)S(1)}, f32[256,64]{0,1:T(8,128)}, u32[]{:S(2)}) copy-start(f32[256,64]{0,1:T(8,128)} %param.8) | copy-start | bytes 196612
  7.2 184.0 %all-gather.2.cloned.1.call-start = ((), (), s32[]{:S(2)}) async-start(), calls=%async_computation.6 | async-start | bytes 2129920 | tf_op jit(solution)/shard_map/all_gather | solution.py:115
  11.8 26.4 %all-to-all-start = ((f32[16,1,3072]{2,1,0:T(1,128)}), f32[16,1,3072]{2,1,0:T(1,128)S(1)}, u32[]{:S(2)}, u32[]{:S(2)}) async-start(f32[16,1,3072]{2,1,0:T(1,128)} %reshape.266), calls=%async_computation | async-start | bytes 393216 | tf_op jit(solution)/shard_map/all_to_all | solution.py:52
  27.0 5.9 copy-start.6
  27.0 10.3 %collective-permute-start = (f32[1,1,256,256]{2,3,1,0:T(8,128)S(1)}, f32[1,1,256,256]{2,3,1,0:T(8,128)S(1)}, u32[]{:S(2)}, u32[]{:S(2)}) collective-permute-start(f32[1,1,256,256]{2,3,1,0:T(8,128)S(1)} %convolution_bitcast_fusion.1), channel_id=1, source_target_pairs={{0,1},{1,0},{2,3},{3,2},{4,5},{5,4},{6,7},{7,6},{8,9},{9,8},{10,11... | collective-permute-start | bytes 786440 | tf_op jit(solution)/shard_map/ppermute | solution.py:16
  41.1 7.9 collective-permute-start.1
  194.9 20.5 %all-to-all-start.2 = ((f32[16,1,1024]{2,1,0:T(1,128)}), f32[16,1,1024]{2,1,0:T(1,128)S(1)}, u32[]{:S(2)}, u32[]{:S(2)}) async-start(f32[16,1,1024]{2,1,0:T(1,128)} %reshape.270), calls=%async_computation.3 | async-start | bytes 131072 | tf_op jit(solution)/shard_map/all_to_all | solution.py:52
  218.5 15.1 %all-to-all-start.1 = ((f32[16,1,1024]{2,1,0:T(1,128)}), f32[16,1,1024]{2,1,0:T(1,128)}, u32[]{:S(2)}, u32[]{:S(2)}) async-start(f32[16,1,1024]{2,1,0:T(1,128)} %reshape.268), calls=%async_computation.1 | async-start | bytes 131072 | tf_op jit(solution)/shard_map/all_to_all | solution.py:60
  225.3 626.9 %reduce-scatter.2.cloned.1.call-start = ((), (), s32[]{:S(2)}) async-start(), calls=%async_computation.5 | async-start | bytes 4259840 | tf_op jit(solution)/shard_map/reduce_scatter | solution.py:100
  240.5 0.9 copy-start
  241.8 8.2 collective-permute-start.3
  244.5 13.1 %copy-start.1 = (f32[256,64]{0,1:T(8,128)S(1)}, f32[256,64]{0,1:T(8,128)}, u32[]{:S(2)}) copy-start(f32[256,64]{0,1:T(8,128)} %param.9) | copy-start | bytes 196612
  251.8 22.7 %all-to-all-start.3 = ((f32[16,1,3072]{2,1,0:T(1,128)}), f32[16,1,3072]{2,1,0:T(1,128)S(1)}, u32[]{:S(2)}, u32[]{:S(2)}) async-start(f32[16,1,3072]{2,1,0:T(1,128)} %reshape.272), calls=%async_computation.4 | async-start | bytes 393216 | tf_op jit(solution)/shard_map/all_to_all | solution.py:60
  258.1 10.4 %collective-permute-start.2 = (f32[1,1,256,257]{2,3,1,0:T(8,128)S(1)}, f32[1,1,256,257]{2,3,1,0:T(8,128)S(1)}, u32[]{:S(2)}, u32[]{:S(2)}) collective-permute-start(f32[1,1,256,257]{2,3,1,0:T(8,128)S(1)} %pad_maximum_fusion.2), channel_id=1, source_target_pairs={{0,1},{1,0},{2,3},{3,2},{4,5},{5,4},{6,7},{7,6},{8,9},{9,8},{10,11... | collective-permute-start | bytes 789512 | tf_op jit(solution)/shard_map/ppermute | solution.py:16
  275.6 1.6 copy-start.3
  275.7 2.5 copy-start.5
Sparse Core Ops, SparseCore 0:
  13.8 177.3 all-gather.1
  240.6 611.4 reduce-scatter.1
where the time goes:
time: 860 us; the launch traced here: 859 us
  waiting for transfers between devices  756 us (88%)
  starting transfers between devices  51.1 us (6%)
  matrix products  15.7 us (2%)
  between operations  14.5 us (2%)
  local copies, waits for them, and re-layouts  13 us (2%)
    reduce_scatter x1, waiting for transfers between devices, local(): lax.psum_scatter(lax.dot_general(w_cols, attn_both, (((0,), (1,)), ((), (...  573 us
    all_gather x1, waiting for transfers between devices, local(): lax.all_gather(grad_out, 'head', axis=1, tiled=True).astype(jnp.float32)  142 us
    all_to_all x2, starting transfers between devices, to_strided(): lax.all_to_all(layout, 'seq', split_axis=1, concat_axis=0, tiled=True)  27 us
    ppermute x4, waiting for transfers between devices, swapped(): lax.ppermute(x, axis, [(i, i ^ 1 << distance) for i in range(lax.axis_siz...  20.3 us
  transfers between devices with their start and end apart: 10, of which 10 were waited for; matrix products, arithmetic and copies ran while one was open for 3% of the time, Pallas kernels for 0%

commit v1 on v0

--- a/solution.py
+++ b/solution.py
@@ -12,12 +12,33 @@
 HIGHEST = lax.Precision.HIGHEST
 
 
+HEAD_AXES = ("zh", "x", "y")
+
+
 def swapped(x, axis, distance):
     return lax.ppermute(x, axis, [(i, i ^ 1 << distance) for i in range(lax.axis_size(axis))])
 
 
 def pair_sum(partial_value):
-    return partial_value + swapped(partial_value, "head", 0)
+    return partial_value + swapped(partial_value, "y", 0)
+
+
+def head_index():
+    return (lax.axis_index("zh") * lax.axis_size("x") + lax.axis_index("x")) * lax.axis_size("y") + lax.axis_index("y")
+
+
+def scatter_head(partial_value):
+    sizes = [lax.axis_size(a) for a in HEAD_AXES]
+    rows, cols = partial_value.shape
+    block = rows // (sizes[0] * sizes[1] * sizes[2])
+    parts = partial_value.reshape(*sizes, block, cols)
+    for dim in (2, 1, 0):
+        parts = lax.all_to_all(parts, HEAD_AXES[dim], dim, dim, tiled=True).sum(dim)
+    return parts
+
+
+def gather_head(piece):
+    return lax.all_gather(piece, HEAD_AXES, axis=1, tiled=True)
 
 
 def attend_forward(query_part, key_part, value_part, allowed):
@@ -68,7 +89,7 @@
     runs_here = tok_rows // per_run
     group_len = GROUP_BLK * BLOCK
     local_layout = (tok_rows // group_len, group_len, 1, head_dim)
-    own_span = local_span[lax.axis_index("head") // 2]
+    own_span = local_span[head_index() // 2]
     stacked = jnp.stack([queries, keys, values], axis=1)
     spread = to_strided(stacked)
     local_q = queries.reshape(local_layout)
@@ -97,22 +118,19 @@
     attn_both = jnp.concatenate([attn_local.reshape(tok_rows, head_dim), strided_home], axis=1)
     wo_both = jnp.concatenate([wo_local, wo_strided], axis=0)
     w_cols = wo_both
-    mixed_cols = lax.psum_scatter(
+    mixed_cols = scatter_head(
         lax.dot_general(
             w_cols,
             attn_both,
             (((0,), (1,)), ((), ())),
             precision=HIGHEST,
             preferred_element_type=jnp.float32,
-        ),
-        "head",
-        scatter_dimension=0,
-        tiled=True,
+        )
     )
     mixed = mixed_cols.T
     w_cols = wo_both
     grad_both = lax.dot_general(
-        lax.all_gather(grad_out, "head", axis=1, tiled=True).astype(jnp.float32),
+        gather_head(grad_out).astype(jnp.float32),
         w_cols,
         (((1,), (1,)), ((), ())),
         precision=HIGHEST,
@@ -137,18 +155,22 @@
 
 
 def solution(mesh):
+    seq_size, head_size = mesh.devices.shape
+    zh = 2
+    xs = 4
+    view = jax.sharding.Mesh(mesh.devices.reshape(seq_size, zh, xs, head_size // (zh * xs)), ("seq",) + HEAD_AXES)
     return jax.shard_map(
         local,
-        mesh=mesh,
+        mesh=view,
         in_specs=(
-            P("seq", "head"),
-            P("seq", "head"),
-            P("seq", "head"),
+            P("seq", HEAD_AXES),
+            P("seq", HEAD_AXES),
+            P("seq", HEAD_AXES),
             P(),
-            P("head", None),
-            P("head", None),
-            P("seq", "head"),
+            P(HEAD_AXES, None),
+            P(HEAD_AXES, None),
+            P("seq", HEAD_AXES),
         ),
-        out_specs=(P("seq", "head"), P("seq", "head"), P("seq", "head"), P("seq", "head")),
+        out_specs=(P("seq", HEAD_AXES), P("seq", HEAD_AXES), P("seq", HEAD_AXES), P("seq", HEAD_AXES)),
         check_vma=False,
     )

time: 860 us -> 409 us (0.48)
  the two profiles are of different devices: /device:TPU:128 before, /device:TPU:1 now
where the time goes in v1:
time: 409 us; the launch traced here: 407 us
  waiting for transfers between devices  294 us (72%)
  starting transfers between devices  60 us (15%)
  local copies, waits for them, and re-layouts  14.6 us (4%)
  between operations  14.5 us (4%)
  matrix products  12.4 us (3%)
  other arithmetic  11.9 us (3%)
    all_gather x1, waiting for transfers between devices, gather_head(): return lax.all_gather(piece, HEAD_AXES, axis=1, tiled=True)  145 us
    ppermute x4, waiting for transfers between devices, swapped(): lax.ppermute(x, axis, [(i, i ^ 1 << distance) for i in range(lax.axis_siz...  101 us
    all_to_all x2, starting transfers between devices, to_strided(): lax.all_to_all(layout, 'seq', split_axis=1, concat_axis=0, tiled=True)  25 us
    all_to_all x3, waiting for transfers between devices, scatter_head(): parts = lax.all_to_all(parts, HEAD_AXES[dim], dim, dim, tiled=True).sum(dim)  18.5 us
    all_to_all x2, waiting for transfers between devices, to_contiguous(): lax.all_to_all(layout, 'seq', split_axis=0, concat_axis=2, tiled=True)  15.1 us
    all_to_all x3, starting transfers between devices, scatter_head(): parts = lax.all_to_all(parts, HEAD_AXES[dim], dim, dim, tiled=True).sum(dim)  14.6 us
    all_to_all x2, waiting for transfers between devices, to_strided(): lax.all_to_all(layout, 'seq', split_axis=1, concat_axis=0, tiled=True)  13.2 us
    ppermute x4, starting transfers between devices, swapped(): lax.ppermute(x, axis, [(i, i ^ 1 << distance) for i in range(lax.axis_siz...  11.4 us
  transfers between devices with their start and end apart: 12, of which 10 were waited for; matrix products, arithmetic and copies ran while one was open for 7% of the time, Pallas kernels for 0%

profile of v1, /device:TPU:1, one launch (start us, length us, event | category | flops | bytes accessed | tf_op | source)
XLA Modules:
  0.0 407.0 jit_solution(8278251424854171489)
XLA Ops:
  7.2 0.7 all-gather.2.cloned.1.call-update
  7.9 0.9 copy.92
  8.9 0.9 copy.93
  9.8 0.9 copy.94
  10.9 0.9 reshape.270
  11.8 17.5 %all-to-all-start = ((f32[16,1,3072]{2,1,0:T(1,128)}), f32[16,1,3072]{2,1,0:T(1,128)S(1)}, u32[]{:S(2)}, u32[]{:S(2)}) async-start(f32[16,1,3072]{2,1,0:T(1,128)} %reshape.270), calls=%async_computation | async-start | bytes 393216 | tf_op jit(solution)/shard_map/all_to_all | solution.py:73
  29.8 3.0 collective-permute-start
  32.8 1.3 constant_dynamic-update-slice_fusion.1
  34.1 1.3 constant_dynamic-update-slice_fusion
  36.0 3.3 collective-permute-done
  39.3 0.8 select_reduce_fusion
  40.1 0.8 fusion.12
  40.9 3.1 all-to-all-done
  44.5 1.1 reduce.7
  46.2 2.9 collective-permute-start.1
  49.2 0.8 fusion.11
  49.9 3.2 collective-permute-done.1
  53.2 145.5 %all-gather.2.cloned.1.call-done = bf16[256,4096]{0,1:T(8,128)(2,1)} async-done(((bf16[256,64]{0,1:T(8,128)(2,1)}), bf16[256,4096]{0,1:T(8,128)(2,1)}) %all-gather.2.cloned.1.call-update) | async-done | bytes 2097168 | tf_op jit(solution)/shard_map/all_gather | solution.py:41
  198.7 2.7 convolution_bitcast_fusion.5
  201.6 0.8 reshape.274
  202.3 7.6 %all-to-all-start.5 = ((f32[16,1,1024]{2,1,0:T(1,128)}), f32[16,1,1024]{2,1,0:T(1,128)S(1)}, u32[]{:S(2)}, u32[]{:S(2)}) async-start(f32[16,1,1024]{2,1,0:T(1,128)} %reshape.274), calls=%async_computation.5 | async-start | bytes 131072 | tf_op jit(solution)/shard_map/all_to_all | solution.py:73
  210.0 10.0 %all-to-all-done.5 = f32[16,1,1024]{2,1,0:T(1,128)S(1)} async-done(((f32[16,1,1024]{2,1,0:T(1,128)}), f32[16,1,1024]{2,1,0:T(1,128)S(1)}, u32[]{:S(2)}, u32[]{:S(2)}) %all-to-all-start.5) | async-done | bytes 65568 | tf_op jit(solution)/shard_map/all_to_all | solution.py:73
  220.0 0.8 reduce.6
  222.4 2.2 collective-permute-start.3
  225.1 0.8 reshape.272
  225.8 4.6 %all-to-all-start.1 = ((f32[16,1,1024]{2,1,0:T(1,128)}), f32[16,1,1024]{2,1,0:T(1,128)S(1)}, u32[]{:S(2)}, u32[]{:S(2)}) async-start(f32[16,1,1024]{2,1,0:T(1,128)} %reshape.272), calls=%async_computation.1 | async-start | bytes 131072 | tf_op jit(solution)/shard_map/all_to_all | solution.py:81
  230.4 0.9 fusion.49
  232.3 0.9 reshape.276
  233.2 7.4 %all-to-all-done.1 = f32[16,1,1024]{2,1,0:T(1,128)S(1)} async-done(((f32[16,1,1024]{2,1,0:T(1,128)}), f32[16,1,1024]{2,1,0:T(1,128)S(1)}, u32[]{:S(2)}, u32[]{:S(2)}) %all-to-all-start.1) | async-done | bytes 65568 | tf_op jit(solution)/shard_map/all_to_all | solution.py:81
  240.6 4.3 %all-to-all-start.6 = ((f32[16,1,3072]{2,1,0:T(1,128)}), f32[16,1,3072]{2,1,0:T(1,128)S(1)}, u32[]{:S(2)}, u32[]{:S(2)}) async-start(f32[16,1,3072]{2,1,0:T(1,128)} %reshape.276), calls=%async_computation.6 | async-start | bytes 393216 | tf_op jit(solution)/shard_map/all_to_all | solution.py:81
  245.1 0.8 reduce.8
  246.2 3.5 fusion.15
  249.7 2.2 copy.105
  251.9 7.7 %all-to-all-done.6 = f32[16,1,3072]{2,1,0:T(1,128)S(1)} async-done(((f32[16,1,3072]{2,1,0:T(1,128)}), f32[16,1,3072]{2,1,0:T(1,128)S(1)}, u32[]{:S(2)}, u32[]{:S(2)}) %all-to-all-start.6) | async-done | bytes 196640 | tf_op jit(solution)/shard_map/all_to_all | solution.py:81
  259.6 4.5 %all-to-all-start.2 = ((f32[2,4,8,64,256]{4,3,1,0,2:T(8,128)}), f32[2,4,8,64,256]{4,3,1,0,2:T(8,128)}, u32[]{:S(2)}, u32[]{:S(2)}) async-start(f32[2,4,8,64,256]{4,3,1,0,2:T(8,128)} %copy.105), calls=%async_computation.2 | async-start | bytes 8388608 | tf_op jit(solution)/shard_map/all_to_all | solution.py:36
  264.6 3.3 collective-permute-start.2
  267.9 94.1 %collective-permute-done.2 = f32[1,1,256,257]{2,3,1,0:T(8,128)S(1)} collective-permute-done((f32[1,1,256,257]{2,3,1,0:T(8,128)S(1)}, f32[1,1,256,257]{2,3,1,0:T(8,128)S(1)}, u32[]{:S(2)}, u32[]{:S(2)}) %collective-permute-start.2) | collective-permute-done | bytes 263200 | tf_op jit(solution)/shard_map/ppermute | solution.py:19
  362.1 1.1 reduce.9
  363.5 2.6 reduce_sum.65
  366.1 0.8 copy.106
  366.9 4.1 %all-to-all-start.3 = ((f32[2,4,64,256]{3,2,0,1:T(8,128)}), f32[2,4,64,256]{3,2,0,1:T(8,128)S(1)}, u32[]{:S(2)}, u32[]{:S(2)}) async-start(f32[2,4,64,256]{3,2,0,1:T(8,128)} %copy.106), calls=%async_computation.3 | async-start | bytes 1048576 | tf_op jit(solution)/shard_map/all_to_all | solution.py:36
  371.2 1.0 fusion.3
  372.2 7.7 %all-to-all-done.3 = f32[2,4,64,256]{3,2,0,1:T(8,128)S(1)} async-done(((f32[2,4,64,256]{3,2,0,1:T(8,128)}), f32[2,4,64,256]{3,2,0,1:T(8,128)S(1)}, u32[]{:S(2)}, u32[]{:S(2)}) %all-to-all-start.3) | async-done | bytes 524320 | tf_op jit(solution)/shard_map/all_to_all | solution.py:36
  379.9 0.7 reduce_sum.66
  380.6 6.0 %all-to-all-start.4 = ((f32[2,64,256]{2,1,0:T(8,128)}), f32[2,64,256]{2,1,0:T(8,128)S(1)}, u32[]{:S(2)}, u32[]{:S(2)}) async-start(f32[2,64,256]{2,1,0:T(8,128)} %reduce_sum.66), calls=%async_computation.4 | async-start | bytes 262144 | tf_op jit(solution)/shard_map/all_to_all | solution.py:36
  386.6 1.0 fusion.2
  387.7 0.9 fusion.4
  388.7 10.8 %all-to-all-done.4 = f32[2,64,256]{2,1,0:T(8,128)S(1)} async-done(((f32[2,64,256]{2,1,0:T(8,128)}), f32[2,64,256]{2,1,0:T(8,128)S(1)}, u32[]{:S(2)}, u32[]{:S(2)}) %all-to-all-start.4) | async-done | bytes 131104 | tf_op jit(solution)/shard_map/all_to_all | solution.py:36
  (63 shorter events, 7.6 us)
Async XLA Ops:
  7.2 22.1 %copy-start.1 = (f32[256,64]{0,1:T(8,128)S(1)}, f32[256,64]{0,1:T(8,128)}, u32[]{:S(2)}) copy-start(f32[256,64]{0,1:T(8,128)} %param.7) | copy-start | bytes 196612
  7.2 22.1 %copy-start.3 = (f32[256,64]{0,1:T(8,128)S(1)}, f32[256,64]{0,1:T(8,128)}, u32[]{:S(2)}) copy-start(f32[256,64]{0,1:T(8,128)} %param.8) | copy-start | bytes 196612
  7.2 191.5 %all-gather.2.cloned.1.call-start = ((), (), s32[]{:S(2)}) async-start(), calls=%async_computation.7 | async-start | bytes 2129920 | tf_op jit(solution)/shard_map/all_gather | solution.py:41
  11.8 32.2 %all-to-all-start = ((f32[16,1,3072]{2,1,0:T(1,128)}), f32[16,1,3072]{2,1,0:T(1,128)S(1)}, u32[]{:S(2)}, u32[]{:S(2)}) async-start(f32[16,1,3072]{2,1,0:T(1,128)} %reshape.270), calls=%async_computation | async-start | bytes 393216 | tf_op jit(solution)/shard_map/all_to_all | solution.py:73
  29.7 5.6 %copy-start.5 = (s32[32]{0:T(128)S(1)}, s32[32]{0:T(128)}, u32[]{:S(2)}) copy-start(s32[32]{0:T(128)} %param.10) | copy-start | bytes 388
  29.8 9.6 %collective-permute-start = (f32[1,1,256,256]{2,3,1,0:T(8,128)S(1)}, f32[1,1,256,256]{2,3,1,0:T(8,128)S(1)}, u32[]{:S(2)}, u32[]{:S(2)}) collective-permute-start(f32[1,1,256,256]{2,3,1,0:T(8,128)S(1)} %convolution_bitcast_fusion.1), channel_id=1, source_target_pairs={{0,1},{1,0},{2,3},{3,2},{4,5},{5,4},{6,7},{7,6},{8,9},{9,8},{10,11... | collective-permute-start | bytes 786440 | tf_op jit(solution)/shard_map/ppermute | solution.py:19
  46.2 6.9 %collective-permute-start.1 = (f32[8,1,32,32]{2,3,0,1:T(8,128)S(1)}, f32[8,1,32,32]{2,3,0,1:T(8,128)S(1)}, u32[]{:S(2)}, u32[]{:S(2)}) collective-permute-start(f32[8,1,32,32]{2,3,0,1:T(8,128)S(1)} %convolution_bitcast_fusion.4), channel_id=1, source_target_pairs={{0,1},{1,0},{2,3},{3,2},{4,5},{5,4},{6,7},{7,6},{8,9},{9,8},{10,11... | collective-permute-start | bytes 98312 | tf_op jit(solution)/shard_map/ppermute | solution.py:19
  202.3 17.7 %all-to-all-start.5 = ((f32[16,1,1024]{2,1,0:T(1,128)}), f32[16,1,1024]{2,1,0:T(1,128)S(1)}, u32[]{:S(2)}, u32[]{:S(2)}) async-start(f32[16,1,1024]{2,1,0:T(1,128)} %reshape.274), calls=%async_computation.5 | async-start | bytes 131072 | tf_op jit(solution)/shard_map/all_to_all | solution.py:73
  222.4 8.0 %collective-permute-start.3 = (f32[8,1,32,33]{2,3,0,1:T(8,128)}, f32[8,1,32,33]{2,3,0,1:T(8,128)}, u32[]{:S(2)}, u32[]{:S(2)}) collective-permute-start(f32[8,1,32,33]{2,3,0,1:T(8,128)} %pad_maximum_fusion.3), channel_id=1, source_target_pairs={{0,1},{1,0},{2,3},{3,2},{4,5},{5,4},{6,7},{7,6},{8,9},{9,8},{10,11... | collective-permute-start | bytes 101384 | tf_op jit(solution)/shard_map/ppermute | solution.py:19
  225.1 19.8 %copy-start = (f32[256,64]{0,1:T(8,128)S(1)}, f32[256,64]{0,1:T(8,128)}, u32[]{:S(2)}) copy-start(f32[256,64]{0,1:T(8,128)} %param.9) | copy-start | bytes 196612
  225.8 14.7 %all-to-all-start.1 = ((f32[16,1,1024]{2,1,0:T(1,128)}), f32[16,1,1024]{2,1,0:T(1,128)S(1)}, u32[]{:S(2)}, u32[]{:S(2)}) async-start(f32[16,1,1024]{2,1,0:T(1,128)} %reshape.272), calls=%async_computation.1 | async-start | bytes 131072 | tf_op jit(solution)/shard_map/all_to_all | solution.py:81
  240.6 19.0 %all-to-all-start.6 = ((f32[16,1,3072]{2,1,0:T(1,128)}), f32[16,1,3072]{2,1,0:T(1,128)S(1)}, u32[]{:S(2)}, u32[]{:S(2)}) async-start(f32[16,1,3072]{2,1,0:T(1,128)} %reshape.276), calls=%async_computation.6 | async-start | bytes 393216 | tf_op jit(solution)/shard_map/all_to_all | solution.py:81
  259.6 103.9 %all-to-all-start.2 = ((f32[2,4,8,64,256]{4,3,1,0,2:T(8,128)}), f32[2,4,8,64,256]{4,3,1,0,2:T(8,128)}, u32[]{:S(2)}, u32[]{:S(2)}) async-start(f32[2,4,8,64,256]{4,3,1,0,2:T(8,128)} %copy.105), calls=%async_computation.2 | async-start | bytes 8388608 | tf_op jit(solution)/shard_map/all_to_all | solution.py:36
  264.6 97.4 %collective-permute-start.2 = (f32[1,1,256,257]{2,3,1,0:T(8,128)S(1)}, f32[1,1,256,257]{2,3,1,0:T(8,128)S(1)}, u32[]{:S(2)}, u32[]{:S(2)}) collective-permute-start(f32[1,1,256,257]{2,3,1,0:T(8,128)S(1)} %pad_maximum_fusion.2), channel_id=1, source_target_pairs={{0,1},{1,0},{2,3},{3,2},{4,5},{5,4},{6,7},{7,6},{8,9},{9,8},{10,11... | collective-permute-start | bytes 789512 | tf_op jit(solution)/shard_map/ppermute | solution.py:19
  366.1 5.1 %copy-start.2 = (f32[256,64]{0,1:T(8,128)S(1)}, f32[256,64]{0,1:T(8,128)}, u32[]{:S(2)}) copy-start(f32[256,64]{0,1:T(8,128)} %param.7) | copy-start | bytes 196612
  366.9 20.8 %copy-start.4 = (f32[256,64]{0,1:T(8,128)S(1)}, f32[256,64]{0,1:T(8,128)}, u32[]{:S(2)}) copy-start(f32[256,64]{0,1:T(8,128)} %param.8) | copy-start | bytes 196612
  366.9 13.0 %all-to-all-start.3 = ((f32[2,4,64,256]{3,2,0,1:T(8,128)}), f32[2,4,64,256]{3,2,0,1:T(8,128)S(1)}, u32[]{:S(2)}, u32[]{:S(2)}) async-start(f32[2,4,64,256]{3,2,0,1:T(8,128)} %copy.106), calls=%async_computation.3 | async-start | bytes 1048576 | tf_op jit(solution)/shard_map/all_to_all | solution.py:36
  380.6 18.9 %all-to-all-start.4 = ((f32[2,64,256]{2,1,0:T(8,128)}), f32[2,64,256]{2,1,0:T(8,128)S(1)}, u32[]{:S(2)}, u32[]{:S(2)}) async-start(f32[2,64,256]{2,1,0:T(8,128)} %reduce_sum.66), calls=%async_computation.4 | async-start | bytes 262144 | tf_op jit(solution)/shard_map/all_to_all | solution.py:36
Sparse Core Ops, SparseCore 0:
  13.8 184.7 all-gather.1

commit v2 on v1

--- a/solution.py
+++ b/solution.py
@@ -27,14 +27,16 @@
     return (lax.axis_index("zh") * lax.axis_size("x") + lax.axis_index("x")) * lax.axis_size("y") + lax.axis_index("y")
 
 
-def scatter_head(partial_value):
+def scatter_head(partial_value, companion):
     sizes = [lax.axis_size(a) for a in HEAD_AXES]
     rows, cols = partial_value.shape
     block = rows // (sizes[0] * sizes[1] * sizes[2])
     parts = partial_value.reshape(*sizes, block, cols)
     for dim in (2, 1, 0):
         parts = lax.all_to_all(parts, HEAD_AXES[dim], dim, dim, tiled=True).sum(dim)
-    return parts
+        if dim == 2:
+            parts, companion = lax.optimization_barrier((parts, companion))
+    return parts, companion
 
 
 def gather_head(piece):
@@ -118,19 +120,20 @@
     attn_both = jnp.concatenate([attn_local.reshape(tok_rows, head_dim), strided_home], axis=1)
     wo_both = jnp.concatenate([wo_local, wo_strided], axis=0)
     w_cols = wo_both
-    mixed_cols = scatter_head(
+    mixed_cols, grad_rows = scatter_head(
         lax.dot_general(
             w_cols,
             attn_both,
             (((0,), (1,)), ((), ())),
             precision=HIGHEST,
             preferred_element_type=jnp.float32,
-        )
+        ),
+        gather_head(grad_out),
     )
     mixed = mixed_cols.T
     w_cols = wo_both
     grad_both = lax.dot_general(
-        gather_head(grad_out).astype(jnp.float32),
+        grad_rows.astype(jnp.float32),
         w_cols,
         (((1,), (1,)), ((), ())),
         precision=HIGHEST,

time: 409 us -> 369 us (0.902)
  waiting for transfers between devices: 294 us -> 248 us
  starting transfers between devices: 60 us -> 66 us
    all_to_all x3, waiting for transfers between devices: 18.5 us -> 108 us  [scatter_head(): parts = lax.all_to_all(parts, HEAD_AXES[dim], dim, dim, tiled=True).sum(dim)]
    ppermute x4, waiting for transfers between devices: 101 us -> 14.7 us  [swapped(): lax.ppermute(x, axis, [(i, i ^ 1 << distance) for i in range(lax.axis_siz...]
    all_gather x1, waiting for transfers between devices: 145 us -> 92.6 us  [gather_head(): return lax.all_gather(piece, HEAD_AXES, axis=1, tiled=True)]
    all_to_all x2, waiting for transfers between devices: 13.2 us -> 19.9 us  [to_strided(): lax.all_to_all(layout, 'seq', split_axis=1, concat_axis=0, tiled=True)]
    all_to_all x2, starting transfers between devices: 8.87 us -> 14.6 us  [to_contiguous(): lax.all_to_all(layout, 'seq', split_axis=0, concat_axis=2, tiled=True)]
  transfers between devices with their start and end apart: 12 -> 12, of which waited for: 10 -> 11; matrix products, arithmetic and copies ran while one was open for 7% -> 5% of each run, Pallas kernels for 0% -> 0%
where the time goes in v2:
time: 369 us; the launch traced here: 368 us
  waiting for transfers between devices  248 us (67%)
  starting transfers between devices  66 us (18%)
  local copies, waits for them, and re-layouts  14.6 us (4%)
  between operations  14.5 us (4%)
  matrix products  14 us (4%)
  other arithmetic  11.3 us (3%)
    all_to_all x3, waiting for transfers between devices, scatter_head(): parts = lax.all_to_all(parts, HEAD_AXES[dim], dim, dim, tiled=True).sum(dim)  108 us
    all_gather x1, waiting for transfers between devices, gather_head(): return lax.all_gather(piece, HEAD_AXES, axis=1, tiled=True)  92.6 us
    all_to_all x2, starting transfers between devices, to_strided(): lax.all_to_all(layout, 'seq', split_axis=1, concat_axis=0, tiled=True)  24.2 us
    all_to_all x2, waiting for transfers between devices, to_strided(): lax.all_to_all(layout, 'seq', split_axis=1, concat_axis=0, tiled=True)  19.9 us
    all_to_all x3, starting transfers between devices, scatter_head(): parts = lax.all_to_all(parts, HEAD_AXES[dim], dim, dim, tiled=True).sum(dim)  16.2 us
    ppermute x4, waiting for transfers between devices, swapped(): lax.ppermute(x, axis, [(i, i ^ 1 << distance) for i in range(lax.axis_siz...  14.7 us
    all_to_all x2, starting transfers between devices, to_contiguous(): lax.all_to_all(layout, 'seq', split_axis=0, concat_axis=2, tiled=True)  14.6 us
    all_to_all x2, waiting for transfers between devices, to_contiguous(): lax.all_to_all(layout, 'seq', split_axis=0, concat_axis=2, tiled=True)  11.8 us
  transfers between devices with their start and end apart: 12, of which 11 were waited for; matrix products, arithmetic and copies ran while one was open for 5% of the time, Pallas kernels for 0%

profile of v2, /device:TPU:1, one launch (start us, length us, event | category | flops | bytes accessed | tf_op | source)
XLA Modules:
  0.0 368.1 jit_solution(10702214480085197232)
XLA Ops:
  7.2 1.3 convolution_bitcast_fusion.1
  8.5 4.0 %collective-permute-start = (f32[1,1,256,256]{2,3,1,0:T(8,128)S(1)}, f32[1,1,256,256]{2,3,1,0:T(8,128)S(1)}, u32[]{:S(2)}, u32[]{:S(2)}) collective-permute-start(f32[1,1,256,256]{2,3,1,0:T(8,128)S(1)} %convolution_bitcast_fusion.1), channel_id=1, source_target_pairs={{0,1},{1,0},{2,3},{3,2},{4,5},{5,4},{6,7},{7,6},{8,9},{9,8},{10,11... | collective-permute-start | bytes 786440 | tf_op jit(solution)/shard_map/ppermute | solution.py:19
  12.5 0.9 copy.92
  13.4 0.9 copy.93
  14.4 0.9 copy.94
  15.5 0.9 reshape.270
  16.4 16.7 %all-to-all-start = ((f32[16,1,3072]{2,1,0:T(1,128)}), f32[16,1,3072]{2,1,0:T(1,128)S(1)}, u32[]{:S(2)}, u32[]{:S(2)}) async-start(f32[16,1,3072]{2,1,0:T(1,128)} %reshape.270), calls=%async_computation | async-start | bytes 393216 | tf_op jit(solution)/shard_map/all_to_all | solution.py:75
  33.1 1.3 constant_dynamic-update-slice_fusion.1
  34.4 1.3 constant_dynamic-update-slice_fusion
  36.3 0.8 select_reduce_fusion
  37.1 10.6 %all-to-all-done = f32[16,1,3072]{2,1,0:T(1,128)S(1)} async-done(((f32[16,1,3072]{2,1,0:T(1,128)}), f32[16,1,3072]{2,1,0:T(1,128)S(1)}, u32[]{:S(2)}, u32[]{:S(2)}) %all-to-all-start) | async-done | bytes 196640 | tf_op jit(solution)/shard_map/all_to_all | solution.py:75
  48.3 1.1 reduce.6
  50.0 2.4 collective-permute-start.1
  52.3 0.8 fusion.12
  53.1 3.3 collective-permute-done.1
  57.0 0.8 reshape.272
  57.8 6.0 %all-to-all-start.1 = ((f32[16,1,1024]{2,1,0:T(1,128)}), f32[16,1,1024]{2,1,0:T(1,128)}, u32[]{:S(2)}, u32[]{:S(2)}) async-start(f32[16,1,1024]{2,1,0:T(1,128)} %reshape.272), calls=%async_computation.1 | async-start | bytes 131072 | tf_op jit(solution)/shard_map/all_to_all | solution.py:83
  63.8 0.8 fusion.11
  64.6 1.1 fusion.8
  65.7 8.3 %all-to-all-done.1 = f32[16,1,1024]{2,1,0:T(1,128)} async-done(((f32[16,1,1024]{2,1,0:T(1,128)}), f32[16,1,1024]{2,1,0:T(1,128)}, u32[]{:S(2)}, u32[]{:S(2)}) %all-to-all-start.1) | async-done | bytes 65568 | tf_op jit(solution)/shard_map/all_to_all | solution.py:83
  74.0 1.6 reduce.7
  75.9 3.5 fusion.15
  79.3 2.3 copy.105
  81.6 5.9 %all-to-all-start.2 = ((f32[2,4,8,64,256]{4,3,1,0,2:T(8,128)}), f32[2,4,8,64,256]{4,3,1,0,2:T(8,128)}, u32[]{:S(2)}, u32[]{:S(2)}) async-start(f32[2,4,8,64,256]{4,3,1,0,2:T(8,128)} %copy.105), calls=%async_computation.2 | async-start | bytes 8388608 | tf_op jit(solution)/shard_map/all_to_all | solution.py:36
  87.6 0.7 all-gather.2.cloned.1.call-update
  88.3 97.6 %all-to-all-done.2 = f32[2,4,8,64,256]{4,3,1,0,2:T(8,128)} async-done(((f32[2,4,8,64,256]{4,3,1,0,2:T(8,128)}), f32[2,4,8,64,256]{4,3,1,0,2:T(8,128)}, u32[]{:S(2)}, u32[]{:S(2)}) %all-to-all-start.2) | async-done | bytes 4194336 | tf_op jit(solution)/shard_map/all_to_all | solution.py:36
  185.8 2.5 reduce_sum.65
  188.4 92.6 %all-gather.2.cloned.1.call-done = bf16[256,4096]{0,1:T(8,128)(2,1)} async-done(((bf16[256,64]{0,1:T(8,128)(2,1)}), bf16[256,4096]{0,1:T(8,128)(2,1)}) %all-gather.2.cloned.1.call-update) | async-done | bytes 2097168 | tf_op jit(solution)/shard_map/all_gather | solution.py:43
  280.9 2.7 fusion.52
  283.8 0.8 reshape.274
  284.6 7.6 %all-to-all-start.5 = ((f32[16,1,1024]{2,1,0:T(1,128)}), f32[16,1,1024]{2,1,0:T(1,128)S(1)}, u32[]{:S(2)}, u32[]{:S(2)}) async-start(f32[16,1,1024]{2,1,0:T(1,128)} %reshape.274), calls=%async_computation.5 | async-start | bytes 131072 | tf_op jit(solution)/shard_map/all_to_all | solution.py:75
  292.2 0.8 copy.106
  293.0 9.3 %all-to-all-done.5 = f32[16,1,1024]{2,1,0:T(1,128)S(1)} async-done(((f32[16,1,1024]{2,1,0:T(1,128)}), f32[16,1,1024]{2,1,0:T(1,128)S(1)}, u32[]{:S(2)}, u32[]{:S(2)}) %all-to-all-start.5) | async-done | bytes 65568 | tf_op jit(solution)/shard_map/all_to_all | solution.py:75
  302.3 4.0 %all-to-all-start.3 = ((f32[2,4,64,256]{3,2,0,1:T(8,128)}), f32[2,4,64,256]{3,2,0,1:T(8,128)S(1)}, u32[]{:S(2)}, u32[]{:S(2)}) async-start(f32[2,4,64,256]{3,2,0,1:T(8,128)} %copy.106), calls=%async_computation.3 | async-start | bytes 1048576 | tf_op jit(solution)/shard_map/all_to_all | solution.py:36
  306.3 0.8 reduce.8
  307.7 2.3 collective-permute-start.3
  310.4 3.7 collective-permute-done.3
  314.9 6.3 %all-to-all-start.4 = ((f32[2,64,256]{2,1,0:T(8,128)}), f32[2,64,256]{2,1,0:T(8,128)S(1)}, u32[]{:S(2)}, u32[]{:S(2)}) async-start(f32[2,64,256]{2,1,0:T(8,128)} %reduce_sum.66), calls=%async_computation.4 | async-start | bytes 262144 | tf_op jit(solution)/shard_map/all_to_all | solution.py:36
  322.1 0.9 reshape.276
  323.0 10.3 %all-to-all-done.4 = f32[2,64,256]{2,1,0:T(8,128)S(1)} async-done(((f32[2,64,256]{2,1,0:T(8,128)}), f32[2,64,256]{2,1,0:T(8,128)S(1)}, u32[]{:S(2)}, u32[]{:S(2)}) %all-to-all-start.4) | async-done | bytes 131104 | tf_op jit(solution)/shard_map/all_to_all | solution.py:36
  333.2 8.7 %all-to-all-start.6 = ((f32[16,1,3072]{2,1,0:T(1,128)}), f32[16,1,3072]{2,1,0:T(1,128)S(1)}, u32[]{:S(2)}, u32[]{:S(2)}) async-start(f32[16,1,3072]{2,1,0:T(1,128)} %reshape.276), calls=%async_computation.6 | async-start | bytes 393216 | tf_op jit(solution)/shard_map/all_to_all | solution.py:83
  342.4 2.2 collective-permute-start.2
  344.6 7.7 %collective-permute-done.2 = f32[1,1,256,257]{2,3,1,0:T(8,128)S(1)} collective-permute-done((f32[1,1,256,257]{2,3,1,0:T(8,128)S(1)}, f32[1,1,256,257]{2,3,1,0:T(8,128)S(1)}, u32[]{:S(2)}, u32[]{:S(2)}) %collective-permute-start.2) | collective-permute-done | bytes 263200 | tf_op jit(solution)/shard_map/ppermute | solution.py:19
  353.0 3.5 all-to-all-done.6
  356.6 1.1 reduce.9
  358.1 1.0 fusion.2
  359.3 1.0 fusion.3
  360.3 0.9 fusion.4
  (69 shorter events, 7.2 us)
Async XLA Ops:
  8.5 27.9 %collective-permute-start = (f32[1,1,256,256]{2,3,1,0:T(8,128)S(1)}, f32[1,1,256,256]{2,3,1,0:T(8,128)S(1)}, u32[]{:S(2)}, u32[]{:S(2)}) collective-permute-start(f32[1,1,256,256]{2,3,1,0:T(8,128)S(1)} %convolution_bitcast_fusion.1), channel_id=1, source_target_pairs={{0,1},{1,0},{2,3},{3,2},{4,5},{5,4},{6,7},{7,6},{8,9},{9,8},{10,11... | collective-permute-start | bytes 786440 | tf_op jit(solution)/shard_map/ppermute | solution.py:19
  16.4 31.3 %all-to-all-start = ((f32[16,1,3072]{2,1,0:T(1,128)}), f32[16,1,3072]{2,1,0:T(1,128)S(1)}, u32[]{:S(2)}, u32[]{:S(2)}) async-start(f32[16,1,3072]{2,1,0:T(1,128)} %reshape.270), calls=%async_computation | async-start | bytes 393216 | tf_op jit(solution)/shard_map/all_to_all | solution.py:75
  33.1 2.6 copy-start.7
  49.6 7.0 %copy-start = (f32[32,8,1,64]{3,1,0,2:T(8,128)}, f32[32,8,1,64]{3,1,0,2:T(8,128)S(1)}, u32[]{:S(2)}) copy-start(f32[32,8,1,64]{3,1,0,2:T(8,128)S(1)} %get-tuple-element.12) | copy-start | bytes 196612
  50.0 6.4 %collective-permute-start.1 = (f32[8,1,32,32]{2,3,0,1:T(8,128)S(1)}, f32[8,1,32,32]{2,3,0,1:T(8,128)S(1)}, u32[]{:S(2)}, u32[]{:S(2)}) collective-permute-start(f32[8,1,32,32]{2,3,0,1:T(8,128)S(1)} %convolution_bitcast_fusion.4), channel_id=1, source_target_pairs={{0,1},{1,0},{2,3},{3,2},{4,5},{5,4},{6,7},{7,6},{8,9},{9,8},{10,11... | collective-permute-start | bytes 98312 | tf_op jit(solution)/shard_map/ppermute | solution.py:19
  57.8 16.2 %all-to-all-start.1 = ((f32[16,1,1024]{2,1,0:T(1,128)}), f32[16,1,1024]{2,1,0:T(1,128)}, u32[]{:S(2)}, u32[]{:S(2)}) async-start(f32[16,1,1024]{2,1,0:T(1,128)} %reshape.272), calls=%async_computation.1 | async-start | bytes 131072 | tf_op jit(solution)/shard_map/all_to_all | solution.py:83
  65.7 13.6 %copy-start.2 = (f32[256,64]{0,1:T(8,128)}, f32[256,64]{0,1:T(8,128)S(1)}, u32[]{:S(2)}) copy-start(f32[256,64]{0,1:T(8,128)S(1)} %fusion.8) | copy-start | bytes 196612
  81.6 104.2 %all-to-all-start.2 = ((f32[2,4,8,64,256]{4,3,1,0,2:T(8,128)}), f32[2,4,8,64,256]{4,3,1,0,2:T(8,128)}, u32[]{:S(2)}, u32[]{:S(2)}) async-start(f32[2,4,8,64,256]{4,3,1,0,2:T(8,128)} %copy.105), calls=%async_computation.2 | async-start | bytes 8388608 | tf_op jit(solution)/shard_map/all_to_all | solution.py:36
  87.5 193.4 %all-gather.2.cloned.1.call-start = ((), (), s32[]{:S(2)}) async-start(), calls=%async_computation.7 | async-start | bytes 2129920 | tf_op jit(solution)/shard_map/all_gather | solution.py:43
  284.6 17.7 %all-to-all-start.5 = ((f32[16,1,1024]{2,1,0:T(1,128)}), f32[16,1,1024]{2,1,0:T(1,128)S(1)}, u32[]{:S(2)}, u32[]{:S(2)}) async-start(f32[16,1,1024]{2,1,0:T(1,128)} %reshape.274), calls=%async_computation.5 | async-start | bytes 131072 | tf_op jit(solution)/shard_map/all_to_all | solution.py:75
  293.0 28.2 %copy-start.1 = (f32[32,8,1,64]{3,1,0,2:T(8,128)S(1)}, f32[32,8,1,64]{3,1,0,2:T(8,128)}, u32[]{:S(2)}) copy-start(f32[32,8,1,64]{3,1,0,2:T(8,128)} %copy-done) | copy-start | bytes 196612
  302.3 11.9 %all-to-all-start.3 = ((f32[2,4,64,256]{3,2,0,1:T(8,128)}), f32[2,4,64,256]{3,2,0,1:T(8,128)S(1)}, u32[]{:S(2)}, u32[]{:S(2)}) async-start(f32[2,4,64,256]{3,2,0,1:T(8,128)} %copy.106), calls=%async_computation.3 | async-start | bytes 1048576 | tf_op jit(solution)/shard_map/all_to_all | solution.py:36
  307.7 6.4 %collective-permute-start.3 = (f32[8,1,32,33]{2,3,0,1:T(8,128)S(1)}, f32[8,1,32,33]{2,3,0,1:T(8,128)S(1)}, u32[]{:S(2)}, u32[]{:S(2)}) collective-permute-start(f32[8,1,32,33]{2,3,0,1:T(8,128)S(1)} %pad_maximum_fusion.3), channel_id=1, source_target_pairs={{0,1},{1,0},{2,3},{3,2},{4,5},{5,4},{6,7},{7,6},{8,9},{9,8},{10,11... | collective-permute-start | bytes 101384 | tf_op jit(solution)/shard_map/ppermute | solution.py:19
  314.1 27.8 %copy-start.4 = (f32[256,64]{0,1:T(8,128)S(1)}, f32[256,64]{0,1:T(8,128)}, u32[]{:S(2)}) copy-start(f32[256,64]{0,1:T(8,128)} %param.9) | copy-start | bytes 196612
  314.9 27.4 %copy-start.3 = (f32[256,64]{0,1:T(8,128)S(1)}, f32[256,64]{0,1:T(8,128)}, u32[]{:S(2)}) copy-start(f32[256,64]{0,1:T(8,128)} %copy-done.2) | copy-start | bytes 196612
  314.9 18.3 %all-to-all-start.4 = ((f32[2,64,256]{2,1,0:T(8,128)}), f32[2,64,256]{2,1,0:T(8,128)S(1)}, u32[]{:S(2)}, u32[]{:S(2)}) async-start(f32[2,64,256]{2,1,0:T(8,128)} %reduce_sum.66), calls=%async_computation.4 | async-start | bytes 262144 | tf_op jit(solution)/shard_map/all_to_all | solution.py:36
  333.2 23.3 %all-to-all-start.6 = ((f32[16,1,3072]{2,1,0:T(1,128)}), f32[16,1,3072]{2,1,0:T(1,128)S(1)}, u32[]{:S(2)}, u32[]{:S(2)}) async-start(f32[16,1,3072]{2,1,0:T(1,128)} %reshape.276), calls=%async_computation.6 | async-start | bytes 393216 | tf_op jit(solution)/shard_map/all_to_all | solution.py:83
  342.4 9.9 %collective-permute-start.2 = (f32[1,1,256,257]{2,3,1,0:T(8,128)S(1)}, f32[1,1,256,257]{2,3,1,0:T(8,128)S(1)}, u32[]{:S(2)}, u32[]{:S(2)}) collective-permute-start(f32[1,1,256,257]{2,3,1,0:T(8,128)S(1)} %pad_maximum_fusion.2), channel_id=1, source_target_pairs={{0,1},{1,0},{2,3},{3,2},{4,5},{5,4},{6,7},{7,6},{8,9},{9,8},{10,11... | collective-permute-start | bytes 789512 | tf_op jit(solution)/shard_map/ppermute | solution.py:19
  357.7 1.6 copy-start.5
  357.8 2.5 copy-start.6
Sparse Core Ops, SparseCore 0:
  94.2 186.7 all-gather.1

commit v3 on v2

--- a/solution.py
+++ b/solution.py
@@ -32,10 +32,10 @@
     rows, cols = partial_value.shape
     block = rows // (sizes[0] * sizes[1] * sizes[2])
     parts = partial_value.reshape(*sizes, block, cols)
-    for dim in (2, 1, 0):
-        parts = lax.all_to_all(parts, HEAD_AXES[dim], dim, dim, tiled=True).sum(dim)
-        if dim == 2:
-            parts, companion = lax.optimization_barrier((parts, companion))
+    parts = lax.all_to_all(parts, "x", 1, 1, tiled=True).sum(1)
+    parts, companion = lax.optimization_barrier((parts, companion))
+    for dim in (1, 0):
+        parts = lax.all_to_all(parts, HEAD_AXES[2 * dim], dim, dim, tiled=True).sum(dim)
     return parts, companion
 
 

time: 369 us -> 335 us (0.908)
  waiting for transfers between devices: 248 us -> 159 us
  blocking collectives: 0 us -> 68.5 us
  starting transfers between devices: 66 us -> 51.2 us
    all_to_all x3 -> x2, waiting for transfers between devices: 108 us -> 10.1 us  [scatter_head(): lax.all_to_all(parts, HEAD_AXES[2 * dim], dim, dim, tiled=True).sum(dim)]
    all_to_all x0 -> x2, blocking collectives: none -> 68.5 us  [the longest x1 51.6 us: scatter_head(): parts = lax.all_to_all(parts, 'x', 1, 1, tiled=True).sum(1)]
    ppermute x4, waiting for transfers between devices: 14.7 us -> 33.6 us  [swapped(): lax.ppermute(x, axis, [(i, i ^ 1 << distance) for i in range(lax.axis_siz...]
    all_to_all x2, waiting for transfers between devices: 11.8 us -> 23.2 us  [to_contiguous(): lax.all_to_all(layout, 'seq', split_axis=0, concat_axis=2, tiled=True)]
    all_gather x1, waiting for transfers between devices: 92.6 us -> 81.3 us  [gather_head(): return lax.all_gather(piece, HEAD_AXES, axis=1, tiled=True)]
    all_to_all x2 -> x1, waiting for transfers between devices: 19.9 us -> 9.89 us  [to_strided(): lax.all_to_all(layout, 'seq', split_axis=1, concat_axis=0, tiled=True)]
    all_to_all x2 -> x1, starting transfers between devices: 24.2 us -> 16.7 us  [to_strided(): lax.all_to_all(layout, 'seq', split_axis=1, concat_axis=0, tiled=True)]
    all_to_all x3 -> x2, starting transfers between devices: 16.2 us -> 10.7 us  [scatter_head(): lax.all_to_all(parts, HEAD_AXES[2 * dim], dim, dim, tiled=True).sum(dim)]
  transfers between devices with their start and end apart: 12 -> 10, of which waited for: 11 -> 8; matrix products, arithmetic and copies ran while one was open for 5% -> 8% of each run, Pallas kernels for 0% -> 0%
where the time goes in v3:
time: 335 us; the launch traced here: 332 us
  waiting for transfers between devices  159 us (47%)
  blocking collectives  68.5 us (20%)
  starting transfers between devices  51.2 us (15%)
  between operations  14.7 us (4%)
  matrix products  14.1 us (4%)
  local copies, waits for them, and re-layouts  13.1 us (4%)
  other arithmetic  11.4 us (3%)
    all_gather x1, waiting for transfers between devices, gather_head(): return lax.all_gather(piece, HEAD_AXES, axis=1, tiled=True)  81.3 us
    all_to_all x1, blocking collectives, scatter_head(): parts = lax.all_to_all(parts, 'x', 1, 1, tiled=True).sum(1)  51.6 us
    ppermute x4, waiting for transfers between devices, swapped(): lax.ppermute(x, axis, [(i, i ^ 1 << distance) for i in range(lax.axis_siz...  33.6 us
    all_to_all x2, waiting for transfers between devices, to_contiguous(): lax.all_to_all(layout, 'seq', split_axis=0, concat_axis=2, tiled=True)  23.2 us
    all_to_all x1, blocking collectives, to_strided(): lax.all_to_all(layout, 'seq', split_axis=1, concat_axis=0, tiled=True)  16.8 us
    all_to_all x1, starting transfers between devices, to_strided(): lax.all_to_all(layout, 'seq', split_axis=1, concat_axis=0, tiled=True)  16.7 us
    ppermute x4, starting transfers between devices, swapped(): lax.ppermute(x, axis, [(i, i ^ 1 << distance) for i in range(lax.axis_siz...  12.3 us
    all_to_all x2, starting transfers between devices, to_contiguous(): lax.all_to_all(layout, 'seq', split_axis=0, concat_axis=2, tiled=True)  11.5 us
  transfers between devices with their start and end apart: 10, of which 8 were waited for; matrix products, arithmetic and copies ran while one was open for 8% of the time, Pallas kernels for 0%

profile of v3, /device:TPU:1, one launch (start us, length us, event | category | flops | bytes accessed | tf_op | source)
XLA Modules:
  0.0 331.7 jit_solution(9764091191786310084)
XLA Ops:
  7.2 1.3 convolution_bitcast_fusion.1
  8.5 4.0 %collective-permute-start = (f32[1,1,256,256]{2,3,1,0:T(8,128)S(1)}, f32[1,1,256,256]{2,3,1,0:T(8,128)S(1)}, u32[]{:S(2)}, u32[]{:S(2)}) collective-permute-start(f32[1,1,256,256]{2,3,1,0:T(8,128)S(1)} %convolution_bitcast_fusion.1), channel_id=1, source_target_pairs={{0,1},{1,0},{2,3},{3,2},{4,5},{5,4},{6,7},{7,6},{8,9},{9,8},{10,11... | collective-permute-start | bytes 786440 | tf_op jit(solution)/shard_map/ppermute | solution.py:19
  12.5 0.9 copy.92
  13.4 0.9 copy.93
  14.4 0.9 copy.94
  15.5 0.9 reshape.270
  16.4 16.7 %all-to-all-start = ((f32[16,1,3072]{2,1,0:T(1,128)}), f32[16,1,3072]{2,1,0:T(1,128)S(1)}, u32[]{:S(2)}, u32[]{:S(2)}) async-start(f32[16,1,3072]{2,1,0:T(1,128)} %reshape.270), calls=%async_computation | async-start | bytes 393216 | tf_op jit(solution)/shard_map/all_to_all | solution.py:75
  33.1 0.7 all-gather.2.cloned.1.call-update
  33.8 1.3 constant_dynamic-update-slice_fusion.1
  35.1 1.3 constant_dynamic-update-slice_fusion
  37.1 0.8 select_reduce_fusion
  37.9 9.9 %all-to-all-done = f32[16,1,3072]{2,1,0:T(1,128)S(1)} async-done(((f32[16,1,3072]{2,1,0:T(1,128)}), f32[16,1,3072]{2,1,0:T(1,128)S(1)}, u32[]{:S(2)}, u32[]{:S(2)}) %all-to-all-start) | async-done | bytes 196640 | tf_op jit(solution)/shard_map/all_to_all | solution.py:75
  48.3 1.1 reduce.6
  50.0 2.4 collective-permute-start.1
  52.4 0.8 fusion.12
  53.2 3.3 collective-permute-done.1
  57.1 0.8 reshape.272
  57.9 6.0 %all-to-all-start.1 = ((f32[16,1,1024]{2,1,0:T(1,128)}), f32[16,1,1024]{2,1,0:T(1,128)S(1)}, u32[]{:S(2)}, u32[]{:S(2)}) async-start(f32[16,1,1024]{2,1,0:T(1,128)} %reshape.272), calls=%async_computation.1 | async-start | bytes 131072 | tf_op jit(solution)/shard_map/all_to_all | solution.py:83
  63.8 0.8 fusion.11
  64.9 9.6 %all-to-all-done.1 = f32[16,1,1024]{2,1,0:T(1,128)S(1)} async-done(((f32[16,1,1024]{2,1,0:T(1,128)}), f32[16,1,1024]{2,1,0:T(1,128)S(1)}, u32[]{:S(2)}, u32[]{:S(2)}) %all-to-all-start.1) | async-done | bytes 65568 | tf_op jit(solution)/shard_map/all_to_all | solution.py:83
  74.5 0.8 reduce.7
  75.6 3.5 %fusion.15 = f32[4096,256]{1,0:T(8,128)S(1)} fusion(f32[128,4096]{1,0:T(8,128)S(1)} %constant_dynamic-update-slice_fusion, f32[256,64]{0,1:T(8,128)S(1)} %copy.104, f32[256,64]{0,1:T(8,128)S(1)} %fusion.8), kind=kOutput, calls=%fused_computation.39 | convolution fusion | flops 1610645504 | bytes 6422528 | tf_op jit(solution)/shard_map/dot_general | solution.py:124
  79.5 51.6 %all_to_all.75 = f32[2,4,8,64,256]{4,3,2,0,1:T(8,128)} all-to-all(f32[2,4,8,64,256]{4,3,2,0,1:T(8,128)S(1)} %copy.105), channel_id=1, replica_groups=mesh['seq'=16,'zh'=2,'x'=4,'y'=8] {'x'}, dimensions={1} | all-to-all | bytes 8388608 | tf_op jit(solution)/shard_map/all_to_all | solution.py:35
  131.2 2.6 reduce_sum.65
  133.8 81.3 %all-gather.2.cloned.1.call-done = bf16[256,4096]{0,1:T(8,128)(2,1)} async-done(((bf16[256,64]{0,1:T(8,128)(2,1)}), bf16[256,4096]{0,1:T(8,128)(2,1)}) %all-gather.2.cloned.1.call-update) | async-done | bytes 2097168 | tf_op jit(solution)/shard_map/all_gather | solution.py:43
  215.1 2.7 fusion.52
  217.9 0.6 copy-done
  218.8 16.8 %all_to_all.76 = f32[16,1,1024]{2,1,0:T(1,128)S(1)} all-to-all(f32[16,1,1024]{2,1,0:T(1,128)S(1)} %reshape.274), channel_id=1, replica_groups=mesh['seq'=16,'zh'=2,'x'=4,'y'=8] {'seq'}, dimensions={0} | all-to-all | bytes 131072 | tf_op jit(solution)/shard_map/all_to_all | solution.py:75
  235.6 0.8 reduce.8
  236.5 1.3 convolution_bitcast_fusion.3
  237.8 1.0 fusion.19
  238.8 2.4 collective-permute-start.3
  241.6 3.9 %collective-permute-done.3 = f32[8,1,32,33]{2,3,0,1:T(8,128)S(1)} collective-permute-done((f32[8,1,32,33]{2,3,0,1:T(8,128)S(1)}, f32[8,1,32,33]{2,3,0,1:T(8,128)S(1)}, u32[]{:S(2)}, u32[]{:S(2)}) %collective-permute-start.3) | collective-permute-done | bytes 33824 | tf_op jit(solution)/shard_map/ppermute | solution.py:19
  246.4 0.9 reshape.276
  247.3 5.5 %all-to-all-start.6 = ((f32[16,1,3072]{2,1,0:T(1,128)}), f32[16,1,3072]{2,1,0:T(1,128)S(1)}, u32[]{:S(2)}, u32[]{:S(2)}) async-start(f32[16,1,3072]{2,1,0:T(1,128)} %reshape.276), calls=%async_computation.6 | async-start | bytes 393216 | tf_op jit(solution)/shard_map/all_to_all | solution.py:83
  252.8 1.1 copy.106
  253.9 13.5 %all-to-all-done.6 = f32[16,1,3072]{2,1,0:T(1,128)S(1)} async-done(((f32[16,1,3072]{2,1,0:T(1,128)}), f32[16,1,3072]{2,1,0:T(1,128)S(1)}, u32[]{:S(2)}, u32[]{:S(2)}) %all-to-all-start.6) | async-done | bytes 196640 | tf_op jit(solution)/shard_map/all_to_all | solution.py:83
  267.5 3.9 %all-to-all-start.3 = ((f32[2,8,64,256]{3,2,0,1:T(8,128)}), f32[2,8,64,256]{3,2,0,1:T(8,128)S(1)}, u32[]{:S(2)}, u32[]{:S(2)}) async-start(f32[2,8,64,256]{3,2,0,1:T(8,128)} %copy.106), calls=%async_computation.3 | async-start | bytes 2097152 | tf_op jit(solution)/shard_map/all_to_all | solution.py:38
  271.9 3.5 %collective-permute-start.2 = (f32[1,1,256,257]{2,3,1,0:T(8,128)S(1)}, f32[1,1,256,257]{2,3,1,0:T(8,128)S(1)}, u32[]{:S(2)}, u32[]{:S(2)}) collective-permute-start(f32[1,1,256,257]{2,3,1,0:T(8,128)S(1)} %pad_maximum_fusion.2), channel_id=1, source_target_pairs={{0,1},{1,0},{2,3},{3,2},{4,5},{5,4},{6,7},{7,6},{8,9},{9,8},{10,11... | collective-permute-start | bytes 789512 | tf_op jit(solution)/shard_map/ppermute | solution.py:19
  275.4 26.5 %collective-permute-done.2 = f32[1,1,256,257]{2,3,1,0:T(8,128)S(1)} collective-permute-done((f32[1,1,256,257]{2,3,1,0:T(8,128)S(1)}, f32[1,1,256,257]{2,3,1,0:T(8,128)S(1)}, u32[]{:S(2)}, u32[]{:S(2)}) %collective-permute-start.2) | collective-permute-done | bytes 263200 | tf_op jit(solution)/shard_map/ppermute | solution.py:19
  301.9 1.1 reduce.9
  303.5 1.0 fusion.3
  304.5 0.7 reduce_sum.66
  305.2 6.8 %all-to-all-start.4 = ((f32[2,64,256]{2,1,0:T(8,128)}), f32[2,64,256]{2,1,0:T(8,128)S(1)}, u32[]{:S(2)}, u32[]{:S(2)}) async-start(f32[2,64,256]{2,1,0:T(8,128)} %reduce_sum.66), calls=%async_computation.4 | async-start | bytes 262144 | tf_op jit(solution)/shard_map/all_to_all | solution.py:38
  312.0 1.0 fusion.2
  313.1 0.9 fusion.4
  314.1 10.1 %all-to-all-done.4 = f32[2,64,256]{2,1,0:T(8,128)S(1)} async-done(((f32[2,64,256]{2,1,0:T(8,128)}), f32[2,64,256]{2,1,0:T(8,128)S(1)}, u32[]{:S(2)}, u32[]{:S(2)}) %all-to-all-start.4) | async-done | bytes 131104 | tf_op jit(solution)/shard_map/all_to_all | solution.py:38
  324.2 0.6 reduce_sum.67
  (81 shorter events, 6.2 us)
Async XLA Ops:
  8.5 28.6 %collective-permute-start = (f32[1,1,256,256]{2,3,1,0:T(8,128)S(1)}, f32[1,1,256,256]{2,3,1,0:T(8,128)S(1)}, u32[]{:S(2)}, u32[]{:S(2)}) collective-permute-start(f32[1,1,256,256]{2,3,1,0:T(8,128)S(1)} %convolution_bitcast_fusion.1), channel_id=1, source_target_pairs={{0,1},{1,0},{2,3},{3,2},{4,5},{5,4},{6,7},{7,6},{8,9},{9,8},{10,11... | collective-permute-start | bytes 786440 | tf_op jit(solution)/shard_map/ppermute | solution.py:19
  16.4 31.3 %all-to-all-start = ((f32[16,1,3072]{2,1,0:T(1,128)}), f32[16,1,3072]{2,1,0:T(1,128)S(1)}, u32[]{:S(2)}, u32[]{:S(2)}) async-start(f32[16,1,3072]{2,1,0:T(1,128)} %reshape.270), calls=%async_computation | async-start | bytes 393216 | tf_op jit(solution)/shard_map/all_to_all | solution.py:75
  33.1 182.1 %all-gather.2.cloned.1.call-start = ((), (), s32[]{:S(2)}) async-start(), calls=%async_computation.7 | async-start | bytes 2129920 | tf_op jit(solution)/shard_map/all_gather | solution.py:43
  33.8 2.6 copy-start.14
  49.6 15.1 %copy-start.10 = (f32[256,64]{0,1:T(8,128)S(1)}, f32[256,64]{0,1:T(8,128)}, u32[]{:S(2)}) copy-start(f32[256,64]{0,1:T(8,128)} %param.9) | copy-start | bytes 196612
  49.6 7.0 %copy-start.4 = (f32[32,8,1,64]{3,1,0,2:T(8,128)}, f32[32,8,1,64]{3,1,0,2:T(8,128)S(1)}, u32[]{:S(2)}) copy-start(f32[32,8,1,64]{3,1,0,2:T(8,128)S(1)} %get-tuple-element.13) | copy-start | bytes 196612
  49.6 7.0 %copy-start.6 = (f32[32,8,1,64]{3,1,0,2:T(8,128)}, f32[32,8,1,64]{3,1,0,2:T(8,128)S(1)}, u32[]{:S(2)}) copy-start(f32[32,8,1,64]{3,1,0,2:T(8,128)S(1)} %get-tuple-element.12) | copy-start | bytes 196612
  49.6 8.2 %copy-start.2 = (f32[32,8,1,64]{3,1,0,2:T(8,128)}, f32[32,8,1,64]{3,1,0,2:T(8,128)S(1)}, u32[]{:S(2)}) copy-start(f32[32,8,1,64]{3,1,0,2:T(8,128)S(1)} %get-tuple-element.11) | copy-start | bytes 196612
  50.0 6.4 %collective-permute-start.1 = (f32[8,1,32,32]{2,3,0,1:T(8,128)S(1)}, f32[8,1,32,32]{2,3,0,1:T(8,128)S(1)}, u32[]{:S(2)}, u32[]{:S(2)}) collective-permute-start(f32[8,1,32,32]{2,3,0,1:T(8,128)S(1)} %convolution_bitcast_fusion.4), channel_id=1, source_target_pairs={{0,1},{1,0},{2,3},{3,2},{4,5},{5,4},{6,7},{7,6},{8,9},{9,8},{10,11... | collective-permute-start | bytes 98312 | tf_op jit(solution)/shard_map/ppermute | solution.py:19
  57.0 0.9 copy-start.3
  57.9 16.7 %all-to-all-start.1 = ((f32[16,1,1024]{2,1,0:T(1,128)}), f32[16,1,1024]{2,1,0:T(1,128)S(1)}, u32[]{:S(2)}, u32[]{:S(2)}) async-start(f32[16,1,1024]{2,1,0:T(1,128)} %reshape.272), calls=%async_computation.1 | async-start | bytes 131072 | tf_op jit(solution)/shard_map/all_to_all | solution.py:83
  64.9 14.2 %copy-start.8 = (f32[256,64]{0,1:T(8,128)}, f32[256,64]{0,1:T(8,128)S(1)}, u32[]{:S(2)}) copy-start(f32[256,64]{0,1:T(8,128)S(1)} %fusion.8) | copy-start | bytes 196612
  217.9 0.6 copy-start
  218.5 27.0 %copy-start.7 = (f32[32,8,1,64]{3,1,0,2:T(8,128)S(1)}, f32[32,8,1,64]{3,1,0,2:T(8,128)}, u32[]{:S(2)}) copy-start(f32[32,8,1,64]{3,1,0,2:T(8,128)} %copy-done.6) | copy-start | bytes 196612
  218.5 27.4 %copy-start.5 = (f32[32,8,1,64]{3,1,0,2:T(8,128)S(1)}, f32[32,8,1,64]{3,1,0,2:T(8,128)}, u32[]{:S(2)}) copy-start(f32[32,8,1,64]{3,1,0,2:T(8,128)} %copy-done.4) | copy-start | bytes 196612
  238.8 6.6 %collective-permute-start.3 = (f32[8,1,32,33]{2,3,0,1:T(8,128)S(1)}, f32[8,1,32,33]{2,3,0,1:T(8,128)S(1)}, u32[]{:S(2)}, u32[]{:S(2)}) collective-permute-start(f32[8,1,32,33]{2,3,0,1:T(8,128)S(1)} %pad_maximum_fusion.3), channel_id=1, source_target_pairs={{0,1},{1,0},{2,3},{3,2},{4,5},{5,4},{6,7},{7,6},{8,9},{9,8},{10,11... | collective-permute-start | bytes 101384 | tf_op jit(solution)/shard_map/ppermute | solution.py:19
  247.3 20.2 %all-to-all-start.6 = ((f32[16,1,3072]{2,1,0:T(1,128)}), f32[16,1,3072]{2,1,0:T(1,128)S(1)}, u32[]{:S(2)}, u32[]{:S(2)}) async-start(f32[16,1,3072]{2,1,0:T(1,128)} %reshape.276), calls=%async_computation.6 | async-start | bytes 393216 | tf_op jit(solution)/shard_map/all_to_all | solution.py:83
  252.8 18.5 %copy-start.1 = (f32[256,128]{0,1:T(8,128)S(1)}, f32[256,128]{0,1:T(8,128)}, u32[]{:S(2)}) copy-start(f32[256,128]{0,1:T(8,128)} %copy-done) | copy-start | bytes 393220
  252.8 18.5 %copy-start.11 = (f32[256,64]{0,1:T(8,128)S(1)}, f32[256,64]{0,1:T(8,128)}, u32[]{:S(2)}) copy-start(f32[256,64]{0,1:T(8,128)} %param.9) | copy-start | bytes 196612
  252.8 19.0 %copy-start.9 = (f32[256,64]{0,1:T(8,128)S(1)}, f32[256,64]{0,1:T(8,128)}, u32[]{:S(2)}) copy-start(f32[256,64]{0,1:T(8,128)} %copy-done.8) | copy-start | bytes 196612
  267.5 37.0 %all-to-all-start.3 = ((f32[2,8,64,256]{3,2,0,1:T(8,128)}), f32[2,8,64,256]{3,2,0,1:T(8,128)S(1)}, u32[]{:S(2)}, u32[]{:S(2)}) async-start(f32[2,8,64,256]{3,2,0,1:T(8,128)} %copy.106), calls=%async_computation.3 | async-start | bytes 2097152 | tf_op jit(solution)/shard_map/all_to_all | solution.py:38
  271.8 31.6 %copy-start.12 = (f32[256,64]{0,1:T(8,128)S(1)}, f32[256,64]{0,1:T(8,128)}, u32[]{:S(2)}) copy-start(f32[256,64]{0,1:T(8,128)} %param.7) | copy-start | bytes 196612
  271.9 30.0 %collective-permute-start.2 = (f32[1,1,256,257]{2,3,1,0:T(8,128)S(1)}, f32[1,1,256,257]{2,3,1,0:T(8,128)S(1)}, u32[]{:S(2)}, u32[]{:S(2)}) collective-permute-start(f32[1,1,256,257]{2,3,1,0:T(8,128)S(1)} %pad_maximum_fusion.2), channel_id=1, source_target_pairs={{0,1},{1,0},{2,3},{3,2},{4,5},{5,4},{6,7},{7,6},{8,9},{9,8},{10,11... | collective-permute-start | bytes 789512 | tf_op jit(solution)/shard_map/ppermute | solution.py:19
  303.3 9.9 %copy-start.13 = (f32[256,64]{0,1:T(8,128)S(1)}, f32[256,64]{0,1:T(8,128)}, u32[]{:S(2)}) copy-start(f32[256,64]{0,1:T(8,128)} %param.8) | copy-start | bytes 196612
  305.2 19.0 %all-to-all-start.4 = ((f32[2,64,256]{2,1,0:T(8,128)}), f32[2,64,256]{2,1,0:T(8,128)S(1)}, u32[]{:S(2)}, u32[]{:S(2)}) async-start(f32[2,64,256]{2,1,0:T(8,128)} %reduce_sum.66), calls=%async_computation.4 | async-start | bytes 262144 | tf_op jit(solution)/shard_map/all_to_all | solution.py:38
Sparse Core Ops, SparseCore 0:
  39.7 175.3 all-gather.1

commit v4 on v3

--- a/solution.py
+++ b/solution.py
@@ -33,10 +33,9 @@
     block = rows // (sizes[0] * sizes[1] * sizes[2])
     parts = partial_value.reshape(*sizes, block, cols)
     parts = lax.all_to_all(parts, "x", 1, 1, tiled=True).sum(1)
-    parts, companion = lax.optimization_barrier((parts, companion))
     for dim in (1, 0):
         parts = lax.all_to_all(parts, HEAD_AXES[2 * dim], dim, dim, tiled=True).sum(dim)
-    return parts, companion
+    return lax.optimization_barrier((parts, companion))
 
 
 def gather_head(piece):

time: 335 us -> 341 us (1.018)
  waiting for transfers between devices: 159 us -> 172 us
  starting transfers between devices: 51.2 us -> 44.1 us
  blocking collectives: 68.5 us -> 72.9 us
    all_to_all x2 -> x1, waiting for transfers between devices: 10.1 us -> 47.4 us  [scatter_head(): parts = lax.all_to_all(parts, 'x', 1, 1, tiled=True).sum(1)]
    ppermute x4, waiting for transfers between devices: 33.6 us -> 14.8 us  [swapped(): lax.ppermute(x, axis, [(i, i ^ 1 << distance) for i in range(lax.axis_siz...]
    all_to_all x2, waiting for transfers between devices: 23.2 us -> 13.2 us  [to_contiguous(): lax.all_to_all(layout, 'seq', split_axis=0, concat_axis=2, tiled=True)]
    all_to_all x2 -> x1, starting transfers between devices: 10.7 us -> 4.86 us  [scatter_head(): parts = lax.all_to_all(parts, 'x', 1, 1, tiled=True).sum(1)]
    all_to_all x1 -> x2, blocking collectives: 51.6 us -> 56 us  [scatter_head(): lax.all_to_all(parts, HEAD_AXES[2 * dim], dim, dim, tiled=True).sum(dim)]
    all_gather x1, waiting for transfers between devices: 81.3 us -> 84.8 us  [gather_head(): return lax.all_gather(piece, HEAD_AXES, axis=1, tiled=True)]
  transfers between devices with their start and end apart: 10 -> 9, of which waited for: 8 -> 8; matrix products, arithmetic and copies ran while one was open for 8% -> 4% of each run, Pallas kernels for 0% -> 0%
where the time goes in v4:
time: 341 us; the launch traced here: 340 us
  waiting for transfers between devices  172 us (50%)
  blocking collectives  72.9 us (21%)
  starting transfers between devices  44.1 us (13%)
  between operations  14.7 us (4%)
  local copies, waits for them, and re-layouts  13.3 us (4%)
  matrix products  13.2 us (4%)
  other arithmetic  10.5 us (3%)
    all_gather x1, waiting for transfers between devices, gather_head(): return lax.all_gather(piece, HEAD_AXES, axis=1, tiled=True)  84.8 us
    all_to_all x2, blocking collectives, scatter_head(): lax.all_to_all(parts, HEAD_AXES[2 * dim], dim, dim, tiled=True).sum(dim)  56 us
    all_to_all x1, waiting for transfers between devices, scatter_head(): parts = lax.all_to_all(parts, 'x', 1, 1, tiled=True).sum(1)  47.4 us
    all_to_all x1, blocking collectives, to_strided(): lax.all_to_all(layout, 'seq', split_axis=1, concat_axis=0, tiled=True)  16.8 us
    all_to_all x1, starting transfers between devices, to_strided(): lax.all_to_all(layout, 'seq', split_axis=1, concat_axis=0, tiled=True)  16.7 us
    ppermute x4, waiting for transfers between devices, swapped(): lax.ppermute(x, axis, [(i, i ^ 1 << distance) for i in range(lax.axis_siz...  14.8 us
    all_to_all x2, waiting for transfers between devices, to_contiguous(): lax.all_to_all(layout, 'seq', split_axis=0, concat_axis=2, tiled=True)  13.2 us
    all_to_all x2, starting transfers between devices, to_contiguous(): lax.all_to_all(layout, 'seq', split_axis=0, concat_axis=2, tiled=True)  11.5 us
  transfers between devices with their start and end apart: 9, of which 8 were waited for; matrix products, arithmetic and copies ran while one was open for 4% of the time, Pallas kernels for 0%

profile of v4, /device:TPU:1, one launch (start us, length us, event | category | flops | bytes accessed | tf_op | source)
XLA Modules:
  0.0 340.1 jit_solution(13395438279742205660)
XLA Ops:
  7.2 1.3 convolution_bitcast_fusion.1
  8.5 4.0 %collective-permute-start = (f32[1,1,256,256]{2,3,1,0:T(8,128)S(1)}, f32[1,1,256,256]{2,3,1,0:T(8,128)S(1)}, u32[]{:S(2)}, u32[]{:S(2)}) collective-permute-start(f32[1,1,256,256]{2,3,1,0:T(8,128)S(1)} %convolution_bitcast_fusion.1), channel_id=1, source_target_pairs={{0,1},{1,0},{2,3},{3,2},{4,5},{5,4},{6,7},{7,6},{8,9},{9,8},{10,11... | collective-permute-start | bytes 786440 | tf_op jit(solution)/shard_map/ppermute | solution.py:19
  12.5 0.9 copy.92
  13.4 0.9 copy.93
  14.4 0.9 copy.94
  15.5 0.9 reshape.270
  16.4 16.7 %all-to-all-start = ((f32[16,1,3072]{2,1,0:T(1,128)}), f32[16,1,3072]{2,1,0:T(1,128)S(1)}, u32[]{:S(2)}, u32[]{:S(2)}) async-start(f32[16,1,3072]{2,1,0:T(1,128)} %reshape.270), calls=%async_computation | async-start | bytes 393216 | tf_op jit(solution)/shard_map/all_to_all | solution.py:74
  33.1 1.3 constant_dynamic-update-slice_fusion.1
  34.4 1.3 constant_dynamic-update-slice_fusion
  35.7 0.6 dynamic_slice.3
  36.3 0.8 select_reduce_fusion
  37.1 10.6 %all-to-all-done = f32[16,1,3072]{2,1,0:T(1,128)S(1)} async-done(((f32[16,1,3072]{2,1,0:T(1,128)}), f32[16,1,3072]{2,1,0:T(1,128)S(1)}, u32[]{:S(2)}, u32[]{:S(2)}) %all-to-all-start) | async-done | bytes 196640 | tf_op jit(solution)/shard_map/all_to_all | solution.py:74
  47.7 0.5 broadcast.151
  48.3 1.1 reduce.6
  50.0 2.4 collective-permute-start.1
  52.4 0.8 fusion.12
  53.2 3.3 collective-permute-done.1
  57.1 0.8 reshape.272
  57.9 6.0 %all-to-all-start.1 = ((f32[16,1,1024]{2,1,0:T(1,128)}), f32[16,1,1024]{2,1,0:T(1,128)S(1)}, u32[]{:S(2)}, u32[]{:S(2)}) async-start(f32[16,1,1024]{2,1,0:T(1,128)} %reshape.272), calls=%async_computation.1 | async-start | bytes 131072 | tf_op jit(solution)/shard_map/all_to_all | solution.py:82
  63.8 0.8 fusion.11
  64.9 9.0 %all-to-all-done.1 = f32[16,1,1024]{2,1,0:T(1,128)S(1)} async-done(((f32[16,1,1024]{2,1,0:T(1,128)}), f32[16,1,1024]{2,1,0:T(1,128)S(1)}, u32[]{:S(2)}, u32[]{:S(2)}) %all-to-all-start.1) | async-done | bytes 65568 | tf_op jit(solution)/shard_map/all_to_all | solution.py:82
  73.9 0.8 reduce.7
  75.0 3.5 %fusion.15 = f32[4096,256]{1,0:T(8,128)S(1)} fusion(f32[128,4096]{1,0:T(8,128)S(1)} %constant_dynamic-update-slice_fusion, f32[256,64]{0,1:T(8,128)S(1)} %copy.104, f32[256,64]{0,1:T(8,128)S(1)} %fusion.8), kind=kOutput, calls=%fused_computation.39 | convolution fusion | flops 1610645504 | bytes 6422528 | tf_op jit(solution)/shard_map/dot_general | solution.py:123
  78.4 2.3 copy.105
  80.7 4.9 %all-to-all-start.2 = ((f32[2,4,8,64,256]{4,3,2,0,1:T(8,128)}), f32[2,4,8,64,256]{4,3,2,0,1:T(8,128)}, u32[]{:S(2)}, u32[]{:S(2)}) async-start(f32[2,4,8,64,256]{4,3,2,0,1:T(8,128)} %copy.105), calls=%async_computation.2 | async-start | bytes 8388608 | tf_op jit(solution)/shard_map/all_to_all | solution.py:35
  85.6 0.7 all-gather.2.cloned.1.call-update
  86.3 47.4 %all-to-all-done.2 = f32[2,4,8,64,256]{4,3,2,0,1:T(8,128)} async-done(((f32[2,4,8,64,256]{4,3,2,0,1:T(8,128)}), f32[2,4,8,64,256]{4,3,2,0,1:T(8,128)}, u32[]{:S(2)}, u32[]{:S(2)}) %all-to-all-start.2) | async-done | bytes 4194336 | tf_op jit(solution)/shard_map/all_to_all | solution.py:35
  133.7 2.6 reduce_sum.65
  136.4 31.4 %all_to_all.75 = f32[2,8,64,256]{3,2,0,1:T(8,128)S(1)} all-to-all(f32[2,8,64,256]{3,2,0,1:T(8,128)S(1)} %copy.106), channel_id=1, replica_groups=mesh['seq'=16,'zh'=2,'x'=4,'y'=8] {'y'}, dimensions={1} | all-to-all | bytes 2097152 | tf_op jit(solution)/shard_map/all_to_all | solution.py:37
  167.8 0.7 reduce_sum.66
  168.5 24.6 %all_to_all.76 = f32[2,64,256]{2,1,0:T(8,128)S(1)} all-to-all(f32[2,64,256]{2,1,0:T(8,128)} %reduce_sum.66), channel_id=1, replica_groups=mesh['seq'=16,'zh'=2,'x'=4,'y'=8] {'zh'}, dimensions={0} | all-to-all | bytes 262144 | tf_op jit(solution)/shard_map/all_to_all | solution.py:37
  193.1 0.6 reduce_sum.67
  193.8 84.8 %all-gather.2.cloned.1.call-done = bf16[256,4096]{0,1:T(8,128)(2,1)} async-done(((bf16[256,64]{0,1:T(8,128)(2,1)}), bf16[256,4096]{0,1:T(8,128)(2,1)}) %all-gather.2.cloned.1.call-update) | async-done | bytes 2097168 | tf_op jit(solution)/shard_map/all_gather | solution.py:42
  278.6 2.7 fusion.52
  281.7 16.8 %all_to_all.77 = f32[16,1,1024]{2,1,0:T(1,128)S(1)} all-to-all(f32[16,1,1024]{2,1,0:T(1,128)S(1)} %reshape.274), channel_id=1, replica_groups=mesh['seq'=16,'zh'=2,'x'=4,'y'=8] {'seq'}, dimensions={0} | all-to-all | bytes 131072 | tf_op jit(solution)/shard_map/all_to_all | solution.py:74
  298.5 0.8 reduce.8
  299.9 2.4 collective-permute-start.3
  302.7 3.8 %collective-permute-done.3 = f32[8,1,32,33]{2,3,0,1:T(8,128)S(1)} collective-permute-done((f32[8,1,32,33]{2,3,0,1:T(8,128)S(1)}, f32[8,1,32,33]{2,3,0,1:T(8,128)S(1)}, u32[]{:S(2)}, u32[]{:S(2)}) %collective-permute-start.3) | collective-permute-done | bytes 33824 | tf_op jit(solution)/shard_map/ppermute | solution.py:19
  307.5 0.9 reshape.276
  308.4 5.5 %all-to-all-start.6 = ((f32[16,1,3072]{2,1,0:T(1,128)}), f32[16,1,3072]{2,1,0:T(1,128)S(1)}, u32[]{:S(2)}, u32[]{:S(2)}) async-start(f32[16,1,3072]{2,1,0:T(1,128)} %reshape.276), calls=%async_computation.6 | async-start | bytes 393216 | tf_op jit(solution)/shard_map/all_to_all | solution.py:82
  313.9 0.4 convolution_bitcast_fusion
  314.4 2.2 collective-permute-start.2
  316.6 7.7 %collective-permute-done.2 = f32[1,1,256,257]{2,3,1,0:T(8,128)S(1)} collective-permute-done((f32[1,1,256,257]{2,3,1,0:T(8,128)S(1)}, f32[1,1,256,257]{2,3,1,0:T(8,128)S(1)}, u32[]{:S(2)}, u32[]{:S(2)}) %collective-permute-start.2) | collective-permute-done | bytes 263200 | tf_op jit(solution)/shard_map/ppermute | solution.py:19
  324.4 4.2 %all-to-all-done.6 = f32[16,1,3072]{2,1,0:T(1,128)S(1)} async-done(((f32[16,1,3072]{2,1,0:T(1,128)}), f32[16,1,3072]{2,1,0:T(1,128)S(1)}, u32[]{:S(2)}, u32[]{:S(2)}) %all-to-all-start.6) | async-done | bytes 196640 | tf_op jit(solution)/shard_map/all_to_all | solution.py:82
  328.6 1.1 reduce.9
  330.1 1.0 fusion.2
  331.3 1.0 fusion.3
  332.3 0.9 fusion.4
  (80 shorter events, 4.7 us)
Async XLA Ops:
  8.5 27.9 %collective-permute-start = (f32[1,1,256,256]{2,3,1,0:T(8,128)S(1)}, f32[1,1,256,256]{2,3,1,0:T(8,128)S(1)}, u32[]{:S(2)}, u32[]{:S(2)}) collective-permute-start(f32[1,1,256,256]{2,3,1,0:T(8,128)S(1)} %convolution_bitcast_fusion.1), channel_id=1, source_target_pairs={{0,1},{1,0},{2,3},{3,2},{4,5},{5,4},{6,7},{7,6},{8,9},{9,8},{10,11... | collective-permute-start | bytes 786440 | tf_op jit(solution)/shard_map/ppermute | solution.py:19
  16.4 31.3 %all-to-all-start = ((f32[16,1,3072]{2,1,0:T(1,128)}), f32[16,1,3072]{2,1,0:T(1,128)S(1)}, u32[]{:S(2)}, u32[]{:S(2)}) async-start(f32[16,1,3072]{2,1,0:T(1,128)} %reshape.270), calls=%async_computation | async-start | bytes 393216 | tf_op jit(solution)/shard_map/all_to_all | solution.py:74
  33.1 2.6 copy-start.14
  49.6 15.1 %copy-start.10 = (f32[256,64]{0,1:T(8,128)S(1)}, f32[256,64]{0,1:T(8,128)}, u32[]{:S(2)}) copy-start(f32[256,64]{0,1:T(8,128)} %param.9) | copy-start | bytes 196612
  49.6 7.0 %copy-start.4 = (f32[32,8,1,64]{3,1,0,2:T(8,128)}, f32[32,8,1,64]{3,1,0,2:T(8,128)S(1)}, u32[]{:S(2)}) copy-start(f32[32,8,1,64]{3,1,0,2:T(8,128)S(1)} %get-tuple-element.13) | copy-start | bytes 196612
  49.6 7.0 %copy-start.6 = (f32[32,8,1,64]{3,1,0,2:T(8,128)}, f32[32,8,1,64]{3,1,0,2:T(8,128)S(1)}, u32[]{:S(2)}) copy-start(f32[32,8,1,64]{3,1,0,2:T(8,128)S(1)} %get-tuple-element.12) | copy-start | bytes 196612
  49.6 8.2 %copy-start = (f32[32,8,1,64]{3,1,0,2:T(8,128)}, f32[32,8,1,64]{3,1,0,2:T(8,128)S(1)}, u32[]{:S(2)}) copy-start(f32[32,8,1,64]{3,1,0,2:T(8,128)S(1)} %get-tuple-element.11) | copy-start | bytes 196612
  50.0 6.4 %collective-permute-start.1 = (f32[8,1,32,32]{2,3,0,1:T(8,128)S(1)}, f32[8,1,32,32]{2,3,0,1:T(8,128)S(1)}, u32[]{:S(2)}, u32[]{:S(2)}) collective-permute-start(f32[8,1,32,32]{2,3,0,1:T(8,128)S(1)} %convolution_bitcast_fusion.4), channel_id=1, source_target_pairs={{0,1},{1,0},{2,3},{3,2},{4,5},{5,4},{6,7},{7,6},{8,9},{9,8},{10,11... | collective-permute-start | bytes 98312 | tf_op jit(solution)/shard_map/ppermute | solution.py:19
  57.0 0.9 copy-start.2
  57.9 16.1 %all-to-all-start.1 = ((f32[16,1,1024]{2,1,0:T(1,128)}), f32[16,1,1024]{2,1,0:T(1,128)S(1)}, u32[]{:S(2)}, u32[]{:S(2)}) async-start(f32[16,1,1024]{2,1,0:T(1,128)} %reshape.272), calls=%async_computation.1 | async-start | bytes 131072 | tf_op jit(solution)/shard_map/all_to_all | solution.py:82
  64.9 13.5 %copy-start.8 = (f32[256,64]{0,1:T(8,128)}, f32[256,64]{0,1:T(8,128)S(1)}, u32[]{:S(2)}) copy-start(f32[256,64]{0,1:T(8,128)S(1)} %fusion.8) | copy-start | bytes 196612
  80.7 53.0 %all-to-all-start.2 = ((f32[2,4,8,64,256]{4,3,2,0,1:T(8,128)}), f32[2,4,8,64,256]{4,3,2,0,1:T(8,128)}, u32[]{:S(2)}, u32[]{:S(2)}) async-start(f32[2,4,8,64,256]{4,3,2,0,1:T(8,128)} %copy.105), calls=%async_computation.2 | async-start | bytes 8388608 | tf_op jit(solution)/shard_map/all_to_all | solution.py:35
  85.6 193.1 %all-gather.2.cloned.1.call-start = ((), (), s32[]{:S(2)}) async-start(), calls=%async_computation.7 | async-start | bytes 2129920 | tf_op jit(solution)/shard_map/all_gather | solution.py:42
  193.8 105.6 %copy-start.1 = (f32[32,8,1,64]{3,1,0,2:T(8,128)S(1)}, f32[32,8,1,64]{3,1,0,2:T(8,128)}, u32[]{:S(2)}) copy-start(f32[32,8,1,64]{3,1,0,2:T(8,128)} %copy-done) | copy-start | bytes 196612
  193.8 106.0 %copy-start.3 = (f32[8,64,32]{1,2,0:T(8,128)S(1)}, f32[8,64,32]{1,2,0:T(8,128)}, u32[]{:S(2)}) copy-start(f32[8,64,32]{1,2,0:T(8,128)} %copy-done.2) | copy-start | bytes 196612
  281.4 25.2 %copy-start.7 = (f32[32,8,1,64]{3,1,0,2:T(8,128)S(1)}, f32[32,8,1,64]{3,1,0,2:T(8,128)}, u32[]{:S(2)}) copy-start(f32[32,8,1,64]{3,1,0,2:T(8,128)} %copy-done.6) | copy-start | bytes 196612
  281.4 25.6 %copy-start.5 = (f32[32,8,1,64]{3,1,0,2:T(8,128)S(1)}, f32[32,8,1,64]{3,1,0,2:T(8,128)}, u32[]{:S(2)}) copy-start(f32[32,8,1,64]{3,1,0,2:T(8,128)} %copy-done.4) | copy-start | bytes 196612
  299.9 6.6 %collective-permute-start.3 = (f32[8,1,32,33]{2,3,0,1:T(8,128)S(1)}, f32[8,1,32,33]{2,3,0,1:T(8,128)S(1)}, u32[]{:S(2)}, u32[]{:S(2)}) collective-permute-start(f32[8,1,32,33]{2,3,0,1:T(8,128)S(1)} %pad_maximum_fusion.3), channel_id=1, source_target_pairs={{0,1},{1,0},{2,3},{3,2},{4,5},{5,4},{6,7},{7,6},{8,9},{9,8},{10,11... | collective-permute-start | bytes 101384 | tf_op jit(solution)/shard_map/ppermute | solution.py:19
  302.6 11.3 %copy-start.11 = (f32[256,64]{0,1:T(8,128)S(1)}, f32[256,64]{0,1:T(8,128)}, u32[]{:S(2)}) copy-start(f32[256,64]{0,1:T(8,128)} %param.9) | copy-start | bytes 196612
  302.7 11.6 %copy-start.9 = (f32[256,64]{0,1:T(8,128)S(1)}, f32[256,64]{0,1:T(8,128)}, u32[]{:S(2)}) copy-start(f32[256,64]{0,1:T(8,128)} %copy-done.8) | copy-start | bytes 196612
  308.4 20.2 %all-to-all-start.6 = ((f32[16,1,3072]{2,1,0:T(1,128)}), f32[16,1,3072]{2,1,0:T(1,128)S(1)}, u32[]{:S(2)}, u32[]{:S(2)}) async-start(f32[16,1,3072]{2,1,0:T(1,128)} %reshape.276), calls=%async_computation.6 | async-start | bytes 393216 | tf_op jit(solution)/shard_map/all_to_all | solution.py:82
  314.4 9.9 %collective-permute-start.2 = (f32[1,1,256,257]{2,3,1,0:T(8,128)S(1)}, f32[1,1,256,257]{2,3,1,0:T(8,128)S(1)}, u32[]{:S(2)}, u32[]{:S(2)}) collective-permute-start(f32[1,1,256,257]{2,3,1,0:T(8,128)S(1)} %pad_maximum_fusion.2), channel_id=1, source_target_pairs={{0,1},{1,0},{2,3},{3,2},{4,5},{5,4},{6,7},{7,6},{8,9},{9,8},{10,11... | collective-permute-start | bytes 789512 | tf_op jit(solution)/shard_map/ppermute | solution.py:19
  329.7 1.6 copy-start.12
  329.8 2.5 copy-start.13
Sparse Core Ops, SparseCore 0:
  92.2 186.3 all-gather.1

commit v5 on v3

--- a/solution.py
+++ b/solution.py
@@ -40,7 +40,14 @@
 
 
 def gather_head(piece):
-    return lax.all_gather(piece, HEAD_AXES, axis=1, tiled=True)
+    rows, cols = piece.shape
+    stacked = piece
+    for axis in ("zh", "y", "x"):
+        count = lax.axis_size(axis)
+        copies = jnp.broadcast_to(stacked[None], (count,) + stacked.shape)
+        stacked = lax.all_to_all(copies, axis, 0, 0, tiled=True)
+    order = stacked.reshape(stacked.shape[:3] + (rows, cols)).transpose(3, 2, 0, 1, 4)
+    return order.reshape(rows, -1)
 
 
 def attend_forward(query_part, key_part, value_part, allowed):

time: 335 us -> 298 us (0.89)
  blocking collectives: 68.5 us -> 17.1 us
  starting transfers between devices: 51.2 us -> 77.9 us
  between operations: 14.7 us -> 1.37 us
  local copies, waits for them, and re-layouts: 13.1 us -> 22.9 us
  waiting for transfers between devices: 159 us -> 150 us
    all_gather x1 -> x0, waiting for transfers between devices: 81.3 us -> none  [gather_head(): return lax.all_gather(piece, HEAD_AXES, axis=1, tiled=True)]
    all_to_all x0 -> x4, waiting for transfers between devices: none -> 66.3 us  [the longest x1 43.8 us: scatter_head(): parts = lax.all_to_all(parts, 'x', 1, 1, tiled=True).sum(1)]
    all_to_all x1 -> x0, blocking collectives: 51.6 us -> none  [scatter_head(): parts = lax.all_to_all(parts, 'x', 1, 1, tiled=True).sum(1)]
    all_to_all x0 -> x4, starting transfers between devices: none -> 35.4 us  [the longest x3 30.6 us: gather_head(): stacked = lax.all_to_all(copies, axis, 0, 0, tiled=True)]
    ppermute x4, waiting for transfers between devices: 33.6 us -> 40.8 us  [swapped(): lax.ppermute(x, axis, [(i, i ^ 1 << distance) for i in range(lax.axis_siz...]
    all_to_all x1, starting transfers between devices: 16.7 us -> 9.66 us  [to_strided(): lax.all_to_all(layout, 'seq', split_axis=1, concat_axis=0, tiled=True)]
    broadcast_in_dim x0 -> x3, local copies, waits for them, and re-layouts: none -> 3.86 us  [gather_head(): copies = jnp.broadcast_to(stacked[None], (count,) + stacked.shape)]
    unnamed x45 -> x57, local copies, waits for them, and re-layouts: 8.15 us -> 9.03 us
  transfers between devices with their start and end apart: 10 -> 13, of which waited for: 8 -> 10; matrix products, arithmetic and copies ran while one was open for 8% -> 11% of each run, Pallas kernels for 0% -> 0%
where the time goes in v5:
time: 298 us; the launch traced here: 294 us
  waiting for transfers between devices  150 us (50%)
  starting transfers between devices  77.9 us (26%)
  local copies, waits for them, and re-layouts  22.9 us (8%)
  blocking collectives  17.1 us (6%)
  matrix products  13.2 us (4%)
  other arithmetic  11.5 us (4%)
    all_to_all x1, waiting for transfers between devices, scatter_head(): parts = lax.all_to_all(parts, 'x', 1, 1, tiled=True).sum(1)  43.8 us
    ppermute x4, waiting for transfers between devices, swapped(): lax.ppermute(x, axis, [(i, i ^ 1 << distance) for i in range(lax.axis_siz...  40.8 us
    all_to_all x3, starting transfers between devices, gather_head(): stacked = lax.all_to_all(copies, axis, 0, 0, tiled=True)  30.6 us
    all_to_all x3, waiting for transfers between devices, gather_head(): stacked = lax.all_to_all(copies, axis, 0, 0, tiled=True)  22.5 us
    all_to_all x2, waiting for transfers between devices, to_contiguous(): lax.all_to_all(layout, 'seq', split_axis=0, concat_axis=2, tiled=True)  22.2 us
    all_to_all x1, blocking collectives, to_strided(): lax.all_to_all(layout, 'seq', split_axis=1, concat_axis=0, tiled=True)  17.1 us
    ppermute x4, starting transfers between devices, swapped(): lax.ppermute(x, axis, [(i, i ^ 1 << distance) for i in range(lax.axis_siz...  13 us
    all_to_all x2, starting transfers between devices, to_contiguous(): lax.all_to_all(layout, 'seq', split_axis=0, concat_axis=2, tiled=True)  11 us
  transfers between devices with their start and end apart: 13, of which 10 were waited for; matrix products, arithmetic and copies ran while one was open for 11% of the time, Pallas kernels for 0%

profile of v5, /device:TPU:1, one launch (start us, length us, event | category | flops | bytes accessed | tf_op | source)
XLA Modules:
  0.0 294.1 jit_solution(15620570328177495195)
XLA Ops:
  0.7 1.4 broadcast_in_dim.62
  2.1 19.3 %all-to-all-start.3 = ((bf16[2,256,64]{1,2,0:T(8,128)(2,1)}), bf16[2,256,64]{1,2,0:T(8,128)(2,1)S(1)}, u32[]{:S(2)}, u32[]{:S(2)}) async-start(bf16[2,256,64]{1,2,0:T(8,128)(2,1)} %broadcast_in_dim.62), calls=%async_computation.3 | async-start | bytes 131072 | tf_op jit(solution)/shard_map/all_to_all | solution.py:48
  21.3 0.9 copy.97
  22.3 0.9 copy.98
  23.2 0.9 copy.99
  24.3 0.9 reshape.277
  25.2 8.5 %all-to-all-done.3 = bf16[2,256,64]{1,2,0:T(8,128)(2,1)S(1)} async-done(((bf16[2,256,64]{1,2,0:T(8,128)(2,1)}), bf16[2,256,64]{1,2,0:T(8,128)(2,1)S(1)}, u32[]{:S(2)}, u32[]{:S(2)}) %all-to-all-start.3) | async-done | bytes 65568 | tf_op jit(solution)/shard_map/all_to_all | solution.py:48
  33.7 9.7 %all-to-all-start = ((f32[16,1,3072]{2,1,0:T(1,128)}), f32[16,1,3072]{2,1,0:T(1,128)S(1)}, u32[]{:S(2)}, u32[]{:S(2)}) async-start(f32[16,1,3072]{2,1,0:T(1,128)} %reshape.277), calls=%async_computation | async-start | bytes 393216 | tf_op jit(solution)/shard_map/all_to_all | solution.py:82
  43.8 3.2 %collective-permute-start = (f32[1,1,256,256]{2,3,1,0:T(8,128)S(1)}, f32[1,1,256,256]{2,3,1,0:T(8,128)S(1)}, u32[]{:S(2)}, u32[]{:S(2)}) collective-permute-start(f32[1,1,256,256]{2,3,1,0:T(8,128)S(1)} %convolution_bitcast_fusion.1), channel_id=1, source_target_pairs={{0,1},{1,0},{2,3},{3,2},{4,5},{5,4},{6,7},{7,6},{8,9},{9,8},{10,11... | collective-permute-start | bytes 786440 | tf_op jit(solution)/shard_map/ppermute | solution.py:19
  47.0 11.0 %all-to-all-done = f32[16,1,3072]{2,1,0:T(1,128)S(1)} async-done(((f32[16,1,3072]{2,1,0:T(1,128)}), f32[16,1,3072]{2,1,0:T(1,128)S(1)}, u32[]{:S(2)}, u32[]{:S(2)}) %all-to-all-start) | async-done | bytes 196640 | tf_op jit(solution)/shard_map/all_to_all | solution.py:82
  58.0 0.8 broadcast_in_dim.63
  58.9 6.8 %all-to-all-start.4 = ((bf16[8,2,256,64]{2,3,1,0:T(8,128)(2,1)}), bf16[8,2,256,64]{2,3,1,0:T(8,128)(2,1)S(1)}, u32[]{:S(2)}, u32[]{:S(2)}) async-start(bf16[8,2,256,64]{2,3,1,0:T(8,128)(2,1)} %broadcast_in_dim.63), calls=%async_computation.4 | async-start | bytes 1048576 | tf_op jit(solution)/shard_map/all_to_all | solution.py:48
  66.2 1.1 reduce.6
  67.9 3.4 %collective-permute-start.1 = (f32[8,1,32,32]{2,3,0,1:T(8,128)S(1)}, f32[8,1,32,32]{2,3,0,1:T(8,128)S(1)}, u32[]{:S(2)}, u32[]{:S(2)}) collective-permute-start(f32[8,1,32,32]{2,3,0,1:T(8,128)S(1)} %convolution_bitcast_fusion.4), channel_id=1, source_target_pairs={{0,1},{1,0},{2,3},{3,2},{4,5},{5,4},{6,7},{7,6},{8,9},{9,8},{10,11... | collective-permute-start | bytes 98312 | tf_op jit(solution)/shard_map/ppermute | solution.py:19
  71.3 10.9 %collective-permute-done.1 = f32[8,1,32,32]{2,3,0,1:T(8,128)S(1)} collective-permute-done((f32[8,1,32,32]{2,3,0,1:T(8,128)S(1)}, f32[8,1,32,32]{2,3,0,1:T(8,128)S(1)}, u32[]{:S(2)}, u32[]{:S(2)}) %collective-permute-start.1) | collective-permute-done | bytes 32800 | tf_op jit(solution)/shard_map/ppermute | solution.py:19
  84.4 5.4 %all-to-all-start.1 = ((f32[16,1,1024]{2,1,0:T(1,128)}), f32[16,1,1024]{2,1,0:T(1,128)S(1)}, u32[]{:S(2)}, u32[]{:S(2)}) async-start(f32[16,1,1024]{2,1,0:T(1,128)} %reshape.279), calls=%async_computation.1 | async-start | bytes 131072 | tf_op jit(solution)/shard_map/all_to_all | solution.py:90
  89.9 1.4 constant_dynamic-update-slice_fusion.1
  91.3 8.6 %all-to-all-done.1 = f32[16,1,1024]{2,1,0:T(1,128)S(1)} async-done(((f32[16,1,1024]{2,1,0:T(1,128)}), f32[16,1,1024]{2,1,0:T(1,128)S(1)}, u32[]{:S(2)}, u32[]{:S(2)}) %all-to-all-start.1) | async-done | bytes 65568 | tf_op jit(solution)/shard_map/all_to_all | solution.py:90
  99.9 1.6 broadcast_in_dim.64
  101.5 4.5 %all-to-all-start.5 = ((bf16[4,8,2,256,64]{3,4,1,2,0:T(8,128)(2,1)}), bf16[4,8,2,256,64]{3,4,1,2,0:T(8,128)(2,1)}, u32[]{:S(2)}, u32[]{:S(2)}) async-start(bf16[4,8,2,256,64]{3,4,1,2,0:T(8,128)(2,1)} %broadcast_in_dim.64), calls=%async_computation.5 | async-start | bytes 4194304 | tf_op jit(solution)/shard_map/all_to_all | solution.py:48
  106.1 1.3 constant_dynamic-update-slice_fusion
  110.7 0.8 reduce.7
  111.7 3.5 %fusion.15 = f32[4096,256]{1,0:T(8,128)S(1)} fusion(f32[128,4096]{1,0:T(8,128)S(1)} %constant_dynamic-update-slice_fusion, f32[256,64]{0,1:T(8,128)S(1)} %copy.109, f32[256,64]{0,1:T(8,128)S(1)} %fusion.8), kind=kOutput, calls=%fused_computation.39 | convolution fusion | flops 1610645504 | bytes 6422528 | tf_op jit(solution)/shard_map/dot_general | solution.py:131
  115.2 2.2 copy.110
  117.4 14.0 %all-to-all-done.5 = bf16[4,8,2,256,64]{3,4,1,2,0:T(8,128)(2,1)} async-done(((bf16[4,8,2,256,64]{3,4,1,2,0:T(8,128)(2,1)}), bf16[4,8,2,256,64]{3,4,1,2,0:T(8,128)(2,1)}, u32[]{:S(2)}, u32[]{:S(2)}) %all-to-all-start.5) | async-done | bytes 2097184 | tf_op jit(solution)/shard_map/all_to_all | solution.py:48
  131.5 4.8 %all-to-all-start.2 = ((f32[2,4,8,64,256]{4,3,2,0,1:T(8,128)}), f32[2,4,8,64,256]{4,3,2,0,1:T(8,128)}, u32[]{:S(2)}, u32[]{:S(2)}) async-start(f32[2,4,8,64,256]{4,3,2,0,1:T(8,128)} %copy.110), calls=%async_computation.2 | async-start | bytes 8388608 | tf_op jit(solution)/shard_map/all_to_all | solution.py:35
  136.3 3.2 %copy.112 = bf16[4,8,2,256,64]{3,4,1,0,2:T(8,128)(2,1)} copy(bf16[4,8,2,256,64]{3,4,1,2,0:T(8,128)(2,1)} %all-to-all-done.5) | data formatting | bytes 4194304 | tf_op jit(solution)/shard_map/all_to_all | solution.py:48
  139.5 43.8 %all-to-all-done.2 = f32[2,4,8,64,256]{4,3,2,0,1:T(8,128)} async-done(((f32[2,4,8,64,256]{4,3,2,0,1:T(8,128)}), f32[2,4,8,64,256]{4,3,2,0,1:T(8,128)}, u32[]{:S(2)}, u32[]{:S(2)}) %all-to-all-start.2) | async-done | bytes 4194336 | tf_op jit(solution)/shard_map/all_to_all | solution.py:35
  183.3 2.6 reduce_sum.65
  185.9 2.7 fusion.52
  189.6 17.1 %all_to_all.90 = f32[16,1,1024]{2,1,0:T(1,128)S(1)} all-to-all(f32[16,1,1024]{2,1,0:T(1,128)S(1)} %reshape.281), channel_id=1, replica_groups=mesh['seq'=16,'zh'=2,'x'=4,'y'=8] {'seq'}, dimensions={0} | all-to-all | bytes 131072 | tf_op jit(solution)/shard_map/all_to_all | solution.py:82
  207.6 1.3 convolution_bitcast_fusion.3
  208.8 1.0 fusion.19
  209.9 2.9 collective-permute-start.3
  213.1 3.4 %collective-permute-done.3 = f32[8,1,32,33]{2,3,0,1:T(8,128)S(1)} collective-permute-done((f32[8,1,32,33]{2,3,0,1:T(8,128)S(1)}, f32[8,1,32,33]{2,3,0,1:T(8,128)S(1)}, u32[]{:S(2)}, u32[]{:S(2)}) %collective-permute-start.3) | collective-permute-done | bytes 33824 | tf_op jit(solution)/shard_map/ppermute | solution.py:19
  217.4 0.9 reshape.283
  218.3 5.6 %all-to-all-start.9 = ((f32[16,1,3072]{2,1,0:T(1,128)}), f32[16,1,3072]{2,1,0:T(1,128)S(1)}, u32[]{:S(2)}, u32[]{:S(2)}) async-start(f32[16,1,3072]{2,1,0:T(1,128)} %reshape.283), calls=%async_computation.9 | async-start | bytes 393216 | tf_op jit(solution)/shard_map/all_to_all | solution.py:90
  224.0 1.1 copy.113
  225.0 13.6 %all-to-all-done.9 = f32[16,1,3072]{2,1,0:T(1,128)S(1)} async-done(((f32[16,1,3072]{2,1,0:T(1,128)}), f32[16,1,3072]{2,1,0:T(1,128)S(1)}, u32[]{:S(2)}, u32[]{:S(2)}) %all-to-all-start.9) | async-done | bytes 196640 | tf_op jit(solution)/shard_map/all_to_all | solution.py:90
  238.6 5.5 %all-to-all-start.6 = ((f32[2,8,64,256]{3,2,0,1:T(8,128)}), f32[2,8,64,256]{3,2,0,1:T(8,128)S(1)}, u32[]{:S(2)}, u32[]{:S(2)}) async-start(f32[2,8,64,256]{3,2,0,1:T(8,128)} %copy.113), calls=%async_computation.6 | async-start | bytes 2097152 | tf_op jit(solution)/shard_map/all_to_all | solution.py:38
  244.6 3.5 %collective-permute-start.2 = (f32[1,1,256,257]{2,3,1,0:T(8,128)S(1)}, f32[1,1,256,257]{2,3,1,0:T(8,128)S(1)}, u32[]{:S(2)}, u32[]{:S(2)}) collective-permute-start(f32[1,1,256,257]{2,3,1,0:T(8,128)S(1)} %pad_maximum_fusion.2), channel_id=1, source_target_pairs={{0,1},{1,0},{2,3},{3,2},{4,5},{5,4},{6,7},{7,6},{8,9},{9,8},{10,11... | collective-permute-start | bytes 789512 | tf_op jit(solution)/shard_map/ppermute | solution.py:19
  248.1 26.5 %collective-permute-done.2 = f32[1,1,256,257]{2,3,1,0:T(8,128)S(1)} collective-permute-done((f32[1,1,256,257]{2,3,1,0:T(8,128)S(1)}, f32[1,1,256,257]{2,3,1,0:T(8,128)S(1)}, u32[]{:S(2)}, u32[]{:S(2)}) %collective-permute-start.2) | collective-permute-done | bytes 263200 | tf_op jit(solution)/shard_map/ppermute | solution.py:19
  274.6 1.1 reduce.9
  276.2 1.0 fusion.3
  278.0 3.4 %all-to-all-start.7 = ((f32[2,64,256]{2,1,0:T(8,128)}), f32[2,64,256]{2,1,0:T(8,128)S(1)}, u32[]{:S(2)}, u32[]{:S(2)}) async-start(f32[2,64,256]{2,1,0:T(8,128)} %reduce_sum.66), calls=%async_computation.7 | async-start | bytes 262144 | tf_op jit(solution)/shard_map/all_to_all | solution.py:38
  281.4 1.0 fusion.2
  282.5 0.9 fusion.4
  283.4 10.1 %all-to-all-done.7 = f32[2,64,256]{2,1,0:T(8,128)S(1)} async-done(((f32[2,64,256]{2,1,0:T(8,128)}), f32[2,64,256]{2,1,0:T(8,128)S(1)}, u32[]{:S(2)}, u32[]{:S(2)}) %all-to-all-start.7) | async-done | bytes 131104 | tf_op jit(solution)/shard_map/all_to_all | solution.py:38
  (102 shorter events, 12.8 us)
Async XLA Ops:
  0.6 42.7 %copy-start.14 = (f32[256,64]{0,1:T(8,128)S(1)}, f32[256,64]{0,1:T(8,128)}, u32[]{:S(2)}) copy-start(f32[256,64]{0,1:T(8,128)} %param.7) | copy-start | bytes 196612
  0.6 42.7 %copy-start.16 = (f32[256,64]{0,1:T(8,128)S(1)}, f32[256,64]{0,1:T(8,128)}, u32[]{:S(2)}) copy-start(f32[256,64]{0,1:T(8,128)} %param.8) | copy-start | bytes 196612
  2.1 31.6 %all-to-all-start.3 = ((bf16[2,256,64]{1,2,0:T(8,128)(2,1)}), bf16[2,256,64]{1,2,0:T(8,128)(2,1)S(1)}, u32[]{:S(2)}, u32[]{:S(2)}) async-start(bf16[2,256,64]{1,2,0:T(8,128)(2,1)} %broadcast_in_dim.62), calls=%async_computation.3 | async-start | bytes 131072 | tf_op jit(solution)/shard_map/all_to_all | solution.py:48
  33.7 24.3 %all-to-all-start = ((f32[16,1,3072]{2,1,0:T(1,128)}), f32[16,1,3072]{2,1,0:T(1,128)S(1)}, u32[]{:S(2)}, u32[]{:S(2)}) async-start(f32[16,1,3072]{2,1,0:T(1,128)} %reshape.277), calls=%async_computation | async-start | bytes 393216 | tf_op jit(solution)/shard_map/all_to_all | solution.py:82
  43.8 64.2 %collective-permute-start = (f32[1,1,256,256]{2,3,1,0:T(8,128)S(1)}, f32[1,1,256,256]{2,3,1,0:T(8,128)S(1)}, u32[]{:S(2)}, u32[]{:S(2)}) collective-permute-start(f32[1,1,256,256]{2,3,1,0:T(8,128)S(1)} %convolution_bitcast_fusion.1), channel_id=1, source_target_pairs={{0,1},{1,0},{2,3},{3,2},{4,5},{5,4},{6,7},{7,6},{8,9},{9,8},{10,11... | collective-permute-start | bytes 786440 | tf_op jit(solution)/shard_map/ppermute | solution.py:19
  58.9 24.8 %all-to-all-start.4 = ((bf16[8,2,256,64]{2,3,1,0:T(8,128)(2,1)}), bf16[8,2,256,64]{2,3,1,0:T(8,128)(2,1)S(1)}, u32[]{:S(2)}, u32[]{:S(2)}) async-start(bf16[8,2,256,64]{2,3,1,0:T(8,128)(2,1)} %broadcast_in_dim.63), calls=%async_computation.4 | async-start | bytes 1048576 | tf_op jit(solution)/shard_map/all_to_all | solution.py:48
  67.5 16.1 %copy-start.6 = (f32[32,8,1,64]{3,1,0,2:T(8,128)}, f32[32,8,1,64]{3,1,0,2:T(8,128)S(1)}, u32[]{:S(2)}) copy-start(f32[32,8,1,64]{3,1,0,2:T(8,128)S(1)} %get-tuple-element.13) | copy-start | bytes 196612
  67.5 16.1 %copy-start.8 = (f32[32,8,1,64]{3,1,0,2:T(8,128)}, f32[32,8,1,64]{3,1,0,2:T(8,128)S(1)}, u32[]{:S(2)}) copy-start(f32[32,8,1,64]{3,1,0,2:T(8,128)S(1)} %get-tuple-element.12) | copy-start | bytes 196612
  67.6 22.3 %copy-start.2 = (f32[32,8,1,64]{3,1,0,2:T(8,128)}, f32[32,8,1,64]{3,1,0,2:T(8,128)S(1)}, u32[]{:S(2)}) copy-start(f32[32,8,1,64]{3,1,0,2:T(8,128)S(1)} %get-tuple-element.11) | copy-start | bytes 196612
  67.9 14.3 %collective-permute-start.1 = (f32[8,1,32,32]{2,3,0,1:T(8,128)S(1)}, f32[8,1,32,32]{2,3,0,1:T(8,128)S(1)}, u32[]{:S(2)}, u32[]{:S(2)}) collective-permute-start(f32[8,1,32,32]{2,3,0,1:T(8,128)S(1)} %convolution_bitcast_fusion.4), channel_id=1, source_target_pairs={{0,1},{1,0},{2,3},{3,2},{4,5},{5,4},{6,7},{7,6},{8,9},{9,8},{10,11... | collective-permute-start | bytes 98312 | tf_op jit(solution)/shard_map/ppermute | solution.py:19
  82.8 7.1 %copy-start.3 = (f32[8,64,32]{1,2,0:T(8,128)}, f32[8,64,32]{1,2,0:T(8,128)S(1)}, u32[]{:S(2)}) copy-start(f32[8,64,32]{1,2,0:T(8,128)S(1)} %fusion.25) | copy-start | bytes 196612
  83.7 0.8 copy-start
  84.4 15.5 %all-to-all-start.1 = ((f32[16,1,1024]{2,1,0:T(1,128)}), f32[16,1,1024]{2,1,0:T(1,128)S(1)}, u32[]{:S(2)}, u32[]{:S(2)}) async-start(f32[16,1,1024]{2,1,0:T(1,128)} %reshape.279), calls=%async_computation.1 | async-start | bytes 131072 | tf_op jit(solution)/shard_map/all_to_all | solution.py:90
  89.9 1.4 copy-start.1
  99.9 1.6 copy-start.18
  101.5 29.9 %all-to-all-start.5 = ((bf16[4,8,2,256,64]{3,4,1,2,0:T(8,128)(2,1)}), bf16[4,8,2,256,64]{3,4,1,2,0:T(8,128)(2,1)}, u32[]{:S(2)}, u32[]{:S(2)}) async-start(bf16[4,8,2,256,64]{3,4,1,2,0:T(8,128)(2,1)} %broadcast_in_dim.64), calls=%async_computation.5 | async-start | bytes 4194304 | tf_op jit(solution)/shard_map/all_to_all | solution.py:48
  106.0 1.4 copy-start.20
  106.0 4.3 %copy-start.12 = (f32[256,64]{0,1:T(8,128)S(1)}, f32[256,64]{0,1:T(8,128)}, u32[]{:S(2)}) copy-start(f32[256,64]{0,1:T(8,128)} %param.9) | copy-start | bytes 196612
  106.0 4.6 %copy-start.19 = (f32[16,1,1024]{2,1,0:T(1,128)S(1)}, f32[16,1,1024]{2,1,0:T(1,128)}, u32[]{:S(2)}) copy-start(f32[16,1,1024]{2,1,0:T(1,128)} %copy-done.18) | copy-start | bytes 196612
  110.6 4.5 %copy-start.10 = (f32[256,64]{0,1:T(8,128)}, f32[256,64]{0,1:T(8,128)S(1)}, u32[]{:S(2)}) copy-start(f32[256,64]{0,1:T(8,128)S(1)} %fusion.8) | copy-start | bytes 196612
  131.5 51.8 %all-to-all-start.2 = ((f32[2,4,8,64,256]{4,3,2,0,1:T(8,128)}), f32[2,4,8,64,256]{4,3,2,0,1:T(8,128)}, u32[]{:S(2)}, u32[]{:S(2)}) async-start(f32[2,4,8,64,256]{4,3,2,0,1:T(8,128)} %copy.110), calls=%async_computation.2 | async-start | bytes 8388608 | tf_op jit(solution)/shard_map/all_to_all | solution.py:35
  188.7 0.7 copy-start.4
  189.3 27.2 %copy-start.9 = (f32[32,8,1,64]{3,1,0,2:T(8,128)S(1)}, f32[32,8,1,64]{3,1,0,2:T(8,128)}, u32[]{:S(2)}) copy-start(f32[32,8,1,64]{3,1,0,2:T(8,128)} %copy-done.8) | copy-start | bytes 196612
  189.3 27.6 %copy-start.7 = (f32[32,8,1,64]{3,1,0,2:T(8,128)S(1)}, f32[32,8,1,64]{3,1,0,2:T(8,128)}, u32[]{:S(2)}) copy-start(f32[32,8,1,64]{3,1,0,2:T(8,128)} %copy-done.6) | copy-start | bytes 196612
  209.9 6.6 %collective-permute-start.3 = (f32[8,1,32,33]{2,3,0,1:T(8,128)S(1)}, f32[8,1,32,33]{2,3,0,1:T(8,128)S(1)}, u32[]{:S(2)}, u32[]{:S(2)}) collective-permute-start(f32[8,1,32,33]{2,3,0,1:T(8,128)S(1)} %pad_maximum_fusion.3), channel_id=1, source_target_pairs={{0,1},{1,0},{2,3},{3,2},{4,5},{5,4},{6,7},{7,6},{8,9},{9,8},{10,11... | collective-permute-start | bytes 101384 | tf_op jit(solution)/shard_map/ppermute | solution.py:19
  218.3 20.3 %all-to-all-start.9 = ((f32[16,1,3072]{2,1,0:T(1,128)}), f32[16,1,3072]{2,1,0:T(1,128)S(1)}, u32[]{:S(2)}, u32[]{:S(2)}) async-start(f32[16,1,3072]{2,1,0:T(1,128)} %reshape.283), calls=%async_computation.9 | async-start | bytes 393216 | tf_op jit(solution)/shard_map/all_to_all | solution.py:90
  223.9 20.1 %copy-start.5 = (f32[256,128]{0,1:T(8,128)S(1)}, f32[256,128]{0,1:T(8,128)}, u32[]{:S(2)}) copy-start(f32[256,128]{0,1:T(8,128)} %copy-done.4) | copy-start | bytes 393220
  223.9 20.1 %copy-start.13 = (f32[256,64]{0,1:T(8,128)S(1)}, f32[256,64]{0,1:T(8,128)}, u32[]{:S(2)}) copy-start(f32[256,64]{0,1:T(8,128)} %param.9) | copy-start | bytes 196612
  224.0 20.6 %copy-start.11 = (f32[256,64]{0,1:T(8,128)S(1)}, f32[256,64]{0,1:T(8,128)}, u32[]{:S(2)}) copy-start(f32[256,64]{0,1:T(8,128)} %copy-done.10) | copy-start | bytes 196612
  238.6 38.7 %all-to-all-start.6 = ((f32[2,8,64,256]{3,2,0,1:T(8,128)}), f32[2,8,64,256]{3,2,0,1:T(8,128)S(1)}, u32[]{:S(2)}, u32[]{:S(2)}) async-start(f32[2,8,64,256]{3,2,0,1:T(8,128)} %copy.113), calls=%async_computation.6 | async-start | bytes 2097152 | tf_op jit(solution)/shard_map/all_to_all | solution.py:38
  244.6 31.6 %copy-start.15 = (f32[256,64]{0,1:T(8,128)S(1)}, f32[256,64]{0,1:T(8,128)}, u32[]{:S(2)}) copy-start(f32[256,64]{0,1:T(8,128)} %param.7) | copy-start | bytes 196612
  244.6 30.0 %collective-permute-start.2 = (f32[1,1,256,257]{2,3,1,0:T(8,128)S(1)}, f32[1,1,256,257]{2,3,1,0:T(8,128)S(1)}, u32[]{:S(2)}, u32[]{:S(2)}) collective-permute-start(f32[1,1,256,257]{2,3,1,0:T(8,128)S(1)} %pad_maximum_fusion.2), channel_id=1, source_target_pairs={{0,1},{1,0},{2,3},{3,2},{4,5},{5,4},{6,7},{7,6},{8,9},{9,8},{10,11... | collective-permute-start | bytes 789512 | tf_op jit(solution)/shard_map/ppermute | solution.py:19
  276.0 6.4 %copy-start.17 = (f32[256,64]{0,1:T(8,128)S(1)}, f32[256,64]{0,1:T(8,128)}, u32[]{:S(2)}) copy-start(f32[256,64]{0,1:T(8,128)} %param.8) | copy-start | bytes 196612
  278.0 15.5 %all-to-all-start.7 = ((f32[2,64,256]{2,1,0:T(8,128)}), f32[2,64,256]{2,1,0:T(8,128)S(1)}, u32[]{:S(2)}, u32[]{:S(2)}) async-start(f32[2,64,256]{2,1,0:T(8,128)} %reduce_sum.66), calls=%async_computation.7 | async-start | bytes 262144 | tf_op jit(solution)/shard_map/all_to_all | solution.py:38

commit v6 on v5

--- a/solution.py
+++ b/solution.py
@@ -33,7 +33,6 @@
     block = rows // (sizes[0] * sizes[1] * sizes[2])
     parts = partial_value.reshape(*sizes, block, cols)
     parts = lax.all_to_all(parts, "x", 1, 1, tiled=True).sum(1)
-    parts, companion = lax.optimization_barrier((parts, companion))
     for dim in (1, 0):
         parts = lax.all_to_all(parts, HEAD_AXES[2 * dim], dim, dim, tiled=True).sum(dim)
     return parts, companion

time: 298 us -> 289 us (0.970)
  starting transfers between devices: 77.9 us -> 60.4 us
  blocking collectives: 17.1 us -> 31.4 us
  local copies, waits for them, and re-layouts: 22.9 us -> 19.8 us
  waiting for transfers between devices: 150 us -> 147 us
    all_to_all x3 -> x2, starting transfers between devices: 30.6 us -> 11.4 us  [gather_head(): stacked = lax.all_to_all(copies, axis, 0, 0, tiled=True)]
    all_to_all x1, blocking collectives: 17.1 us -> 31.4 us  [gather_head(): stacked = lax.all_to_all(copies, axis, 0, 0, tiled=True)]
    all_to_all x1 -> x2, waiting for transfers between devices: 11 us -> 20.5 us  [to_strided(): lax.all_to_all(layout, 'seq', split_axis=1, concat_axis=0, tiled=True)]
    ppermute x4, waiting for transfers between devices: 40.8 us -> 33.5 us  [swapped(): lax.ppermute(x, axis, [(i, i ^ 1 << distance) for i in range(lax.axis_siz...]
    all_to_all x1 -> x2, starting transfers between devices: 9.66 us -> 16.5 us  [to_strided(): lax.all_to_all(layout, 'seq', split_axis=1, concat_axis=0, tiled=True)]
    all_to_all x1, waiting for transfers between devices: 43.8 us -> 38.9 us  [scatter_head(): parts = lax.all_to_all(parts, 'x', 1, 1, tiled=True).sum(1)]
    all_to_all x2, waiting for transfers between devices: 22.2 us -> 18.6 us  [to_contiguous(): lax.all_to_all(layout, 'seq', split_axis=0, concat_axis=2, tiled=True)]
    all_to_all x3 -> x2, waiting for transfers between devices: 22.5 us -> 25.1 us  [gather_head(): stacked = lax.all_to_all(copies, axis, 0, 0, tiled=True)]
  transfers between devices with their start and end apart: 13 -> 13, of which waited for: 10 -> 11; matrix products, arithmetic and copies ran while one was open for 11% -> 10% of each run, Pallas kernels for 0% -> 0%
where the time goes in v6:
time: 289 us; the launch traced here: 286 us
  waiting for transfers between devices  147 us (51%)
  starting transfers between devices  60.4 us (21%)
  blocking collectives  31.4 us (11%)
  local copies, waits for them, and re-layouts  19.8 us (7%)
  other arithmetic  13.2 us (5%)
  matrix products  12.7 us (4%)
    all_to_all x1, waiting for transfers between devices, scatter_head(): parts = lax.all_to_all(parts, 'x', 1, 1, tiled=True).sum(1)  38.9 us
    ppermute x4, waiting for transfers between devices, swapped(): lax.ppermute(x, axis, [(i, i ^ 1 << distance) for i in range(lax.axis_siz...  33.5 us
    all_to_all x1, blocking collectives, gather_head(): stacked = lax.all_to_all(copies, axis, 0, 0, tiled=True)  31.4 us
    all_to_all x2, waiting for transfers between devices, gather_head(): stacked = lax.all_to_all(copies, axis, 0, 0, tiled=True)  25.1 us
    all_to_all x2, waiting for transfers between devices, to_strided(): lax.all_to_all(layout, 'seq', split_axis=1, concat_axis=0, tiled=True)  20.5 us
    all_to_all x2, waiting for transfers between devices, to_contiguous(): lax.all_to_all(layout, 'seq', split_axis=0, concat_axis=2, tiled=True)  18.6 us
    all_to_all x2, starting transfers between devices, to_strided(): lax.all_to_all(layout, 'seq', split_axis=1, concat_axis=0, tiled=True)  16.5 us
    all_to_all x2, starting transfers between devices, gather_head(): stacked = lax.all_to_all(copies, axis, 0, 0, tiled=True)  11.4 us
  transfers between devices with their start and end apart: 13, of which 11 were waited for; matrix products, arithmetic and copies ran while one was open for 10% of the time, Pallas kernels for 0%

profile of v6, /device:TPU:1, one launch (start us, length us, event | category | flops | bytes accessed | tf_op | source)
XLA Modules:
  0.0 286.0 jit_solution(10591746082472891781)
XLA Ops:
  1.5 31.4 %all_to_all.90 = bf16[2,256,64]{1,2,0:T(8,128)(2,1)S(1)} all-to-all(bf16[2,256,64]{1,2,0:T(8,128)(2,1)S(1)} %broadcast_in_dim.62), channel_id=1, replica_groups=mesh['seq'=16,'zh'=2,'x'=4,'y'=8] {'zh'}, dimensions={0} | all-to-all | bytes 131072 | tf_op jit(solution)/shard_map/all_to_all | solution.py:47
  33.7 7.0 %all-to-all-start.6 = ((bf16[8,2,256,64]{2,3,1,0:T(8,128)(2,1)}), bf16[8,2,256,64]{2,3,1,0:T(8,128)(2,1)S(1)}, u32[]{:S(2)}, u32[]{:S(2)}) async-start(bf16[8,2,256,64]{2,3,1,0:T(8,128)(2,1)} %broadcast_in_dim.63), calls=%async_computation.6 | async-start | bytes 1048576 | tf_op jit(solution)/shard_map/all_to_all | solution.py:47
  40.7 0.9 copy.97
  42.0 0.9 reshape.277
  42.9 13.3 %all-to-all-done.6 = bf16[8,2,256,64]{2,3,1,0:T(8,128)(2,1)S(1)} async-done(((bf16[8,2,256,64]{2,3,1,0:T(8,128)(2,1)}), bf16[8,2,256,64]{2,3,1,0:T(8,128)(2,1)S(1)}, u32[]{:S(2)}, u32[]{:S(2)}) %all-to-all-start.6) | async-done | bytes 524320 | tf_op jit(solution)/shard_map/all_to_all | solution.py:47
  56.1 10.5 %all-to-all-start = ((f32[16,1,3072]{2,1,0:T(1,128)}), f32[16,1,3072]{2,1,0:T(1,128)S(1)}, u32[]{:S(2)}, u32[]{:S(2)}) async-start(f32[16,1,3072]{2,1,0:T(1,128)} %reshape.277), calls=%async_computation | async-start | bytes 393216 | tf_op jit(solution)/shard_map/all_to_all | solution.py:81
  67.1 2.2 collective-permute-start
  69.3 1.4 constant_dynamic-update-slice_fusion.1
  70.8 10.6 %all-to-all-done = f32[16,1,3072]{2,1,0:T(1,128)S(1)} async-done(((f32[16,1,3072]{2,1,0:T(1,128)}), f32[16,1,3072]{2,1,0:T(1,128)S(1)}, u32[]{:S(2)}, u32[]{:S(2)}) %all-to-all-start) | async-done | bytes 196640 | tf_op jit(solution)/shard_map/all_to_all | solution.py:81
  81.3 1.6 broadcast_in_dim.64
  82.9 4.4 %all-to-all-start.7 = ((bf16[4,8,2,256,64]{3,4,1,2,0:T(8,128)(2,1)}), bf16[4,8,2,256,64]{3,4,1,2,0:T(8,128)(2,1)}, u32[]{:S(2)}, u32[]{:S(2)}) async-start(bf16[4,8,2,256,64]{3,4,1,2,0:T(8,128)(2,1)} %broadcast_in_dim.64), calls=%async_computation.7 | async-start | bytes 4194304 | tf_op jit(solution)/shard_map/all_to_all | solution.py:47
  87.4 1.3 constant_dynamic-update-slice_fusion
  90.6 1.8 reduce.7
  92.4 1.0 reshape.278
  94.6 2.2 collective-permute-start.1
  96.8 1.3 fusion.12
  98.1 3.3 %collective-permute-done.1 = f32[8,1,32,32]{2,3,0,1:T(8,128)S(1)} collective-permute-done((f32[8,1,32,32]{2,3,0,1:T(8,128)S(1)}, f32[8,1,32,32]{2,3,0,1:T(8,128)S(1)}, u32[]{:S(2)}, u32[]{:S(2)}) %collective-permute-start.1) | collective-permute-done | bytes 32800 | tf_op jit(solution)/shard_map/ppermute | solution.py:19
  101.4 11.9 %all-to-all-done.7 = bf16[4,8,2,256,64]{3,4,1,2,0:T(8,128)(2,1)} async-done(((bf16[4,8,2,256,64]{3,4,1,2,0:T(8,128)(2,1)}), bf16[4,8,2,256,64]{3,4,1,2,0:T(8,128)(2,1)}, u32[]{:S(2)}, u32[]{:S(2)}) %all-to-all-start.7) | async-done | bytes 2097184 | tf_op jit(solution)/shard_map/all_to_all | solution.py:47
  113.3 1.7 copy.113
  115.1 1.3 convolution_bitcast_fusion.5
  117.3 6.0 %all-to-all-start.8 = ((f32[16,1,1024]{2,1,0:T(1,128)}), f32[16,1,1024]{2,1,0:T(1,128)S(1)}, u32[]{:S(2)}, u32[]{:S(2)}) async-start(f32[16,1,1024]{2,1,0:T(1,128)} %reshape.281), calls=%async_computation.8 | async-start | bytes 131072 | tf_op jit(solution)/shard_map/all_to_all | solution.py:81
  123.4 10.0 %all-to-all-done.8 = f32[16,1,1024]{2,1,0:T(1,128)S(1)} async-done(((f32[16,1,1024]{2,1,0:T(1,128)}), f32[16,1,1024]{2,1,0:T(1,128)S(1)}, u32[]{:S(2)}, u32[]{:S(2)}) %all-to-all-start.8) | async-done | bytes 65568 | tf_op jit(solution)/shard_map/all_to_all | solution.py:81
  134.3 1.4 fusion.19
  136.5 4.9 %all-to-all-start.1 = ((f32[16,1,1024]{2,1,0:T(1,128)}), f32[16,1,1024]{2,1,0:T(1,128)}, u32[]{:S(2)}, u32[]{:S(2)}) async-start(f32[16,1,1024]{2,1,0:T(1,128)} %reshape.279), calls=%async_computation.1 | async-start | bytes 131072 | tf_op jit(solution)/shard_map/all_to_all | solution.py:89
  141.4 1.4 fusion.11
  142.8 1.1 fusion.43
  144.0 7.7 %all-to-all-done.1 = f32[16,1,1024]{2,1,0:T(1,128)} async-done(((f32[16,1,1024]{2,1,0:T(1,128)}), f32[16,1,1024]{2,1,0:T(1,128)}, u32[]{:S(2)}, u32[]{:S(2)}) %all-to-all-start.1) | async-done | bytes 65568 | tf_op jit(solution)/shard_map/all_to_all | solution.py:89
  151.6 1.6 reduce.8
  153.5 3.5 %fusion.15 = f32[4096,256]{1,0:T(8,128)S(1)} fusion(f32[128,4096]{1,0:T(8,128)S(1)} %constant_dynamic-update-slice_fusion, f32[256,64]{0,1:T(8,128)S(1)} %copy.109, f32[256,64]{0,1:T(8,128)S(1)} %get-tuple-element.11), kind=kOutput, calls=%fused_computation.40 | convolution fusion | flops 1610645504 | bytes 6422528 | tf_op jit(solution)/shard_map/dot_general | solution.py:130
  157.0 2.3 copy.110
  159.3 5.0 %all-to-all-start.2 = ((f32[2,4,8,64,256]{4,3,2,0,1:T(8,128)}), f32[2,4,8,64,256]{4,3,2,0,1:T(8,128)}, u32[]{:S(2)}, u32[]{:S(2)}) async-start(f32[2,4,8,64,256]{4,3,2,0,1:T(8,128)} %copy.110), calls=%async_computation.2 | async-start | bytes 8388608 | tf_op jit(solution)/shard_map/all_to_all | solution.py:35
  164.7 2.4 collective-permute-start.3
  167.4 4.0 %collective-permute-done.3 = f32[8,1,32,33]{2,3,0,1:T(8,128)S(1)} collective-permute-done((f32[8,1,32,33]{2,3,0,1:T(8,128)S(1)}, f32[8,1,32,33]{2,3,0,1:T(8,128)S(1)}, u32[]{:S(2)}, u32[]{:S(2)}) %collective-permute-start.3) | collective-permute-done | bytes 33824 | tf_op jit(solution)/shard_map/ppermute | solution.py:19
  172.3 0.9 reshape.283
  173.2 38.9 %all-to-all-done.2 = f32[2,4,8,64,256]{4,3,2,0,1:T(8,128)} async-done(((f32[2,4,8,64,256]{4,3,2,0,1:T(8,128)}), f32[2,4,8,64,256]{4,3,2,0,1:T(8,128)}, u32[]{:S(2)}, u32[]{:S(2)}) %all-to-all-start.2) | async-done | bytes 4194336 | tf_op jit(solution)/shard_map/all_to_all | solution.py:35
  212.2 5.5 %all-to-all-start.9 = ((f32[16,1,3072]{2,1,0:T(1,128)}), f32[16,1,3072]{2,1,0:T(1,128)S(1)}, u32[]{:S(2)}, u32[]{:S(2)}) async-start(f32[16,1,3072]{2,1,0:T(1,128)} %reshape.283), calls=%async_computation.9 | async-start | bytes 393216 | tf_op jit(solution)/shard_map/all_to_all | solution.py:89
  217.7 2.6 reduce_sum.65
  220.3 1.1 copy.111
  221.4 10.9 %all-to-all-done.9 = f32[16,1,3072]{2,1,0:T(1,128)S(1)} async-done(((f32[16,1,3072]{2,1,0:T(1,128)}), f32[16,1,3072]{2,1,0:T(1,128)S(1)}, u32[]{:S(2)}, u32[]{:S(2)}) %all-to-all-start.9) | async-done | bytes 196640 | tf_op jit(solution)/shard_map/all_to_all | solution.py:89
  232.3 3.6 %all-to-all-start.3 = ((f32[2,8,64,256]{3,2,0,1:T(8,128)}), f32[2,8,64,256]{3,2,0,1:T(8,128)S(1)}, u32[]{:S(2)}, u32[]{:S(2)}) async-start(f32[2,8,64,256]{3,2,0,1:T(8,128)} %copy.111), calls=%async_computation.3 | async-start | bytes 2097152 | tf_op jit(solution)/shard_map/all_to_all | solution.py:37
  236.4 3.4 %collective-permute-start.2 = (f32[1,1,256,257]{2,3,1,0:T(8,128)S(1)}, f32[1,1,256,257]{2,3,1,0:T(8,128)S(1)}, u32[]{:S(2)}, u32[]{:S(2)}) collective-permute-start(f32[1,1,256,257]{2,3,1,0:T(8,128)S(1)} %pad_maximum_fusion.2), channel_id=1, source_target_pairs={{0,1},{1,0},{2,3},{3,2},{4,5},{5,4},{6,7},{7,6},{8,9},{9,8},{10,11... | collective-permute-start | bytes 789512 | tf_op jit(solution)/shard_map/ppermute | solution.py:19
  239.8 26.2 %collective-permute-done.2 = f32[1,1,256,257]{2,3,1,0:T(8,128)S(1)} collective-permute-done((f32[1,1,256,257]{2,3,1,0:T(8,128)S(1)}, f32[1,1,256,257]{2,3,1,0:T(8,128)S(1)}, u32[]{:S(2)}, u32[]{:S(2)}) %collective-permute-start.2) | collective-permute-done | bytes 263200 | tf_op jit(solution)/shard_map/ppermute | solution.py:19
  266.0 1.1 reduce.9
  267.7 1.0 fusion.3
  269.4 3.4 %all-to-all-start.4 = ((f32[2,64,256]{2,1,0:T(8,128)}), f32[2,64,256]{2,1,0:T(8,128)S(1)}, u32[]{:S(2)}, u32[]{:S(2)}) async-start(f32[2,64,256]{2,1,0:T(8,128)} %reduce_sum.66), calls=%async_computation.4 | async-start | bytes 262144 | tf_op jit(solution)/shard_map/all_to_all | solution.py:37
  272.8 1.0 fusion.2
  273.9 0.9 fusion.4
  274.8 10.5 %all-to-all-done.4 = f32[2,64,256]{2,1,0:T(8,128)S(1)} async-done(((f32[2,64,256]{2,1,0:T(8,128)}), f32[2,64,256]{2,1,0:T(8,128)S(1)}, u32[]{:S(2)}, u32[]{:S(2)}) %all-to-all-start.4) | async-done | bytes 131104 | tf_op jit(solution)/shard_map/all_to_all | solution.py:37
  (78 shorter events, 12.4 us)
Async XLA Ops:
  0.6 41.0 %copy-start.7 = (f32[256,64]{0,1:T(8,128)S(1)}, f32[256,64]{0,1:T(8,128)}, u32[]{:S(2)}) copy-start(f32[256,64]{0,1:T(8,128)} %param.8) | copy-start | bytes 196612
  0.6 41.1 %copy-start.3 = (f32[256,64]{0,1:T(8,128)S(1)}, f32[256,64]{0,1:T(8,128)}, u32[]{:S(2)}) copy-start(f32[256,64]{0,1:T(8,128)} %param.9) | copy-start | bytes 196612
  33.7 33.0 %copy-start.5 = (f32[256,64]{0,1:T(8,128)S(1)}, f32[256,64]{0,1:T(8,128)}, u32[]{:S(2)}) copy-start(f32[256,64]{0,1:T(8,128)} %param.7) | copy-start | bytes 196612
  33.7 22.4 %all-to-all-start.6 = ((bf16[8,2,256,64]{2,3,1,0:T(8,128)(2,1)}), bf16[8,2,256,64]{2,3,1,0:T(8,128)(2,1)S(1)}, u32[]{:S(2)}, u32[]{:S(2)}) async-start(bf16[8,2,256,64]{2,3,1,0:T(8,128)(2,1)} %broadcast_in_dim.63), calls=%async_computation.6 | async-start | bytes 1048576 | tf_op jit(solution)/shard_map/all_to_all | solution.py:47
  56.1 11.0 %copy-start = (bf16[8,2,256,64]{2,3,1,0:T(8,128)(2,1)}, bf16[8,2,256,64]{2,3,1,0:T(8,128)(2,1)S(1)}, u32[]{:S(2)}) copy-start(bf16[8,2,256,64]{2,3,1,0:T(8,128)(2,1)S(1)} %all-to-all-done.6) | copy-start | bytes 1572868
  56.1 25.2 %all-to-all-start = ((f32[16,1,3072]{2,1,0:T(1,128)}), f32[16,1,3072]{2,1,0:T(1,128)S(1)}, u32[]{:S(2)}, u32[]{:S(2)}) async-start(f32[16,1,3072]{2,1,0:T(1,128)} %reshape.277), calls=%async_computation | async-start | bytes 393216 | tf_op jit(solution)/shard_map/all_to_all | solution.py:81
  67.1 22.2 %collective-permute-start = (f32[1,1,256,256]{2,3,1,0:T(8,128)S(1)}, f32[1,1,256,256]{2,3,1,0:T(8,128)S(1)}, u32[]{:S(2)}, u32[]{:S(2)}) collective-permute-start(f32[1,1,256,256]{2,3,1,0:T(8,128)S(1)} %convolution_bitcast_fusion.1), channel_id=1, source_target_pairs={{0,1},{1,0},{2,3},{3,2},{4,5},{5,4},{6,7},{7,6},{8,9},{9,8},{10,11... | collective-permute-start | bytes 786440 | tf_op jit(solution)/shard_map/ppermute | solution.py:19
  69.3 1.4 copy-start.1
  82.9 30.4 %all-to-all-start.7 = ((bf16[4,8,2,256,64]{3,4,1,2,0:T(8,128)(2,1)}), bf16[4,8,2,256,64]{3,4,1,2,0:T(8,128)(2,1)}, u32[]{:S(2)}, u32[]{:S(2)}) async-start(bf16[4,8,2,256,64]{3,4,1,2,0:T(8,128)(2,1)} %broadcast_in_dim.64), calls=%async_computation.7 | async-start | bytes 4194304 | tf_op jit(solution)/shard_map/all_to_all | solution.py:47
  87.3 1.3 copy-start.9
  94.6 6.8 %collective-permute-start.1 = (f32[8,1,32,32]{2,3,0,1:T(8,128)S(1)}, f32[8,1,32,32]{2,3,0,1:T(8,128)S(1)}, u32[]{:S(2)}, u32[]{:S(2)}) collective-permute-start(f32[8,1,32,32]{2,3,0,1:T(8,128)S(1)} %convolution_bitcast_fusion.4), channel_id=1, source_target_pairs={{0,1},{1,0},{2,3},{3,2},{4,5},{5,4},{6,7},{7,6},{8,9},{9,8},{10,11... | collective-permute-start | bytes 98312 | tf_op jit(solution)/shard_map/ppermute | solution.py:19
  117.3 16.1 %all-to-all-start.8 = ((f32[16,1,1024]{2,1,0:T(1,128)}), f32[16,1,1024]{2,1,0:T(1,128)S(1)}, u32[]{:S(2)}, u32[]{:S(2)}) async-start(f32[16,1,1024]{2,1,0:T(1,128)} %reshape.281), calls=%async_computation.8 | async-start | bytes 131072 | tf_op jit(solution)/shard_map/all_to_all | solution.py:81
  136.5 15.1 %all-to-all-start.1 = ((f32[16,1,1024]{2,1,0:T(1,128)}), f32[16,1,1024]{2,1,0:T(1,128)}, u32[]{:S(2)}, u32[]{:S(2)}) async-start(f32[16,1,1024]{2,1,0:T(1,128)} %reshape.279), calls=%async_computation.1 | async-start | bytes 131072 | tf_op jit(solution)/shard_map/all_to_all | solution.py:89
  159.3 5.0 %copy-start.2 = (f32[32,8,1,64]{3,1,0,2:T(8,128)S(1)}, f32[32,8,1,64]{3,1,0,2:T(8,128)}, u32[]{:S(2)}) copy-start(f32[32,8,1,64]{3,1,0,2:T(8,128)} %get-tuple-element.7) | copy-start | bytes 196612
  159.3 52.9 %all-to-all-start.2 = ((f32[2,4,8,64,256]{4,3,2,0,1:T(8,128)}), f32[2,4,8,64,256]{4,3,2,0,1:T(8,128)}, u32[]{:S(2)}, u32[]{:S(2)}) async-start(f32[2,4,8,64,256]{4,3,2,0,1:T(8,128)} %copy.110), calls=%async_computation.2 | async-start | bytes 8388608 | tf_op jit(solution)/shard_map/all_to_all | solution.py:35
  164.7 6.7 %collective-permute-start.3 = (f32[8,1,32,33]{2,3,0,1:T(8,128)S(1)}, f32[8,1,32,33]{2,3,0,1:T(8,128)S(1)}, u32[]{:S(2)}, u32[]{:S(2)}) collective-permute-start(f32[8,1,32,33]{2,3,0,1:T(8,128)S(1)} %pad_maximum_fusion.3), channel_id=1, source_target_pairs={{0,1},{1,0},{2,3},{3,2},{4,5},{5,4},{6,7},{7,6},{8,9},{9,8},{10,11... | collective-permute-start | bytes 101384 | tf_op jit(solution)/shard_map/ppermute | solution.py:19
  212.2 20.2 %all-to-all-start.9 = ((f32[16,1,3072]{2,1,0:T(1,128)}), f32[16,1,3072]{2,1,0:T(1,128)S(1)}, u32[]{:S(2)}, u32[]{:S(2)}) async-start(f32[16,1,3072]{2,1,0:T(1,128)} %reshape.283), calls=%async_computation.9 | async-start | bytes 393216 | tf_op jit(solution)/shard_map/all_to_all | solution.py:89
  220.3 15.6 %copy-start.4 = (f32[256,64]{0,1:T(8,128)S(1)}, f32[256,64]{0,1:T(8,128)}, u32[]{:S(2)}) copy-start(f32[256,64]{0,1:T(8,128)} %param.9) | copy-start | bytes 196612
  232.3 36.4 %all-to-all-start.3 = ((f32[2,8,64,256]{3,2,0,1:T(8,128)}), f32[2,8,64,256]{3,2,0,1:T(8,128)S(1)}, u32[]{:S(2)}, u32[]{:S(2)}) async-start(f32[2,8,64,256]{3,2,0,1:T(8,128)} %copy.111), calls=%async_computation.3 | async-start | bytes 2097152 | tf_op jit(solution)/shard_map/all_to_all | solution.py:37
  236.4 31.3 %copy-start.6 = (f32[256,64]{0,1:T(8,128)S(1)}, f32[256,64]{0,1:T(8,128)}, u32[]{:S(2)}) copy-start(f32[256,64]{0,1:T(8,128)} %param.7) | copy-start | bytes 196612
  236.4 29.6 %collective-permute-start.2 = (f32[1,1,256,257]{2,3,1,0:T(8,128)S(1)}, f32[1,1,256,257]{2,3,1,0:T(8,128)S(1)}, u32[]{:S(2)}, u32[]{:S(2)}) collective-permute-start(f32[1,1,256,257]{2,3,1,0:T(8,128)S(1)} %pad_maximum_fusion.2), channel_id=1, source_target_pairs={{0,1},{1,0},{2,3},{3,2},{4,5},{5,4},{6,7},{7,6},{8,9},{9,8},{10,11... | collective-permute-start | bytes 789512 | tf_op jit(solution)/shard_map/ppermute | solution.py:19
  267.4 6.4 %copy-start.8 = (f32[256,64]{0,1:T(8,128)S(1)}, f32[256,64]{0,1:T(8,128)}, u32[]{:S(2)}) copy-start(f32[256,64]{0,1:T(8,128)} %param.8) | copy-start | bytes 196612
  269.4 16.0 %all-to-all-start.4 = ((f32[2,64,256]{2,1,0:T(8,128)}), f32[2,64,256]{2,1,0:T(8,128)S(1)}, u32[]{:S(2)}, u32[]{:S(2)}) async-start(f32[2,64,256]{2,1,0:T(8,128)} %reduce_sum.66), calls=%async_computation.4 | async-start | bytes 262144 | tf_op jit(solution)/shard_map/all_to_all | solution.py:37

commit v7 on v6

--- a/solution.py
+++ b/solution.py
@@ -41,11 +41,12 @@
 def gather_head(piece):
     rows, cols = piece.shape
     stacked = piece
-    for axis in ("zh", "y", "x"):
+    for axis in (("zh", "y"), "x"):
         count = lax.axis_size(axis)
         copies = jnp.broadcast_to(stacked[None], (count,) + stacked.shape)
         stacked = lax.all_to_all(copies, axis, 0, 0, tiled=True)
-    order = stacked.reshape(stacked.shape[:3] + (rows, cols)).transpose(3, 2, 0, 1, 4)
+    zh, ys = lax.axis_size("zh"), lax.axis_size("y")
+    order = stacked.reshape((stacked.shape[0], zh, ys, rows, cols)).transpose(3, 1, 0, 2, 4)
     return order.reshape(rows, -1)
 
 

time: 289 us -> 296 us (1.024)
  starting transfers between devices: 60.4 us -> 73.1 us
  waiting for transfers between devices: 147 us -> 141 us
    all_to_all x2 -> x1, waiting for transfers between devices: 20.5 us -> 9.96 us  [to_strided(): lax.all_to_all(layout, 'seq', split_axis=1, concat_axis=0, tiled=True)]
    all_to_all x2, starting transfers between devices: 11.4 us -> 20.8 us  [gather_head(): stacked = lax.all_to_all(copies, axis, 0, 0, tiled=True)]
    all_to_all x2, waiting for transfers between devices: 25.1 us -> 30.3 us  [gather_head(): stacked = lax.all_to_all(copies, axis, 0, 0, tiled=True)]
    ppermute x4, starting transfers between devices: 10.2 us -> 13.9 us  [swapped(): lax.ppermute(x, axis, [(i, i ^ 1 << distance) for i in range(lax.axis_siz...]
    unnamed x35 -> x31, local copies, waits for them, and re-layouts: 7.43 us -> 8.39 us
    all_to_all x2 -> x1, starting transfers between devices: 16.5 us -> 16.1 us  [to_strided(): lax.all_to_all(layout, 'seq', split_axis=1, concat_axis=0, tiled=True)]
  transfers between devices with their start and end apart: 13 -> 12, of which waited for: 11 -> 10; matrix products, arithmetic and copies ran while one was open for 10% -> 9% of each run, Pallas kernels for 0% -> 0%
where the time goes in v7:
time: 296 us; the launch traced here: 293 us
  waiting for transfers between devices  141 us (48%)
  starting transfers between devices  73.1 us (25%)
  blocking collectives  31.7 us (11%)
  local copies, waits for them, and re-layouts  19.9 us (7%)
  other arithmetic  13.2 us (4%)
  matrix products  12.8 us (4%)
    all_to_all x1, waiting for transfers between devices, scatter_head(): parts = lax.all_to_all(parts, 'x', 1, 1, tiled=True).sum(1)  38.9 us
    ppermute x4, waiting for transfers between devices, swapped(): lax.ppermute(x, axis, [(i, i ^ 1 << distance) for i in range(lax.axis_siz...  33 us
    all_to_all x1, blocking collectives, to_strided(): lax.all_to_all(layout, 'seq', split_axis=1, concat_axis=0, tiled=True)  31.7 us
    all_to_all x2, waiting for transfers between devices, gather_head(): stacked = lax.all_to_all(copies, axis, 0, 0, tiled=True)  30.3 us
    all_to_all x2, starting transfers between devices, gather_head(): stacked = lax.all_to_all(copies, axis, 0, 0, tiled=True)  20.8 us
    all_to_all x2, waiting for transfers between devices, to_contiguous(): lax.all_to_all(layout, 'seq', split_axis=0, concat_axis=2, tiled=True)  18.6 us
    all_to_all x1, starting transfers between devices, to_strided(): lax.all_to_all(layout, 'seq', split_axis=1, concat_axis=0, tiled=True)  16.1 us
    ppermute x4, starting transfers between devices, swapped(): lax.ppermute(x, axis, [(i, i ^ 1 << distance) for i in range(lax.axis_siz...  13.9 us
  transfers between devices with their start and end apart: 12, of which 10 were waited for; matrix products, arithmetic and copies ran while one was open for 9% of the time, Pallas kernels for 0%

profile of v7, /device:TPU:1, one launch (start us, length us, event | category | flops | bytes accessed | tf_op | source)
XLA Modules:
  0.0 292.8 jit_solution(3019500000075711157)
XLA Ops:
  0.6 0.9 copy.120
  1.6 0.9 copy.121
  2.5 0.9 copy.122
  3.9 31.7 %all_to_all.85 = f32[16,1,3072]{2,1,0:T(1,128)S(1)} all-to-all(f32[16,1,3072]{2,1,0:T(1,128)S(1)} %reshape.280), channel_id=1, replica_groups=mesh['seq'=16,'zh'=2,'x'=4,'y'=8] {'seq'}, dimensions={0} | all-to-all | bytes 393216 | tf_op jit(solution)/shard_map/all_to_all | solution.py:82
  35.6 0.8 broadcast_in_dim.56
  36.4 16.3 %all-to-all-start.5 = ((bf16[16,256,64]{1,2,0:T(8,128)(2,1)}), bf16[16,256,64]{1,2,0:T(8,128)(2,1)S(1)}, u32[]{:S(2)}, u32[]{:S(2)}) async-start(bf16[16,256,64]{1,2,0:T(8,128)(2,1)} %broadcast_in_dim.56), calls=%async_computation.5 | async-start | bytes 1048576 | tf_op jit(solution)/shard_map/all_to_all | solution.py:47
  53.2 3.3 %collective-permute-start = (f32[1,1,256,256]{2,3,1,0:T(8,128)S(1)}, f32[1,1,256,256]{2,3,1,0:T(8,128)S(1)}, u32[]{:S(2)}, u32[]{:S(2)}) collective-permute-start(f32[1,1,256,256]{2,3,1,0:T(8,128)S(1)} %convolution_bitcast_fusion.1), channel_id=1, source_target_pairs={{0,1},{1,0},{2,3},{3,2},{4,5},{5,4},{6,7},{7,6},{8,9},{9,8},{10,11... | collective-permute-start | bytes 786440 | tf_op jit(solution)/shard_map/ppermute | solution.py:19
  56.5 1.3 constant_dynamic-update-slice_fusion.1
  57.8 20.3 %all-to-all-done.5 = bf16[16,256,64]{1,2,0:T(8,128)(2,1)S(1)} async-done(((bf16[16,256,64]{1,2,0:T(8,128)(2,1)}), bf16[16,256,64]{1,2,0:T(8,128)(2,1)S(1)}, u32[]{:S(2)}, u32[]{:S(2)}) %all-to-all-start.5) | async-done | bytes 524320 | tf_op jit(solution)/shard_map/all_to_all | solution.py:47
  78.0 1.6 broadcast_in_dim.57
  79.6 4.4 %all-to-all-start.6 = ((bf16[4,16,256,64]{2,3,1,0:T(8,128)(2,1)}), bf16[4,16,256,64]{2,3,1,0:T(8,128)(2,1)}, u32[]{:S(2)}, u32[]{:S(2)}) async-start(bf16[4,16,256,64]{2,3,1,0:T(8,128)(2,1)} %broadcast_in_dim.57), calls=%async_computation.6 | async-start | bytes 4194304 | tf_op jit(solution)/shard_map/all_to_all | solution.py:47
  84.1 1.3 constant_dynamic-update-slice_fusion
  87.3 1.8 reduce.7
  89.1 1.0 reshape.281
  91.3 4.8 %collective-permute-start.1 = (f32[8,1,32,32]{2,3,0,1:T(8,128)S(1)}, f32[8,1,32,32]{2,3,0,1:T(8,128)S(1)}, u32[]{:S(2)}, u32[]{:S(2)}) collective-permute-start(f32[8,1,32,32]{2,3,0,1:T(8,128)S(1)} %convolution_bitcast_fusion.4), channel_id=1, source_target_pairs={{0,1},{1,0},{2,3},{3,2},{4,5},{5,4},{6,7},{7,6},{8,9},{9,8},{10,11... | collective-permute-start | bytes 98312 | tf_op jit(solution)/shard_map/ppermute | solution.py:19
  96.1 1.3 fusion.12
  97.5 2.4 collective-permute-done.1
  99.9 10.1 %all-to-all-done.6 = bf16[4,16,256,64]{2,3,1,0:T(8,128)(2,1)} async-done(((bf16[4,16,256,64]{2,3,1,0:T(8,128)(2,1)}), bf16[4,16,256,64]{2,3,1,0:T(8,128)(2,1)}, u32[]{:S(2)}, u32[]{:S(2)}) %all-to-all-start.6) | async-done | bytes 2097184 | tf_op jit(solution)/shard_map/all_to_all | solution.py:47
  110.0 1.7 copy.135
  111.7 1.3 convolution_bitcast_fusion.5
  114.0 16.1 %all-to-all-start.7 = ((f32[16,1,1024]{2,1,0:T(1,128)}), f32[16,1,1024]{2,1,0:T(1,128)S(1)}, u32[]{:S(2)}, u32[]{:S(2)}) async-start(f32[16,1,1024]{2,1,0:T(1,128)} %reshape.284), calls=%async_computation.7 | async-start | bytes 131072 | tf_op jit(solution)/shard_map/all_to_all | solution.py:82
  130.1 10.0 %all-to-all-done.7 = f32[16,1,1024]{2,1,0:T(1,128)S(1)} async-done(((f32[16,1,1024]{2,1,0:T(1,128)}), f32[16,1,1024]{2,1,0:T(1,128)S(1)}, u32[]{:S(2)}, u32[]{:S(2)}) %all-to-all-start.7) | async-done | bytes 65568 | tf_op jit(solution)/shard_map/all_to_all | solution.py:82
  141.0 1.4 fusion.19
  143.2 4.9 %all-to-all-start.1 = ((f32[16,1,1024]{2,1,0:T(1,128)}), f32[16,1,1024]{2,1,0:T(1,128)}, u32[]{:S(2)}, u32[]{:S(2)}) async-start(f32[16,1,1024]{2,1,0:T(1,128)} %reshape.282), calls=%async_computation.1 | async-start | bytes 131072 | tf_op jit(solution)/shard_map/all_to_all | solution.py:90
  148.1 1.4 fusion.11
  149.5 1.1 fusion.43
  150.7 7.7 %all-to-all-done.1 = f32[16,1,1024]{2,1,0:T(1,128)} async-done(((f32[16,1,1024]{2,1,0:T(1,128)}), f32[16,1,1024]{2,1,0:T(1,128)}, u32[]{:S(2)}, u32[]{:S(2)}) %all-to-all-start.1) | async-done | bytes 65568 | tf_op jit(solution)/shard_map/all_to_all | solution.py:90
  158.4 1.6 reduce.8
  160.2 3.5 %fusion.15 = f32[4096,256]{1,0:T(8,128)S(1)} fusion(f32[128,4096]{1,0:T(8,128)S(1)} %constant_dynamic-update-slice_fusion, f32[256,64]{0,1:T(8,128)S(1)} %copy.132, f32[256,64]{0,1:T(8,128)S(1)} %get-tuple-element.11), kind=kOutput, calls=%fused_computation.40 | convolution fusion | flops 1610645504 | bytes 6422528 | tf_op jit(solution)/shard_map/dot_general | solution.py:131
  163.7 2.3 copy.133
  166.0 5.0 %all-to-all-start.2 = ((f32[2,4,8,64,256]{4,3,2,0,1:T(8,128)}), f32[2,4,8,64,256]{4,3,2,0,1:T(8,128)}, u32[]{:S(2)}, u32[]{:S(2)}) async-start(f32[2,4,8,64,256]{4,3,2,0,1:T(8,128)} %copy.133), calls=%async_computation.2 | async-start | bytes 8388608 | tf_op jit(solution)/shard_map/all_to_all | solution.py:35
  171.4 2.3 collective-permute-start.3
  174.0 4.1 %collective-permute-done.3 = f32[8,1,32,33]{2,3,0,1:T(8,128)S(1)} collective-permute-done((f32[8,1,32,33]{2,3,0,1:T(8,128)S(1)}, f32[8,1,32,33]{2,3,0,1:T(8,128)S(1)}, u32[]{:S(2)}, u32[]{:S(2)}) %collective-permute-start.3) | collective-permute-done | bytes 33824 | tf_op jit(solution)/shard_map/ppermute | solution.py:19
  179.0 0.9 reshape.286
  179.9 38.9 %all-to-all-done.2 = f32[2,4,8,64,256]{4,3,2,0,1:T(8,128)} async-done(((f32[2,4,8,64,256]{4,3,2,0,1:T(8,128)}), f32[2,4,8,64,256]{4,3,2,0,1:T(8,128)}, u32[]{:S(2)}, u32[]{:S(2)}) %all-to-all-start.2) | async-done | bytes 4194336 | tf_op jit(solution)/shard_map/all_to_all | solution.py:35
  218.9 5.5 %all-to-all-start.8 = ((f32[16,1,3072]{2,1,0:T(1,128)}), f32[16,1,3072]{2,1,0:T(1,128)S(1)}, u32[]{:S(2)}, u32[]{:S(2)}) async-start(f32[16,1,3072]{2,1,0:T(1,128)} %reshape.286), calls=%async_computation.8 | async-start | bytes 393216 | tf_op jit(solution)/shard_map/all_to_all | solution.py:90
  224.4 2.6 reduce_sum.65
  227.0 1.1 copy.134
  228.1 10.9 %all-to-all-done.8 = f32[16,1,3072]{2,1,0:T(1,128)S(1)} async-done(((f32[16,1,3072]{2,1,0:T(1,128)}), f32[16,1,3072]{2,1,0:T(1,128)S(1)}, u32[]{:S(2)}, u32[]{:S(2)}) %all-to-all-start.8) | async-done | bytes 196640 | tf_op jit(solution)/shard_map/all_to_all | solution.py:90
  239.0 3.7 %all-to-all-start.3 = ((f32[2,8,64,256]{3,2,0,1:T(8,128)}), f32[2,8,64,256]{3,2,0,1:T(8,128)S(1)}, u32[]{:S(2)}, u32[]{:S(2)}) async-start(f32[2,8,64,256]{3,2,0,1:T(8,128)} %copy.134), calls=%async_computation.3 | async-start | bytes 2097152 | tf_op jit(solution)/shard_map/all_to_all | solution.py:37
  243.2 3.5 %collective-permute-start.2 = (f32[1,1,256,257]{2,3,1,0:T(8,128)S(1)}, f32[1,1,256,257]{2,3,1,0:T(8,128)S(1)}, u32[]{:S(2)}, u32[]{:S(2)}) collective-permute-start(f32[1,1,256,257]{2,3,1,0:T(8,128)S(1)} %pad_maximum_fusion.2), channel_id=1, source_target_pairs={{0,1},{1,0},{2,3},{3,2},{4,5},{5,4},{6,7},{7,6},{8,9},{9,8},{10,11... | collective-permute-start | bytes 789512 | tf_op jit(solution)/shard_map/ppermute | solution.py:19
  246.7 26.5 %collective-permute-done.2 = f32[1,1,256,257]{2,3,1,0:T(8,128)S(1)} collective-permute-done((f32[1,1,256,257]{2,3,1,0:T(8,128)S(1)}, f32[1,1,256,257]{2,3,1,0:T(8,128)S(1)}, u32[]{:S(2)}, u32[]{:S(2)}) %collective-permute-start.2) | collective-permute-done | bytes 263200 | tf_op jit(solution)/shard_map/ppermute | solution.py:19
  273.3 1.1 reduce.9
  274.9 1.0 fusion.3
  276.6 3.4 %all-to-all-start.4 = ((f32[2,64,256]{2,1,0:T(8,128)}), f32[2,64,256]{2,1,0:T(8,128)S(1)}, u32[]{:S(2)}, u32[]{:S(2)}) async-start(f32[2,64,256]{2,1,0:T(8,128)} %reduce_sum.66), calls=%async_computation.4 | async-start | bytes 262144 | tf_op jit(solution)/shard_map/all_to_all | solution.py:37
  280.0 1.0 fusion.2
  281.1 0.9 fusion.4
  282.1 10.1 %all-to-all-done.4 = f32[2,64,256]{2,1,0:T(8,128)S(1)} async-done(((f32[2,64,256]{2,1,0:T(8,128)}), f32[2,64,256]{2,1,0:T(8,128)S(1)}, u32[]{:S(2)}, u32[]{:S(2)}) %all-to-all-start.4) | async-done | bytes 131104 | tf_op jit(solution)/shard_map/all_to_all | solution.py:37
  (70 shorter events, 10.8 us)
Async XLA Ops:
  0.6 35.0 %copy-start.6 = (bf16[256,64]{0,1:T(8,128)(2,1)S(1)}, bf16[256,64]{0,1:T(8,128)(2,1)}, u32[]{:S(2)}) copy-start(bf16[256,64]{0,1:T(8,128)(2,1)} %param.13) | copy-start | bytes 98308
  3.5 49.3 %copy-start.2 = (f32[256,64]{0,1:T(8,128)S(1)}, f32[256,64]{0,1:T(8,128)}, u32[]{:S(2)}) copy-start(f32[256,64]{0,1:T(8,128)} %param.7) | copy-start | bytes 196612
  3.5 49.3 %copy-start.4 = (f32[256,64]{0,1:T(8,128)S(1)}, f32[256,64]{0,1:T(8,128)}, u32[]{:S(2)}) copy-start(f32[256,64]{0,1:T(8,128)} %param.8) | copy-start | bytes 196612
  36.4 41.6 %all-to-all-start.5 = ((bf16[16,256,64]{1,2,0:T(8,128)(2,1)}), bf16[16,256,64]{1,2,0:T(8,128)(2,1)S(1)}, u32[]{:S(2)}, u32[]{:S(2)}) async-start(bf16[16,256,64]{1,2,0:T(8,128)(2,1)} %broadcast_in_dim.56), calls=%async_computation.5 | async-start | bytes 1048576 | tf_op jit(solution)/shard_map/all_to_all | solution.py:47
  53.2 32.8 %collective-permute-start = (f32[1,1,256,256]{2,3,1,0:T(8,128)S(1)}, f32[1,1,256,256]{2,3,1,0:T(8,128)S(1)}, u32[]{:S(2)}, u32[]{:S(2)}) collective-permute-start(f32[1,1,256,256]{2,3,1,0:T(8,128)S(1)} %convolution_bitcast_fusion.1), channel_id=1, source_target_pairs={{0,1},{1,0},{2,3},{3,2},{4,5},{5,4},{6,7},{7,6},{8,9},{9,8},{10,11... | collective-permute-start | bytes 786440 | tf_op jit(solution)/shard_map/ppermute | solution.py:19
  79.6 30.3 %all-to-all-start.6 = ((bf16[4,16,256,64]{2,3,1,0:T(8,128)(2,1)}), bf16[4,16,256,64]{2,3,1,0:T(8,128)(2,1)}, u32[]{:S(2)}, u32[]{:S(2)}) async-start(bf16[4,16,256,64]{2,3,1,0:T(8,128)(2,1)} %broadcast_in_dim.57), calls=%async_computation.6 | async-start | bytes 4194304 | tf_op jit(solution)/shard_map/all_to_all | solution.py:47
  84.1 1.3 copy-start.7
  91.3 8.6 %collective-permute-start.1 = (f32[8,1,32,32]{2,3,0,1:T(8,128)S(1)}, f32[8,1,32,32]{2,3,0,1:T(8,128)S(1)}, u32[]{:S(2)}, u32[]{:S(2)}) collective-permute-start(f32[8,1,32,32]{2,3,0,1:T(8,128)S(1)} %convolution_bitcast_fusion.4), channel_id=1, source_target_pairs={{0,1},{1,0},{2,3},{3,2},{4,5},{5,4},{6,7},{7,6},{8,9},{9,8},{10,11... | collective-permute-start | bytes 98312 | tf_op jit(solution)/shard_map/ppermute | solution.py:19
  114.0 26.1 %all-to-all-start.7 = ((f32[16,1,1024]{2,1,0:T(1,128)}), f32[16,1,1024]{2,1,0:T(1,128)S(1)}, u32[]{:S(2)}, u32[]{:S(2)}) async-start(f32[16,1,1024]{2,1,0:T(1,128)} %reshape.284), calls=%async_computation.7 | async-start | bytes 131072 | tf_op jit(solution)/shard_map/all_to_all | solution.py:82
  143.2 15.1 %all-to-all-start.1 = ((f32[16,1,1024]{2,1,0:T(1,128)}), f32[16,1,1024]{2,1,0:T(1,128)}, u32[]{:S(2)}, u32[]{:S(2)}) async-start(f32[16,1,1024]{2,1,0:T(1,128)} %reshape.282), calls=%async_computation.1 | async-start | bytes 131072 | tf_op jit(solution)/shard_map/all_to_all | solution.py:90
  166.0 5.0 %copy-start = (f32[32,8,1,64]{3,1,0,2:T(8,128)S(1)}, f32[32,8,1,64]{3,1,0,2:T(8,128)}, u32[]{:S(2)}) copy-start(f32[32,8,1,64]{3,1,0,2:T(8,128)} %get-tuple-element.7) | copy-start | bytes 196612
  166.0 52.9 %all-to-all-start.2 = ((f32[2,4,8,64,256]{4,3,2,0,1:T(8,128)}), f32[2,4,8,64,256]{4,3,2,0,1:T(8,128)}, u32[]{:S(2)}, u32[]{:S(2)}) async-start(f32[2,4,8,64,256]{4,3,2,0,1:T(8,128)} %copy.133), calls=%async_computation.2 | async-start | bytes 8388608 | tf_op jit(solution)/shard_map/all_to_all | solution.py:35
  171.4 6.7 %collective-permute-start.3 = (f32[8,1,32,33]{2,3,0,1:T(8,128)S(1)}, f32[8,1,32,33]{2,3,0,1:T(8,128)S(1)}, u32[]{:S(2)}, u32[]{:S(2)}) collective-permute-start(f32[8,1,32,33]{2,3,0,1:T(8,128)S(1)} %pad_maximum_fusion.3), channel_id=1, source_target_pairs={{0,1},{1,0},{2,3},{3,2},{4,5},{5,4},{6,7},{7,6},{8,9},{9,8},{10,11... | collective-permute-start | bytes 101384 | tf_op jit(solution)/shard_map/ppermute | solution.py:19
  218.9 20.2 %all-to-all-start.8 = ((f32[16,1,3072]{2,1,0:T(1,128)}), f32[16,1,3072]{2,1,0:T(1,128)S(1)}, u32[]{:S(2)}, u32[]{:S(2)}) async-start(f32[16,1,3072]{2,1,0:T(1,128)} %reshape.286), calls=%async_computation.8 | async-start | bytes 393216 | tf_op jit(solution)/shard_map/all_to_all | solution.py:90
  227.0 15.8 %copy-start.1 = (f32[256,64]{0,1:T(8,128)S(1)}, f32[256,64]{0,1:T(8,128)}, u32[]{:S(2)}) copy-start(f32[256,64]{0,1:T(8,128)} %param.9) | copy-start | bytes 196612
  239.0 36.9 %all-to-all-start.3 = ((f32[2,8,64,256]{3,2,0,1:T(8,128)}), f32[2,8,64,256]{3,2,0,1:T(8,128)S(1)}, u32[]{:S(2)}, u32[]{:S(2)}) async-start(f32[2,8,64,256]{3,2,0,1:T(8,128)} %copy.134), calls=%async_computation.3 | async-start | bytes 2097152 | tf_op jit(solution)/shard_map/all_to_all | solution.py:37
  243.2 31.7 %copy-start.3 = (f32[256,64]{0,1:T(8,128)S(1)}, f32[256,64]{0,1:T(8,128)}, u32[]{:S(2)}) copy-start(f32[256,64]{0,1:T(8,128)} %param.7) | copy-start | bytes 196612
  243.2 30.0 %collective-permute-start.2 = (f32[1,1,256,257]{2,3,1,0:T(8,128)S(1)}, f32[1,1,256,257]{2,3,1,0:T(8,128)S(1)}, u32[]{:S(2)}, u32[]{:S(2)}) collective-permute-start(f32[1,1,256,257]{2,3,1,0:T(8,128)S(1)} %pad_maximum_fusion.2), channel_id=1, source_target_pairs={{0,1},{1,0},{2,3},{3,2},{4,5},{5,4},{6,7},{7,6},{8,9},{9,8},{10,11... | collective-permute-start | bytes 789512 | tf_op jit(solution)/shard_map/ppermute | solution.py:19
  274.7 6.4 %copy-start.5 = (f32[256,64]{0,1:T(8,128)S(1)}, f32[256,64]{0,1:T(8,128)}, u32[]{:S(2)}) copy-start(f32[256,64]{0,1:T(8,128)} %param.8) | copy-start | bytes 196612
  276.6 15.5 %all-to-all-start.4 = ((f32[2,64,256]{2,1,0:T(8,128)}), f32[2,64,256]{2,1,0:T(8,128)S(1)}, u32[]{:S(2)}, u32[]{:S(2)}) async-start(f32[2,64,256]{2,1,0:T(8,128)} %reduce_sum.66), calls=%async_computation.4 | async-start | bytes 262144 | tf_op jit(solution)/shard_map/all_to_all | solution.py:37

commit v8 on v6

--- a/solution.py
+++ b/solution.py
@@ -33,15 +33,19 @@
     block = rows // (sizes[0] * sizes[1] * sizes[2])
     parts = partial_value.reshape(*sizes, block, cols)
     parts = lax.all_to_all(parts, "x", 1, 1, tiled=True).sum(1)
-    for dim in (1, 0):
-        parts = lax.all_to_all(parts, HEAD_AXES[2 * dim], dim, dim, tiled=True).sum(dim)
-    return parts, companion
+    parts = lax.all_to_all(parts, "y", 1, 1, tiled=True).sum(1)
+    own = lax.axis_index("zh")
+    kept = lax.dynamic_index_in_dim(parts, own, 0, keepdims=False)
+    sent = lax.dynamic_index_in_dim(parts, 1 - own, 0, keepdims=False)
+    return kept + swapped(sent, "zh", 0), companion
 
 
 def gather_head(piece):
     rows, cols = piece.shape
-    stacked = piece
-    for axis in ("zh", "y", "x"):
+    other = swapped(piece, "zh", 0)
+    first = lax.axis_index("zh") == 0
+    stacked = jnp.stack([jnp.where(first, piece, other), jnp.where(first, other, piece)])
+    for axis in ("y", "x"):
         count = lax.axis_size(axis)
         copies = jnp.broadcast_to(stacked[None], (count,) + stacked.shape)
         stacked = lax.all_to_all(copies, axis, 0, 0, tiled=True)

time: 289 us -> 279 us (0.965)
  blocking collectives: 31.4 us -> 0 us
  starting transfers between devices: 60.4 us -> 91.8 us
  waiting for transfers between devices: 147 us -> 138 us
    ppermute x4 -> x6, starting transfers between devices: 10.2 us -> 41.7 us  [swapped(): lax.ppermute(x, axis, [(i, i ^ 1 << distance) for i in range(lax.axis_siz...]
    all_to_all x1 -> x0, blocking collectives: 31.4 us -> none  [gather_head(): stacked = lax.all_to_all(copies, axis, 0, 0, tiled=True)]
    all_to_all x2 -> x1, waiting for transfers between devices: 10.5 us -> 0.01 us  [scatter_head(): parts = lax.all_to_all(parts, 'y', 1, 1, tiled=True).sum(1)]
    ppermute x4 -> x6, waiting for transfers between devices: 33.5 us -> 37 us  [swapped(): lax.ppermute(x, axis, [(i, i ^ 1 << distance) for i in range(lax.axis_siz...]
    all_to_all x2 -> x1, starting transfers between devices: 6.93 us -> 3.56 us  [scatter_head(): parts = lax.all_to_all(parts, 'y', 1, 1, tiled=True).sum(1)]
    all_to_all x2, starting transfers between devices: 16.5 us -> 19.9 us  [to_strided(): lax.all_to_all(layout, 'seq', split_axis=1, concat_axis=0, tiled=True)]
  transfers between devices with their start and end apart: 13 -> 14, of which waited for: 11 -> 12; matrix products, arithmetic and copies ran while one was open for 10% -> 10% of each run, Pallas kernels for 0% -> 0%
where the time goes in v8:
time: 279 us; the launch traced here: 276 us
  waiting for transfers between devices  138 us (49%)
  starting transfers between devices  91.8 us (33%)
  local copies, waits for them, and re-layouts  19 us (7%)
  other arithmetic  13.3 us (5%)
  matrix products  12.8 us (5%)
    ppermute x6, starting transfers between devices, swapped(): lax.ppermute(x, axis, [(i, i ^ 1 << distance) for i in range(lax.axis_siz...  41.7 us
    all_to_all x1, waiting for transfers between devices, scatter_head(): parts = lax.all_to_all(parts, 'x', 1, 1, tiled=True).sum(1)  39 us
    ppermute x6, waiting for transfers between devices, swapped(): lax.ppermute(x, axis, [(i, i ^ 1 << distance) for i in range(lax.axis_siz...  37 us
    all_to_all x2, waiting for transfers between devices, gather_head(): stacked = lax.all_to_all(copies, axis, 0, 0, tiled=True)  22.8 us
    all_to_all x2, waiting for transfers between devices, to_strided(): lax.all_to_all(layout, 'seq', split_axis=1, concat_axis=0, tiled=True)  20.5 us
    all_to_all x2, starting transfers between devices, to_strided(): lax.all_to_all(layout, 'seq', split_axis=1, concat_axis=0, tiled=True)  19.9 us
    all_to_all x2, waiting for transfers between devices, to_contiguous(): lax.all_to_all(layout, 'seq', split_axis=0, concat_axis=2, tiled=True)  18.6 us
    all_to_all x2, starting transfers between devices, gather_head(): stacked = lax.all_to_all(copies, axis, 0, 0, tiled=True)  11.4 us
  transfers between devices with their start and end apart: 14, of which 12 were waited for; matrix products, arithmetic and copies ran while one was open for 10% of the time, Pallas kernels for 0%

profile of v8, /device:TPU:1, one launch (start us, length us, event | category | flops | bytes accessed | tf_op | source)
XLA Modules:
  0.0 276.0 jit_solution(11886226922049619565)
XLA Ops:
  0.7 20.0 %collective-permute-start.3 = (bf16[256,64]{0,1:T(8,128)(2,1)}, bf16[256,64]{0,1:T(8,128)(2,1)S(1)}, u32[]{:S(2)}, u32[]{:S(2)}) collective-permute-start(bf16[256,64]{0,1:T(8,128)(2,1)} %param.13), channel_id=1, source_target_pairs={{0,32},{32,0},{1,33},{33,1},{2,34},{34,2},{3,35},{35,3},{4,36},{36... | collective-permute-start | bytes 98312 | tf_op jit(solution)/shard_map/ppermute | solution.py:19
  20.7 1.6 collective-permute-done.3
  24.0 7.0 %all-to-all-start.4 = ((bf16[8,2,256,64]{2,3,1,0:T(8,128)(2,1)}), bf16[8,2,256,64]{2,3,1,0:T(8,128)(2,1)S(1)}, u32[]{:S(2)}, u32[]{:S(2)}) async-start(bf16[8,2,256,64]{2,3,1,0:T(8,128)(2,1)} %broadcast_in_dim.56), calls=%async_computation.4 | async-start | bytes 1048576 | tf_op jit(solution)/shard_map/all_to_all | solution.py:51
  30.9 0.9 copy.67
  32.2 0.9 reshape.276
  33.1 10.9 %all-to-all-done.4 = bf16[8,2,256,64]{2,3,1,0:T(8,128)(2,1)S(1)} async-done(((bf16[8,2,256,64]{2,3,1,0:T(8,128)(2,1)}), bf16[8,2,256,64]{2,3,1,0:T(8,128)(2,1)S(1)}, u32[]{:S(2)}, u32[]{:S(2)}) %all-to-all-start.4) | async-done | bytes 524320 | tf_op jit(solution)/shard_map/all_to_all | solution.py:51
  44.1 13.9 %all-to-all-start = ((f32[16,1,3072]{2,1,0:T(1,128)}), f32[16,1,3072]{2,1,0:T(1,128)S(1)}, u32[]{:S(2)}, u32[]{:S(2)}) async-start(f32[16,1,3072]{2,1,0:T(1,128)} %reshape.276), calls=%async_computation | async-start | bytes 393216 | tf_op jit(solution)/shard_map/all_to_all | solution.py:85
  58.4 2.2 collective-permute-start
  60.6 1.4 constant_dynamic-update-slice_fusion.1
  62.0 10.6 %all-to-all-done = f32[16,1,3072]{2,1,0:T(1,128)S(1)} async-done(((f32[16,1,3072]{2,1,0:T(1,128)}), f32[16,1,3072]{2,1,0:T(1,128)S(1)}, u32[]{:S(2)}, u32[]{:S(2)}) %all-to-all-start) | async-done | bytes 196640 | tf_op jit(solution)/shard_map/all_to_all | solution.py:85
  72.6 1.6 broadcast_in_dim.57
  74.2 4.4 %all-to-all-start.5 = ((bf16[4,8,2,256,64]{3,4,1,2,0:T(8,128)(2,1)}), bf16[4,8,2,256,64]{3,4,1,2,0:T(8,128)(2,1)}, u32[]{:S(2)}, u32[]{:S(2)}) async-start(bf16[4,8,2,256,64]{3,4,1,2,0:T(8,128)(2,1)} %broadcast_in_dim.57), calls=%async_computation.5 | async-start | bytes 4194304 | tf_op jit(solution)/shard_map/all_to_all | solution.py:51
  78.6 1.3 constant_dynamic-update-slice_fusion
  81.9 1.8 reduce.7
  83.7 1.0 reshape.277
  85.8 2.2 collective-permute-start.1
  88.0 1.3 fusion.12
  89.4 3.3 %collective-permute-done.1 = f32[8,1,32,32]{2,3,0,1:T(8,128)S(1)} collective-permute-done((f32[8,1,32,32]{2,3,0,1:T(8,128)S(1)}, f32[8,1,32,32]{2,3,0,1:T(8,128)S(1)}, u32[]{:S(2)}, u32[]{:S(2)}) %collective-permute-start.1) | collective-permute-done | bytes 32800 | tf_op jit(solution)/shard_map/ppermute | solution.py:19
  92.7 11.9 %all-to-all-done.5 = bf16[4,8,2,256,64]{3,4,1,2,0:T(8,128)(2,1)} async-done(((bf16[4,8,2,256,64]{3,4,1,2,0:T(8,128)(2,1)}), bf16[4,8,2,256,64]{3,4,1,2,0:T(8,128)(2,1)}, u32[]{:S(2)}, u32[]{:S(2)}) %all-to-all-start.5) | async-done | bytes 2097184 | tf_op jit(solution)/shard_map/all_to_all | solution.py:51
  104.6 1.7 copy.83
  106.3 1.3 fusion.53
  108.6 6.0 %all-to-all-start.6 = ((f32[16,1,1024]{2,1,0:T(1,128)}), f32[16,1,1024]{2,1,0:T(1,128)S(1)}, u32[]{:S(2)}, u32[]{:S(2)}) async-start(f32[16,1,1024]{2,1,0:T(1,128)} %reshape.280), calls=%async_computation.6 | async-start | bytes 131072 | tf_op jit(solution)/shard_map/all_to_all | solution.py:85
  114.7 10.0 %all-to-all-done.6 = f32[16,1,1024]{2,1,0:T(1,128)S(1)} async-done(((f32[16,1,1024]{2,1,0:T(1,128)}), f32[16,1,1024]{2,1,0:T(1,128)S(1)}, u32[]{:S(2)}, u32[]{:S(2)}) %all-to-all-start.6) | async-done | bytes 65568 | tf_op jit(solution)/shard_map/all_to_all | solution.py:85
  125.6 1.4 fusion.19
  127.8 4.9 %all-to-all-start.1 = ((f32[16,1,1024]{2,1,0:T(1,128)}), f32[16,1,1024]{2,1,0:T(1,128)}, u32[]{:S(2)}, u32[]{:S(2)}) async-start(f32[16,1,1024]{2,1,0:T(1,128)} %reshape.278), calls=%async_computation.1 | async-start | bytes 131072 | tf_op jit(solution)/shard_map/all_to_all | solution.py:93
  132.7 1.4 fusion.11
  134.1 1.1 fusion.43
  135.2 7.7 %all-to-all-done.1 = f32[16,1,1024]{2,1,0:T(1,128)} async-done(((f32[16,1,1024]{2,1,0:T(1,128)}), f32[16,1,1024]{2,1,0:T(1,128)}, u32[]{:S(2)}, u32[]{:S(2)}) %all-to-all-start.1) | async-done | bytes 65568 | tf_op jit(solution)/shard_map/all_to_all | solution.py:93
  142.9 1.6 reduce.8
  144.8 3.5 %fusion.15 = f32[4096,256]{1,0:T(8,128)S(1)} fusion(f32[128,4096]{1,0:T(8,128)S(1)} %constant_dynamic-update-slice_fusion, f32[256,64]{0,1:T(8,128)S(1)} %copy.79, f32[256,64]{0,1:T(8,128)S(1)} %get-tuple-element.13), kind=kOutput, calls=%fused_computation.39 | convolution fusion | flops 1610645504 | bytes 6422528 | tf_op jit(solution)/shard_map/dot_general | solution.py:134
  148.3 2.3 copy.80
  150.5 5.0 %all-to-all-start.2 = ((f32[2,4,8,64,256]{4,3,2,0,1:T(8,128)}), f32[2,4,8,64,256]{4,3,2,0,1:T(8,128)}, u32[]{:S(2)}, u32[]{:S(2)}) async-start(f32[2,4,8,64,256]{4,3,2,0,1:T(8,128)} %copy.80), calls=%async_computation.2 | async-start | bytes 8388608 | tf_op jit(solution)/shard_map/all_to_all | solution.py:35
  155.9 2.4 collective-permute-start.5
  158.6 4.0 %collective-permute-done.5 = f32[8,1,32,33]{2,3,0,1:T(8,128)S(1)} collective-permute-done((f32[8,1,32,33]{2,3,0,1:T(8,128)S(1)}, f32[8,1,32,33]{2,3,0,1:T(8,128)S(1)}, u32[]{:S(2)}, u32[]{:S(2)}) %collective-permute-start.5) | collective-permute-done | bytes 33824 | tf_op jit(solution)/shard_map/ppermute | solution.py:19
  164.4 39.0 %all-to-all-done.2 = f32[2,4,8,64,256]{4,3,2,0,1:T(8,128)} async-done(((f32[2,4,8,64,256]{4,3,2,0,1:T(8,128)}), f32[2,4,8,64,256]{4,3,2,0,1:T(8,128)}, u32[]{:S(2)}, u32[]{:S(2)}) %all-to-all-start.2) | async-done | bytes 4194336 | tf_op jit(solution)/shard_map/all_to_all | solution.py:35
  203.4 5.5 %all-to-all-start.7 = ((f32[16,1,3072]{2,1,0:T(1,128)}), f32[16,1,3072]{2,1,0:T(1,128)S(1)}, u32[]{:S(2)}, u32[]{:S(2)}) async-start(f32[16,1,3072]{2,1,0:T(1,128)} %reshape.282), calls=%async_computation.7 | async-start | bytes 393216 | tf_op jit(solution)/shard_map/all_to_all | solution.py:93
  208.9 2.6 reduce_sum.56
  211.5 1.1 copy.81
  212.6 11.0 %all-to-all-done.7 = f32[16,1,3072]{2,1,0:T(1,128)S(1)} async-done(((f32[16,1,3072]{2,1,0:T(1,128)}), f32[16,1,3072]{2,1,0:T(1,128)S(1)}, u32[]{:S(2)}, u32[]{:S(2)}) %all-to-all-start.7) | async-done | bytes 196640 | tf_op jit(solution)/shard_map/all_to_all | solution.py:93
  223.6 3.6 %all-to-all-start.3 = ((f32[2,8,64,256]{3,2,0,1:T(8,128)}), f32[2,8,64,256]{3,2,0,1:T(8,128)S(1)}, u32[]{:S(2)}, u32[]{:S(2)}) async-start(f32[2,8,64,256]{3,2,0,1:T(8,128)} %copy.81), calls=%async_computation.3 | async-start | bytes 2097152 | tf_op jit(solution)/shard_map/all_to_all | solution.py:36
  227.6 3.3 %collective-permute-start.4 = (f32[1,1,256,257]{2,3,1,0:T(8,128)S(1)}, f32[1,1,256,257]{2,3,1,0:T(8,128)S(1)}, u32[]{:S(2)}, u32[]{:S(2)}) collective-permute-start(f32[1,1,256,257]{2,3,1,0:T(8,128)S(1)} %pad_maximum_fusion.2), channel_id=1, source_target_pairs={{0,1},{1,0},{2,3},{3,2},{4,5},{5,4},{6,7},{7,6},{8,9},{9,8},{10,11... | collective-permute-start | bytes 789512 | tf_op jit(solution)/shard_map/ppermute | solution.py:19
  230.9 26.4 %collective-permute-done.4 = f32[1,1,256,257]{2,3,1,0:T(8,128)S(1)} collective-permute-done((f32[1,1,256,257]{2,3,1,0:T(8,128)S(1)}, f32[1,1,256,257]{2,3,1,0:T(8,128)S(1)}, u32[]{:S(2)}, u32[]{:S(2)}) %collective-permute-start.4) | collective-permute-done | bytes 263200 | tf_op jit(solution)/shard_map/ppermute | solution.py:19
  257.3 1.1 reduce.9
  259.1 1.0 fusion.3
  260.1 0.9 fusion.4
  261.1 11.6 %collective-permute-start.2 = (f32[64,256]{1,0:T(8,128)S(1)}, f32[64,256]{1,0:T(8,128)S(1)}, u32[]{:S(2)}, u32[]{:S(2)}) collective-permute-start(f32[64,256]{1,0:T(8,128)S(1)} %dynamic-slice_bitcast_fusion), channel_id=1, source_target_pairs={{0,32},{32,0},{1,33},{33,1},{2,34},{34,2},{3,35},{35,3},{4,36},{36... | collective-permute-start | bytes 196616 | tf_op jit(solution)/shard_map/ppermute | solution.py:19
  272.7 1.0 fusion.2
  273.7 1.7 collective-permute-done.2
  (81 shorter events, 12.7 us)
Async XLA Ops:
  0.6 31.2 %copy-start.7 = (f32[256,64]{0,1:T(8,128)S(1)}, f32[256,64]{0,1:T(8,128)}, u32[]{:S(2)}) copy-start(f32[256,64]{0,1:T(8,128)} %param.8) | copy-start | bytes 196612
  0.6 31.3 %copy-start.3 = (f32[256,64]{0,1:T(8,128)S(1)}, f32[256,64]{0,1:T(8,128)}, u32[]{:S(2)}) copy-start(f32[256,64]{0,1:T(8,128)} %param.9) | copy-start | bytes 196612
  0.7 21.7 %collective-permute-start.3 = (bf16[256,64]{0,1:T(8,128)(2,1)}, bf16[256,64]{0,1:T(8,128)(2,1)S(1)}, u32[]{:S(2)}, u32[]{:S(2)}) collective-permute-start(bf16[256,64]{0,1:T(8,128)(2,1)} %param.13), channel_id=1, source_target_pairs={{0,32},{32,0},{1,33},{33,1},{2,34},{34,2},{3,35},{35,3},{4,36},{36... | collective-permute-start | bytes 98312 | tf_op jit(solution)/shard_map/ppermute | solution.py:19
  24.0 34.0 %copy-start.5 = (f32[256,64]{0,1:T(8,128)S(1)}, f32[256,64]{0,1:T(8,128)}, u32[]{:S(2)}) copy-start(f32[256,64]{0,1:T(8,128)} %param.7) | copy-start | bytes 196612
  24.0 20.1 %all-to-all-start.4 = ((bf16[8,2,256,64]{2,3,1,0:T(8,128)(2,1)}), bf16[8,2,256,64]{2,3,1,0:T(8,128)(2,1)S(1)}, u32[]{:S(2)}, u32[]{:S(2)}) async-start(bf16[8,2,256,64]{2,3,1,0:T(8,128)(2,1)} %broadcast_in_dim.56), calls=%async_computation.4 | async-start | bytes 1048576 | tf_op jit(solution)/shard_map/all_to_all | solution.py:51
  44.1 14.3 %copy-start = (bf16[8,2,256,64]{2,3,1,0:T(8,128)(2,1)}, bf16[8,2,256,64]{2,3,1,0:T(8,128)(2,1)S(1)}, u32[]{:S(2)}) copy-start(bf16[8,2,256,64]{2,3,1,0:T(8,128)(2,1)S(1)} %all-to-all-done.4) | copy-start | bytes 1572868
  44.1 28.5 %all-to-all-start = ((f32[16,1,3072]{2,1,0:T(1,128)}), f32[16,1,3072]{2,1,0:T(1,128)S(1)}, u32[]{:S(2)}, u32[]{:S(2)}) async-start(f32[16,1,3072]{2,1,0:T(1,128)} %reshape.276), calls=%async_computation | async-start | bytes 393216 | tf_op jit(solution)/shard_map/all_to_all | solution.py:85
  58.4 22.2 %collective-permute-start = (f32[1,1,256,256]{2,3,1,0:T(8,128)S(1)}, f32[1,1,256,256]{2,3,1,0:T(8,128)S(1)}, u32[]{:S(2)}, u32[]{:S(2)}) collective-permute-start(f32[1,1,256,256]{2,3,1,0:T(8,128)S(1)} %convolution_bitcast_fusion.1), channel_id=1, source_target_pairs={{0,1},{1,0},{2,3},{3,2},{4,5},{5,4},{6,7},{7,6},{8,9},{9,8},{10,11... | collective-permute-start | bytes 786440 | tf_op jit(solution)/shard_map/ppermute | solution.py:19
  60.6 1.4 copy-start.1
  74.2 30.4 %all-to-all-start.5 = ((bf16[4,8,2,256,64]{3,4,1,2,0:T(8,128)(2,1)}), bf16[4,8,2,256,64]{3,4,1,2,0:T(8,128)(2,1)}, u32[]{:S(2)}, u32[]{:S(2)}) async-start(bf16[4,8,2,256,64]{3,4,1,2,0:T(8,128)(2,1)} %broadcast_in_dim.57), calls=%async_computation.5 | async-start | bytes 4194304 | tf_op jit(solution)/shard_map/all_to_all | solution.py:51
  78.6 1.3 copy-start.9
  85.8 6.8 %collective-permute-start.1 = (f32[8,1,32,32]{2,3,0,1:T(8,128)S(1)}, f32[8,1,32,32]{2,3,0,1:T(8,128)S(1)}, u32[]{:S(2)}, u32[]{:S(2)}) collective-permute-start(f32[8,1,32,32]{2,3,0,1:T(8,128)S(1)} %convolution_bitcast_fusion.4), channel_id=1, source_target_pairs={{0,1},{1,0},{2,3},{3,2},{4,5},{5,4},{6,7},{7,6},{8,9},{9,8},{10,11... | collective-permute-start | bytes 98312 | tf_op jit(solution)/shard_map/ppermute | solution.py:19
  108.6 16.1 %all-to-all-start.6 = ((f32[16,1,1024]{2,1,0:T(1,128)}), f32[16,1,1024]{2,1,0:T(1,128)S(1)}, u32[]{:S(2)}, u32[]{:S(2)}) async-start(f32[16,1,1024]{2,1,0:T(1,128)} %reshape.280), calls=%async_computation.6 | async-start | bytes 131072 | tf_op jit(solution)/shard_map/all_to_all | solution.py:85
  127.8 15.1 %all-to-all-start.1 = ((f32[16,1,1024]{2,1,0:T(1,128)}), f32[16,1,1024]{2,1,0:T(1,128)}, u32[]{:S(2)}, u32[]{:S(2)}) async-start(f32[16,1,1024]{2,1,0:T(1,128)} %reshape.278), calls=%async_computation.1 | async-start | bytes 131072 | tf_op jit(solution)/shard_map/all_to_all | solution.py:93
  150.5 5.0 %copy-start.2 = (f32[32,8,1,64]{3,1,0,2:T(8,128)S(1)}, f32[32,8,1,64]{3,1,0,2:T(8,128)}, u32[]{:S(2)}) copy-start(f32[32,8,1,64]{3,1,0,2:T(8,128)} %get-tuple-element.7) | copy-start | bytes 196612
  150.5 52.9 %all-to-all-start.2 = ((f32[2,4,8,64,256]{4,3,2,0,1:T(8,128)}), f32[2,4,8,64,256]{4,3,2,0,1:T(8,128)}, u32[]{:S(2)}, u32[]{:S(2)}) async-start(f32[2,4,8,64,256]{4,3,2,0,1:T(8,128)} %copy.80), calls=%async_computation.2 | async-start | bytes 8388608 | tf_op jit(solution)/shard_map/all_to_all | solution.py:35
  155.9 6.7 %collective-permute-start.5 = (f32[8,1,32,33]{2,3,0,1:T(8,128)S(1)}, f32[8,1,32,33]{2,3,0,1:T(8,128)S(1)}, u32[]{:S(2)}, u32[]{:S(2)}) collective-permute-start(f32[8,1,32,33]{2,3,0,1:T(8,128)S(1)} %pad_maximum_fusion.3), channel_id=1, source_target_pairs={{0,1},{1,0},{2,3},{3,2},{4,5},{5,4},{6,7},{7,6},{8,9},{9,8},{10,11... | collective-permute-start | bytes 101384 | tf_op jit(solution)/shard_map/ppermute | solution.py:19
  203.4 20.2 %all-to-all-start.7 = ((f32[16,1,3072]{2,1,0:T(1,128)}), f32[16,1,3072]{2,1,0:T(1,128)S(1)}, u32[]{:S(2)}, u32[]{:S(2)}) async-start(f32[16,1,3072]{2,1,0:T(1,128)} %reshape.282), calls=%async_computation.7 | async-start | bytes 393216 | tf_op jit(solution)/shard_map/all_to_all | solution.py:93
  211.5 15.6 %copy-start.4 = (f32[256,64]{0,1:T(8,128)S(1)}, f32[256,64]{0,1:T(8,128)}, u32[]{:S(2)}) copy-start(f32[256,64]{0,1:T(8,128)} %param.9) | copy-start | bytes 196612
  223.6 37.4 %all-to-all-start.3 = ((f32[2,8,64,256]{3,2,0,1:T(8,128)}), f32[2,8,64,256]{3,2,0,1:T(8,128)S(1)}, u32[]{:S(2)}, u32[]{:S(2)}) async-start(f32[2,8,64,256]{3,2,0,1:T(8,128)} %copy.81), calls=%async_computation.3 | async-start | bytes 2097152 | tf_op jit(solution)/shard_map/all_to_all | solution.py:36
  227.6 29.6 %collective-permute-start.4 = (f32[1,1,256,257]{2,3,1,0:T(8,128)S(1)}, f32[1,1,256,257]{2,3,1,0:T(8,128)S(1)}, u32[]{:S(2)}, u32[]{:S(2)}) collective-permute-start(f32[1,1,256,257]{2,3,1,0:T(8,128)S(1)} %pad_maximum_fusion.2), channel_id=1, source_target_pairs={{0,1},{1,0},{2,3},{3,2},{4,5},{5,4},{6,7},{7,6},{8,9},{9,8},{10,11... | collective-permute-start | bytes 789512 | tf_op jit(solution)/shard_map/ppermute | solution.py:19
  257.3 1.8 copy-start.6
  258.5 1.6 copy-start.8
  261.1 14.3 %collective-permute-start.2 = (f32[64,256]{1,0:T(8,128)S(1)}, f32[64,256]{1,0:T(8,128)S(1)}, u32[]{:S(2)}, u32[]{:S(2)}) collective-permute-start(f32[64,256]{1,0:T(8,128)S(1)} %dynamic-slice_bitcast_fusion), channel_id=1, source_target_pairs={{0,32},{32,0},{1,33},{33,1},{2,34},{34,2},{3,35},{35,3},{4,36},{36... | collective-permute-start | bytes 196616 | tf_op jit(solution)/shard_map/ppermute | solution.py:19

commit v9 on v8

--- a/solution.py
+++ b/solution.py
@@ -32,12 +32,15 @@
     rows, cols = partial_value.shape
     block = rows // (sizes[0] * sizes[1] * sizes[2])
     parts = partial_value.reshape(*sizes, block, cols)
-    parts = lax.all_to_all(parts, "x", 1, 1, tiled=True).sum(1)
+    return lax.all_to_all(parts, "x", 1, 1, tiled=True).sum(1), companion
+
+
+def finish_scatter(parts):
     parts = lax.all_to_all(parts, "y", 1, 1, tiled=True).sum(1)
     own = lax.axis_index("zh")
     kept = lax.dynamic_index_in_dim(parts, own, 0, keepdims=False)
     sent = lax.dynamic_index_in_dim(parts, 1 - own, 0, keepdims=False)
-    return kept + swapped(sent, "zh", 0), companion
+    return kept + swapped(sent, "zh", 0)
 
 
 def gather_head(piece):
@@ -140,7 +143,7 @@
         ),
         gather_head(grad_out),
     )
-    mixed = mixed_cols.T
+    mixed_stage = mixed_cols
     w_cols = wo_both
     grad_both = lax.dot_general(
         grad_rows.astype(jnp.float32),
@@ -154,6 +157,8 @@
     dq_local, dk_local, dv_local = attend_backward(
         local_q, local_k, local_v, probs_local, attn_local, grad_local.reshape(local_layout)
     )
+    mixed_stage, dq_local = lax.optimization_barrier((mixed_stage, dq_local))
+    mixed = finish_scatter(mixed_stage).T
     dq_strided, dk_strided, dv_strided = attend_backward(
         strided_q, strided_k, strided_v, probs_strided, attn_strided, to_runs(grad_strided)
     )

time: 279 us -> 272 us (0.975)
  waiting for transfers between devices: 138 us -> 134 us
    all_to_all x2, waiting for transfers between devices: 39 us -> 63.9 us  [the longest x1 38.5 us: scatter_head(): return (lax.all_to_all(parts, 'x', 1, 1, tiled=True).sum(1), companion)]
    ppermute x6, waiting for transfers between devices: 37 us -> 18.3 us  [swapped(): lax.ppermute(x, axis, [(i, i ^ 1 << distance) for i in range(lax.axis_siz...]
    all_to_all x2, waiting for transfers between devices: 18.6 us -> 8.27 us  [to_contiguous(): lax.all_to_all(layout, 'seq', split_axis=0, concat_axis=2, tiled=True)]
  transfers between devices with their start and end apart: 14 -> 14, of which waited for: 12 -> 13; matrix products, arithmetic and copies ran while one was open for 10% -> 10% of each run, Pallas kernels for 0% -> 0%
where the time goes in v9:
time: 272 us; the launch traced here: 271 us
  waiting for transfers between devices  134 us (49%)
  starting transfers between devices  90.8 us (33%)
  local copies, waits for them, and re-layouts  19 us (7%)
  other arithmetic  14 us (5%)
  matrix products  12.1 us (4%)
    ppermute x6, starting transfers between devices, swapped(): lax.ppermute(x, axis, [(i, i ^ 1 << distance) for i in range(lax.axis_siz...  40.6 us
    all_to_all x1, waiting for transfers between devices, scatter_head(): return (lax.all_to_all(parts, 'x', 1, 1, tiled=True).sum(1), companion)  38.5 us
    all_to_all x1, waiting for transfers between devices, finish_scatter(): parts = lax.all_to_all(parts, 'y', 1, 1, tiled=True).sum(1)  25.4 us
    all_to_all x2, waiting for transfers between devices, gather_head(): stacked = lax.all_to_all(copies, axis, 0, 0, tiled=True)  22.8 us
    all_to_all x2, waiting for transfers between devices, to_strided(): lax.all_to_all(layout, 'seq', split_axis=1, concat_axis=0, tiled=True)  20.5 us
    all_to_all x2, starting transfers between devices, to_strided(): lax.all_to_all(layout, 'seq', split_axis=1, concat_axis=0, tiled=True)  19.9 us
    ppermute x6, waiting for transfers between devices, swapped(): lax.ppermute(x, axis, [(i, i ^ 1 << distance) for i in range(lax.axis_siz...  18.3 us
    all_to_all x2, starting transfers between devices, gather_head(): stacked = lax.all_to_all(copies, axis, 0, 0, tiled=True)  11.4 us
  transfers between devices with their start and end apart: 14, of which 13 were waited for; matrix products, arithmetic and copies ran while one was open for 10% of the time, Pallas kernels for 0%

profile of v9, /device:TPU:1, one launch (start us, length us, event | category | flops | bytes accessed | tf_op | source)
XLA Modules:
  0.0 271.0 jit_solution(8140618306217463913)
XLA Ops:
  0.7 20.0 %collective-permute-start.2 = (bf16[256,64]{0,1:T(8,128)(2,1)}, bf16[256,64]{0,1:T(8,128)(2,1)S(1)}, u32[]{:S(2)}, u32[]{:S(2)}) collective-permute-start(bf16[256,64]{0,1:T(8,128)(2,1)} %param.13), channel_id=1, source_target_pairs={{0,32},{32,0},{1,33},{33,1},{2,34},{34,2},{3,35},{35,3},{4,36},{36... | collective-permute-start | bytes 98312 | tf_op jit(solution)/shard_map/ppermute | solution.py:19
  20.7 1.6 collective-permute-done.2
  24.0 7.0 %all-to-all-start.3 = ((bf16[8,2,256,64]{2,3,1,0:T(8,128)(2,1)}), bf16[8,2,256,64]{2,3,1,0:T(8,128)(2,1)S(1)}, u32[]{:S(2)}, u32[]{:S(2)}) async-start(bf16[8,2,256,64]{2,3,1,0:T(8,128)(2,1)} %broadcast_in_dim.56), calls=%async_computation.3 | async-start | bytes 1048576 | tf_op jit(solution)/shard_map/all_to_all | solution.py:54
  30.9 0.9 copy.67
  32.2 0.9 reshape.276
  33.1 10.9 %all-to-all-done.3 = bf16[8,2,256,64]{2,3,1,0:T(8,128)(2,1)S(1)} async-done(((bf16[8,2,256,64]{2,3,1,0:T(8,128)(2,1)}), bf16[8,2,256,64]{2,3,1,0:T(8,128)(2,1)S(1)}, u32[]{:S(2)}, u32[]{:S(2)}) %all-to-all-start.3) | async-done | bytes 524320 | tf_op jit(solution)/shard_map/all_to_all | solution.py:54
  44.1 13.9 %all-to-all-start = ((f32[16,1,3072]{2,1,0:T(1,128)}), f32[16,1,3072]{2,1,0:T(1,128)S(1)}, u32[]{:S(2)}, u32[]{:S(2)}) async-start(f32[16,1,3072]{2,1,0:T(1,128)} %reshape.276), calls=%async_computation | async-start | bytes 393216 | tf_op jit(solution)/shard_map/all_to_all | solution.py:88
  58.4 2.2 collective-permute-start
  60.6 1.4 constant_dynamic-update-slice_fusion.1
  62.0 10.6 %all-to-all-done = f32[16,1,3072]{2,1,0:T(1,128)S(1)} async-done(((f32[16,1,3072]{2,1,0:T(1,128)}), f32[16,1,3072]{2,1,0:T(1,128)S(1)}, u32[]{:S(2)}, u32[]{:S(2)}) %all-to-all-start) | async-done | bytes 196640 | tf_op jit(solution)/shard_map/all_to_all | solution.py:88
  72.6 1.6 broadcast_in_dim.57
  74.2 4.4 %all-to-all-start.4 = ((bf16[4,8,2,256,64]{3,4,1,2,0:T(8,128)(2,1)}), bf16[4,8,2,256,64]{3,4,1,2,0:T(8,128)(2,1)}, u32[]{:S(2)}, u32[]{:S(2)}) async-start(bf16[4,8,2,256,64]{3,4,1,2,0:T(8,128)(2,1)} %broadcast_in_dim.57), calls=%async_computation.4 | async-start | bytes 4194304 | tf_op jit(solution)/shard_map/all_to_all | solution.py:54
  78.6 1.3 constant_dynamic-update-slice_fusion
  81.9 1.8 reduce.7
  83.7 1.0 reshape.277
  85.8 2.2 collective-permute-start.1
  88.0 1.3 fusion.12
  89.4 3.3 %collective-permute-done.1 = f32[8,1,32,32]{2,3,0,1:T(8,128)S(1)} collective-permute-done((f32[8,1,32,32]{2,3,0,1:T(8,128)S(1)}, f32[8,1,32,32]{2,3,0,1:T(8,128)S(1)}, u32[]{:S(2)}, u32[]{:S(2)}) %collective-permute-start.1) | collective-permute-done | bytes 32800 | tf_op jit(solution)/shard_map/ppermute | solution.py:19
  92.7 11.9 %all-to-all-done.4 = bf16[4,8,2,256,64]{3,4,1,2,0:T(8,128)(2,1)} async-done(((bf16[4,8,2,256,64]{3,4,1,2,0:T(8,128)(2,1)}), bf16[4,8,2,256,64]{3,4,1,2,0:T(8,128)(2,1)}, u32[]{:S(2)}, u32[]{:S(2)}) %all-to-all-start.4) | async-done | bytes 2097184 | tf_op jit(solution)/shard_map/all_to_all | solution.py:54
  104.6 1.7 copy.82
  106.3 1.3 fusion.53
  108.6 6.0 %all-to-all-start.6 = ((f32[16,1,1024]{2,1,0:T(1,128)}), f32[16,1,1024]{2,1,0:T(1,128)S(1)}, u32[]{:S(2)}, u32[]{:S(2)}) async-start(f32[16,1,1024]{2,1,0:T(1,128)} %reshape.280), calls=%async_computation.6 | async-start | bytes 131072 | tf_op jit(solution)/shard_map/all_to_all | solution.py:88
  114.7 10.0 %all-to-all-done.6 = f32[16,1,1024]{2,1,0:T(1,128)S(1)} async-done(((f32[16,1,1024]{2,1,0:T(1,128)}), f32[16,1,1024]{2,1,0:T(1,128)S(1)}, u32[]{:S(2)}, u32[]{:S(2)}) %all-to-all-start.6) | async-done | bytes 65568 | tf_op jit(solution)/shard_map/all_to_all | solution.py:88
  125.6 1.4 fusion.19
  127.8 4.9 %all-to-all-start.1 = ((f32[16,1,1024]{2,1,0:T(1,128)}), f32[16,1,1024]{2,1,0:T(1,128)}, u32[]{:S(2)}, u32[]{:S(2)}) async-start(f32[16,1,1024]{2,1,0:T(1,128)} %reshape.278), calls=%async_computation.1 | async-start | bytes 131072 | tf_op jit(solution)/shard_map/all_to_all | solution.py:96
  132.7 1.4 fusion.11
  134.1 1.1 fusion.44
  135.2 7.7 %all-to-all-done.1 = f32[16,1,1024]{2,1,0:T(1,128)} async-done(((f32[16,1,1024]{2,1,0:T(1,128)}), f32[16,1,1024]{2,1,0:T(1,128)}, u32[]{:S(2)}, u32[]{:S(2)}) %all-to-all-start.1) | async-done | bytes 65568 | tf_op jit(solution)/shard_map/all_to_all | solution.py:96
  142.9 1.6 reduce.8
  144.8 3.5 %fusion.15 = f32[4096,256]{1,0:T(8,128)S(1)} fusion(f32[128,4096]{1,0:T(8,128)S(1)} %constant_dynamic-update-slice_fusion, f32[256,64]{0,1:T(8,128)S(1)} %copy.79, f32[256,64]{0,1:T(8,128)S(1)} %get-tuple-element.17), kind=kOutput, calls=%fused_computation.39 | convolution fusion | flops 1610645504 | bytes 6422528 | tf_op jit(solution)/shard_map/dot_general | solution.py:137
  148.3 2.3 copy.80
  150.5 5.0 %all-to-all-start.2 = ((f32[2,4,8,64,256]{4,3,2,0,1:T(8,128)}), f32[2,4,8,64,256]{4,3,2,0,1:T(8,128)}, u32[]{:S(2)}, u32[]{:S(2)}) async-start(f32[2,4,8,64,256]{4,3,2,0,1:T(8,128)} %copy.80), calls=%async_computation.2 | async-start | bytes 8388608 | tf_op jit(solution)/shard_map/all_to_all | solution.py:35
  156.3 2.4 collective-permute-start.5
  159.1 4.0 %collective-permute-done.5 = f32[8,1,32,33]{2,3,0,1:T(8,128)S(1)} collective-permute-done((f32[8,1,32,33]{2,3,0,1:T(8,128)S(1)}, f32[8,1,32,33]{2,3,0,1:T(8,128)S(1)}, u32[]{:S(2)}, u32[]{:S(2)}) %collective-permute-start.5) | collective-permute-done | bytes 33824 | tf_op jit(solution)/shard_map/ppermute | solution.py:19
  164.0 0.9 reshape.282
  164.9 38.5 %all-to-all-done.2 = f32[2,4,8,64,256]{4,3,2,0,1:T(8,128)} async-done(((f32[2,4,8,64,256]{4,3,2,0,1:T(8,128)}), f32[2,4,8,64,256]{4,3,2,0,1:T(8,128)}, u32[]{:S(2)}, u32[]{:S(2)}) %all-to-all-start.2) | async-done | bytes 4194336 | tf_op jit(solution)/shard_map/all_to_all | solution.py:35
  203.4 5.5 %all-to-all-start.7 = ((f32[16,1,3072]{2,1,0:T(1,128)}), f32[16,1,3072]{2,1,0:T(1,128)S(1)}, u32[]{:S(2)}, u32[]{:S(2)}) async-start(f32[16,1,3072]{2,1,0:T(1,128)} %reshape.282), calls=%async_computation.7 | async-start | bytes 393216 | tf_op jit(solution)/shard_map/all_to_all | solution.py:96
  208.9 2.2 collective-permute-start.3
  211.2 7.7 %collective-permute-done.3 = f32[1,1,256,257]{2,3,1,0:T(8,128)S(1)} collective-permute-done((f32[1,1,256,257]{2,3,1,0:T(8,128)S(1)}, f32[1,1,256,257]{2,3,1,0:T(8,128)S(1)}, u32[]{:S(2)}, u32[]{:S(2)}) %collective-permute-start.3) | collective-permute-done | bytes 263200 | tf_op jit(solution)/shard_map/ppermute | solution.py:19
  219.2 2.7 reduce_sum.56
  221.9 1.1 copy.83
  223.6 3.6 %all-to-all-start.5 = ((f32[2,8,64,256]{3,2,0,1:T(8,128)}), f32[2,8,64,256]{3,2,0,1:T(8,128)S(1)}, u32[]{:S(2)}, u32[]{:S(2)}) async-start(f32[2,8,64,256]{3,2,0,1:T(8,128)} %copy.83), calls=%async_computation.5 | async-start | bytes 2097152 | tf_op jit(solution)/shard_map/all_to_all | solution.py:39
  227.1 1.1 reduce.9
  228.9 1.0 fusion.2
  229.9 1.0 fusion.3
  230.9 25.4 %all-to-all-done.5 = f32[2,8,64,256]{3,2,0,1:T(8,128)S(1)} async-done(((f32[2,8,64,256]{3,2,0,1:T(8,128)}), f32[2,8,64,256]{3,2,0,1:T(8,128)S(1)}, u32[]{:S(2)}, u32[]{:S(2)}) %all-to-all-start.5) | async-done | bytes 1048608 | tf_op jit(solution)/shard_map/all_to_all | solution.py:39
  256.4 11.6 %collective-permute-start.4 = (f32[64,256]{1,0:T(8,128)S(1)}, f32[64,256]{1,0:T(8,128)S(1)}, u32[]{:S(2)}, u32[]{:S(2)}) collective-permute-start(f32[64,256]{1,0:T(8,128)S(1)} %dynamic-slice_bitcast_fusion), channel_id=1, source_target_pairs={{0,32},{32,0},{1,33},{33,1},{2,34},{34,2},{3,35},{35,3},{4,36},{36... | collective-permute-start | bytes 196616 | tf_op jit(solution)/shard_map/ppermute | solution.py:19
  268.6 1.7 collective-permute-done.4
  (82 shorter events, 13.3 us)
Async XLA Ops:
  0.6 31.2 %copy-start.5 = (f32[256,64]{0,1:T(8,128)S(1)}, f32[256,64]{0,1:T(8,128)}, u32[]{:S(2)}) copy-start(f32[256,64]{0,1:T(8,128)} %param.8) | copy-start | bytes 196612
  0.6 31.3 %copy-start.3 = (f32[256,64]{0,1:T(8,128)S(1)}, f32[256,64]{0,1:T(8,128)}, u32[]{:S(2)}) copy-start(f32[256,64]{0,1:T(8,128)} %param.9) | copy-start | bytes 196612
  0.7 21.7 %collective-permute-start.2 = (bf16[256,64]{0,1:T(8,128)(2,1)}, bf16[256,64]{0,1:T(8,128)(2,1)S(1)}, u32[]{:S(2)}, u32[]{:S(2)}) collective-permute-start(bf16[256,64]{0,1:T(8,128)(2,1)} %param.13), channel_id=1, source_target_pairs={{0,32},{32,0},{1,33},{33,1},{2,34},{34,2},{3,35},{35,3},{4,36},{36... | collective-permute-start | bytes 98312 | tf_op jit(solution)/shard_map/ppermute | solution.py:19
  24.0 34.0 %copy-start.7 = (f32[256,64]{0,1:T(8,128)S(1)}, f32[256,64]{0,1:T(8,128)}, u32[]{:S(2)}) copy-start(f32[256,64]{0,1:T(8,128)} %param.7) | copy-start | bytes 196612
  24.0 20.1 %all-to-all-start.3 = ((bf16[8,2,256,64]{2,3,1,0:T(8,128)(2,1)}), bf16[8,2,256,64]{2,3,1,0:T(8,128)(2,1)S(1)}, u32[]{:S(2)}, u32[]{:S(2)}) async-start(bf16[8,2,256,64]{2,3,1,0:T(8,128)(2,1)} %broadcast_in_dim.56), calls=%async_computation.3 | async-start | bytes 1048576 | tf_op jit(solution)/shard_map/all_to_all | solution.py:54
  44.1 14.3 %copy-start = (bf16[8,2,256,64]{2,3,1,0:T(8,128)(2,1)}, bf16[8,2,256,64]{2,3,1,0:T(8,128)(2,1)S(1)}, u32[]{:S(2)}) copy-start(bf16[8,2,256,64]{2,3,1,0:T(8,128)(2,1)S(1)} %all-to-all-done.3) | copy-start | bytes 1572868
  44.1 28.5 %all-to-all-start = ((f32[16,1,3072]{2,1,0:T(1,128)}), f32[16,1,3072]{2,1,0:T(1,128)S(1)}, u32[]{:S(2)}, u32[]{:S(2)}) async-start(f32[16,1,3072]{2,1,0:T(1,128)} %reshape.276), calls=%async_computation | async-start | bytes 393216 | tf_op jit(solution)/shard_map/all_to_all | solution.py:88
  58.4 22.2 %collective-permute-start = (f32[1,1,256,256]{2,3,1,0:T(8,128)S(1)}, f32[1,1,256,256]{2,3,1,0:T(8,128)S(1)}, u32[]{:S(2)}, u32[]{:S(2)}) collective-permute-start(f32[1,1,256,256]{2,3,1,0:T(8,128)S(1)} %convolution_bitcast_fusion.1), channel_id=1, source_target_pairs={{0,1},{1,0},{2,3},{3,2},{4,5},{5,4},{6,7},{7,6},{8,9},{9,8},{10,11... | collective-permute-start | bytes 786440 | tf_op jit(solution)/shard_map/ppermute | solution.py:19
  60.6 1.4 copy-start.1
  74.2 30.4 %all-to-all-start.4 = ((bf16[4,8,2,256,64]{3,4,1,2,0:T(8,128)(2,1)}), bf16[4,8,2,256,64]{3,4,1,2,0:T(8,128)(2,1)}, u32[]{:S(2)}, u32[]{:S(2)}) async-start(bf16[4,8,2,256,64]{3,4,1,2,0:T(8,128)(2,1)} %broadcast_in_dim.57), calls=%async_computation.4 | async-start | bytes 4194304 | tf_op jit(solution)/shard_map/all_to_all | solution.py:54
  78.6 1.3 copy-start.9
  85.8 6.8 %collective-permute-start.1 = (f32[8,1,32,32]{2,3,0,1:T(8,128)S(1)}, f32[8,1,32,32]{2,3,0,1:T(8,128)S(1)}, u32[]{:S(2)}, u32[]{:S(2)}) collective-permute-start(f32[8,1,32,32]{2,3,0,1:T(8,128)S(1)} %convolution_bitcast_fusion.4), channel_id=1, source_target_pairs={{0,1},{1,0},{2,3},{3,2},{4,5},{5,4},{6,7},{7,6},{8,9},{9,8},{10,11... | collective-permute-start | bytes 98312 | tf_op jit(solution)/shard_map/ppermute | solution.py:19
  108.6 16.1 %all-to-all-start.6 = ((f32[16,1,1024]{2,1,0:T(1,128)}), f32[16,1,1024]{2,1,0:T(1,128)S(1)}, u32[]{:S(2)}, u32[]{:S(2)}) async-start(f32[16,1,1024]{2,1,0:T(1,128)} %reshape.280), calls=%async_computation.6 | async-start | bytes 131072 | tf_op jit(solution)/shard_map/all_to_all | solution.py:88
  127.8 15.1 %all-to-all-start.1 = ((f32[16,1,1024]{2,1,0:T(1,128)}), f32[16,1,1024]{2,1,0:T(1,128)}, u32[]{:S(2)}, u32[]{:S(2)}) async-start(f32[16,1,1024]{2,1,0:T(1,128)} %reshape.278), calls=%async_computation.1 | async-start | bytes 131072 | tf_op jit(solution)/shard_map/all_to_all | solution.py:96
  150.5 5.0 %copy-start.4 = (f32[256,64]{0,1:T(8,128)S(1)}, f32[256,64]{0,1:T(8,128)}, u32[]{:S(2)}) copy-start(f32[256,64]{0,1:T(8,128)} %param.9) | copy-start | bytes 196612
  150.5 5.4 %copy-start.2 = (f32[32,8,1,64]{3,1,0,2:T(8,128)S(1)}, f32[32,8,1,64]{3,1,0,2:T(8,128)}, u32[]{:S(2)}) copy-start(f32[32,8,1,64]{3,1,0,2:T(8,128)} %get-tuple-element.11) | copy-start | bytes 196612
  150.5 52.9 %all-to-all-start.2 = ((f32[2,4,8,64,256]{4,3,2,0,1:T(8,128)}), f32[2,4,8,64,256]{4,3,2,0,1:T(8,128)}, u32[]{:S(2)}, u32[]{:S(2)}) async-start(f32[2,4,8,64,256]{4,3,2,0,1:T(8,128)} %copy.80), calls=%async_computation.2 | async-start | bytes 8388608 | tf_op jit(solution)/shard_map/all_to_all | solution.py:35
  156.3 6.7 %collective-permute-start.5 = (f32[8,1,32,33]{2,3,0,1:T(8,128)S(1)}, f32[8,1,32,33]{2,3,0,1:T(8,128)S(1)}, u32[]{:S(2)}, u32[]{:S(2)}) collective-permute-start(f32[8,1,32,33]{2,3,0,1:T(8,128)S(1)} %pad_maximum_fusion.3), channel_id=1, source_target_pairs={{0,1},{1,0},{2,3},{3,2},{4,5},{5,4},{6,7},{7,6},{8,9},{9,8},{10,11... | collective-permute-start | bytes 101384 | tf_op jit(solution)/shard_map/ppermute | solution.py:19
  163.5 55.4 %copy-start.6 = (f32[256,64]{0,1:T(8,128)S(1)}, f32[256,64]{0,1:T(8,128)}, u32[]{:S(2)}) copy-start(f32[256,64]{0,1:T(8,128)} %param.8) | copy-start | bytes 196612
  203.4 20.2 %all-to-all-start.7 = ((f32[16,1,3072]{2,1,0:T(1,128)}), f32[16,1,3072]{2,1,0:T(1,128)S(1)}, u32[]{:S(2)}, u32[]{:S(2)}) async-start(f32[16,1,3072]{2,1,0:T(1,128)} %reshape.282), calls=%async_computation.7 | async-start | bytes 393216 | tf_op jit(solution)/shard_map/all_to_all | solution.py:96
  208.9 9.9 %collective-permute-start.3 = (f32[1,1,256,257]{2,3,1,0:T(8,128)S(1)}, f32[1,1,256,257]{2,3,1,0:T(8,128)S(1)}, u32[]{:S(2)}, u32[]{:S(2)}) collective-permute-start(f32[1,1,256,257]{2,3,1,0:T(8,128)S(1)} %pad_maximum_fusion.2), channel_id=1, source_target_pairs={{0,1},{1,0},{2,3},{3,2},{4,5},{5,4},{6,7},{7,6},{8,9},{9,8},{10,11... | collective-permute-start | bytes 789512 | tf_op jit(solution)/shard_map/ppermute | solution.py:19
  223.6 32.7 %all-to-all-start.5 = ((f32[2,8,64,256]{3,2,0,1:T(8,128)}), f32[2,8,64,256]{3,2,0,1:T(8,128)S(1)}, u32[]{:S(2)}, u32[]{:S(2)}) async-start(f32[2,8,64,256]{3,2,0,1:T(8,128)} %copy.83), calls=%async_computation.5 | async-start | bytes 2097152 | tf_op jit(solution)/shard_map/all_to_all | solution.py:39
  228.3 1.6 copy-start.8
  256.4 13.9 %collective-permute-start.4 = (f32[64,256]{1,0:T(8,128)S(1)}, f32[64,256]{1,0:T(8,128)S(1)}, u32[]{:S(2)}, u32[]{:S(2)}) collective-permute-start(f32[64,256]{1,0:T(8,128)S(1)} %dynamic-slice_bitcast_fusion), channel_id=1, source_target_pairs={{0,32},{32,0},{1,33},{33,1},{2,34},{34,2},{3,35},{35,3},{4,36},{36... | collective-permute-start | bytes 196616 | tf_op jit(solution)/shard_map/ppermute | solution.py:19

commit v10 on v9

--- a/solution.py
+++ b/solution.py
@@ -165,6 +165,7 @@
     strided_grads = jnp.stack(
         [from_runs(dq_strided), from_runs(dk_strided), from_runs(dv_strided)], axis=1
     )
+    strided_grads, dq_local = lax.optimization_barrier((strided_grads, dq_local))
     grads_home = to_contiguous(strided_grads)
     grad_queries = dq_local.reshape(tok_rows, head_dim) + grads_home[:, 0]
     grad_keys = dk_local.reshape(tok_rows, head_dim) + grads_home[:, 1]

time: 272 us -> 278 us (1.022); the launches traced: 271 us -> 274 us
    all_to_all x2, waiting for transfers between devices: 8.27 us -> 21.3 us  [to_contiguous(): lax.all_to_all(layout, 'seq', split_axis=0, concat_axis=2, tiled=True)]
    ppermute x6, waiting for transfers between devices: 18.3 us -> 12.5 us  [swapped(): lax.ppermute(x, axis, [(i, i ^ 1 << distance) for i in range(lax.axis_siz...]
    all_to_all x1, waiting for transfers between devices: 38.5 us -> 33.9 us  [scatter_head(): return (lax.all_to_all(parts, 'x', 1, 1, tiled=True).sum(1), companion)]
    unnamed x35 -> x33, local copies, waits for them, and re-layouts: 7.41 us -> 7.42 us
  transfers between devices with their start and end apart: 14 -> 14, of which waited for: 13 -> 13; matrix products, arithmetic and copies ran while one was open for 10% -> 9% of each run, Pallas kernels for 0% -> 0%
where the time goes in v10:
time: 278 us; the launch traced here: 274 us
  waiting for transfers between devices  136 us (49%)
  starting transfers between devices  91.5 us (33%)
  local copies, waits for them, and re-layouts  19 us (7%)
  other arithmetic  14 us (5%)
  matrix products  12.1 us (4%)
    ppermute x6, starting transfers between devices, swapped(): lax.ppermute(x, axis, [(i, i ^ 1 << distance) for i in range(lax.axis_siz...  41.5 us
    all_to_all x1, waiting for transfers between devices, scatter_head(): return (lax.all_to_all(parts, 'x', 1, 1, tiled=True).sum(1), companion)  33.9 us
    all_to_all x1, waiting for transfers between devices, finish_scatter(): parts = lax.all_to_all(parts, 'y', 1, 1, tiled=True).sum(1)  24.7 us
    all_to_all x2, waiting for transfers between devices, gather_head(): stacked = lax.all_to_all(copies, axis, 0, 0, tiled=True)  22.8 us
    all_to_all x2, waiting for transfers between devices, to_contiguous(): lax.all_to_all(layout, 'seq', split_axis=0, concat_axis=2, tiled=True)  21.3 us
    all_to_all x2, waiting for transfers between devices, to_strided(): lax.all_to_all(layout, 'seq', split_axis=1, concat_axis=0, tiled=True)  20.5 us
    all_to_all x2, starting transfers between devices, to_strided(): lax.all_to_all(layout, 'seq', split_axis=1, concat_axis=0, tiled=True)  19.9 us
    ppermute x6, waiting for transfers between devices, swapped(): lax.ppermute(x, axis, [(i, i ^ 1 << distance) for i in range(lax.axis_siz...  12.5 us
  transfers between devices with their start and end apart: 14, of which 13 were waited for; matrix products, arithmetic and copies ran while one was open for 9% of the time, Pallas kernels for 0%

profile of v10, /device:TPU:1, one launch (start us, length us, event | category | flops | bytes accessed | tf_op | source)
XLA Modules:
  0.0 273.6 jit_solution(11988497488565537915)
XLA Ops:
  0.7 20.0 %collective-permute-start.2 = (bf16[256,64]{0,1:T(8,128)(2,1)}, bf16[256,64]{0,1:T(8,128)(2,1)S(1)}, u32[]{:S(2)}, u32[]{:S(2)}) collective-permute-start(bf16[256,64]{0,1:T(8,128)(2,1)} %param.13), channel_id=1, source_target_pairs={{0,32},{32,0},{1,33},{33,1},{2,34},{34,2},{3,35},{35,3},{4,36},{36... | collective-permute-start | bytes 98312 | tf_op jit(solution)/shard_map/ppermute | solution.py:19
  20.7 1.6 collective-permute-done.2
  24.0 6.8 %all-to-all-start.3 = ((bf16[8,2,256,64]{2,3,1,0:T(8,128)(2,1)}), bf16[8,2,256,64]{2,3,1,0:T(8,128)(2,1)S(1)}, u32[]{:S(2)}, u32[]{:S(2)}) async-start(bf16[8,2,256,64]{2,3,1,0:T(8,128)(2,1)} %broadcast_in_dim.56), calls=%async_computation.3 | async-start | bytes 1048576 | tf_op jit(solution)/shard_map/all_to_all | solution.py:54
  30.8 0.9 copy.69
  33.0 10.9 %all-to-all-done.3 = bf16[8,2,256,64]{2,3,1,0:T(8,128)(2,1)S(1)} async-done(((bf16[8,2,256,64]{2,3,1,0:T(8,128)(2,1)}), bf16[8,2,256,64]{2,3,1,0:T(8,128)(2,1)S(1)}, u32[]{:S(2)}, u32[]{:S(2)}) %all-to-all-start.3) | async-done | bytes 524320 | tf_op jit(solution)/shard_map/all_to_all | solution.py:54
  43.9 13.9 %all-to-all-start = ((f32[16,1,3072]{2,1,0:T(1,128)}), f32[16,1,3072]{2,1,0:T(1,128)S(1)}, u32[]{:S(2)}, u32[]{:S(2)}) async-start(f32[16,1,3072]{2,1,0:T(1,128)} %reshape.273), calls=%async_computation | async-start | bytes 393216 | tf_op jit(solution)/shard_map/all_to_all | solution.py:88
  58.2 2.2 collective-permute-start
  60.5 1.4 constant_dynamic-update-slice_fusion.1
  61.9 10.6 %all-to-all-done = f32[16,1,3072]{2,1,0:T(1,128)S(1)} async-done(((f32[16,1,3072]{2,1,0:T(1,128)}), f32[16,1,3072]{2,1,0:T(1,128)S(1)}, u32[]{:S(2)}, u32[]{:S(2)}) %all-to-all-start) | async-done | bytes 196640 | tf_op jit(solution)/shard_map/all_to_all | solution.py:88
  72.5 1.6 broadcast_in_dim.57
  74.0 4.4 %all-to-all-start.4 = ((bf16[4,8,2,256,64]{3,4,1,2,0:T(8,128)(2,1)}), bf16[4,8,2,256,64]{3,4,1,2,0:T(8,128)(2,1)}, u32[]{:S(2)}, u32[]{:S(2)}) async-start(bf16[4,8,2,256,64]{3,4,1,2,0:T(8,128)(2,1)} %broadcast_in_dim.57), calls=%async_computation.4 | async-start | bytes 4194304 | tf_op jit(solution)/shard_map/all_to_all | solution.py:54
  78.5 1.3 constant_dynamic-update-slice_fusion
  81.7 1.8 reduce.7
  83.5 1.0 reshape.274
  85.7 2.2 collective-permute-start.1
  87.9 1.3 fusion.12
  89.2 3.3 %collective-permute-done.1 = f32[8,1,32,32]{2,3,0,1:T(8,128)S(1)} collective-permute-done((f32[8,1,32,32]{2,3,0,1:T(8,128)S(1)}, f32[8,1,32,32]{2,3,0,1:T(8,128)S(1)}, u32[]{:S(2)}, u32[]{:S(2)}) %collective-permute-start.1) | collective-permute-done | bytes 32800 | tf_op jit(solution)/shard_map/ppermute | solution.py:19
  92.6 11.9 %all-to-all-done.4 = bf16[4,8,2,256,64]{3,4,1,2,0:T(8,128)(2,1)} async-done(((bf16[4,8,2,256,64]{3,4,1,2,0:T(8,128)(2,1)}), bf16[4,8,2,256,64]{3,4,1,2,0:T(8,128)(2,1)}, u32[]{:S(2)}, u32[]{:S(2)}) %all-to-all-start.4) | async-done | bytes 2097184 | tf_op jit(solution)/shard_map/all_to_all | solution.py:54
  104.5 1.7 copy.82
  106.2 1.3 fusion.53
  108.5 6.0 %all-to-all-start.6 = ((f32[16,1,1024]{2,1,0:T(1,128)}), f32[16,1,1024]{2,1,0:T(1,128)S(1)}, u32[]{:S(2)}, u32[]{:S(2)}) async-start(f32[16,1,1024]{2,1,0:T(1,128)} %reshape.277), calls=%async_computation.6 | async-start | bytes 131072 | tf_op jit(solution)/shard_map/all_to_all | solution.py:88
  114.6 10.0 %all-to-all-done.6 = f32[16,1,1024]{2,1,0:T(1,128)S(1)} async-done(((f32[16,1,1024]{2,1,0:T(1,128)}), f32[16,1,1024]{2,1,0:T(1,128)S(1)}, u32[]{:S(2)}, u32[]{:S(2)}) %all-to-all-start.6) | async-done | bytes 65568 | tf_op jit(solution)/shard_map/all_to_all | solution.py:88
  125.4 1.4 fusion.19
  127.6 4.9 %all-to-all-start.1 = ((f32[16,1,1024]{2,1,0:T(1,128)}), f32[16,1,1024]{2,1,0:T(1,128)}, u32[]{:S(2)}, u32[]{:S(2)}) async-start(f32[16,1,1024]{2,1,0:T(1,128)} %reshape.275), calls=%async_computation.1 | async-start | bytes 131072 | tf_op jit(solution)/shard_map/all_to_all | solution.py:96
  132.5 1.4 fusion.11
  134.0 1.1 fusion.44
  135.1 7.7 %all-to-all-done.1 = f32[16,1,1024]{2,1,0:T(1,128)} async-done(((f32[16,1,1024]{2,1,0:T(1,128)}), f32[16,1,1024]{2,1,0:T(1,128)}, u32[]{:S(2)}, u32[]{:S(2)}) %all-to-all-start.1) | async-done | bytes 65568 | tf_op jit(solution)/shard_map/all_to_all | solution.py:96
  142.8 1.6 reduce.8
  144.7 3.5 %fusion.15 = f32[4096,256]{1,0:T(8,128)S(1)} fusion(f32[128,4096]{1,0:T(8,128)S(1)} %constant_dynamic-update-slice_fusion, f32[256,64]{0,1:T(8,128)S(1)} %copy.79, f32[256,64]{0,1:T(8,128)S(1)} %get-tuple-element.21), kind=kOutput, calls=%fused_computation.39 | convolution fusion | flops 1610645504 | bytes 6422528 | tf_op jit(solution)/shard_map/dot_general | solution.py:137
  148.1 2.3 copy.80
  150.4 5.0 %all-to-all-start.2 = ((f32[2,4,8,64,256]{4,3,2,0,1:T(8,128)}), f32[2,4,8,64,256]{4,3,2,0,1:T(8,128)}, u32[]{:S(2)}, u32[]{:S(2)}) async-start(f32[2,4,8,64,256]{4,3,2,0,1:T(8,128)} %copy.80), calls=%async_computation.2 | async-start | bytes 8388608 | tf_op jit(solution)/shard_map/all_to_all | solution.py:35
  155.9 2.2 collective-permute-start.3
  158.4 3.3 %collective-permute-start.5 = (f32[8,1,32,33]{2,3,0,1:T(8,128)S(1)}, f32[8,1,32,33]{2,3,0,1:T(8,128)S(1)}, u32[]{:S(2)}, u32[]{:S(2)}) collective-permute-start(f32[8,1,32,33]{2,3,0,1:T(8,128)S(1)} %pad_maximum_fusion.3), channel_id=1, source_target_pairs={{0,1},{1,0},{2,3},{3,2},{4,5},{5,4},{6,7},{7,6},{8,9},{9,8},{10,11... | collective-permute-start | bytes 101384 | tf_op jit(solution)/shard_map/ppermute | solution.py:19
  162.0 2.8 %collective-permute-done.3 = f32[1,1,256,257]{2,3,1,0:T(8,128)S(1)} collective-permute-done((f32[1,1,256,257]{2,3,1,0:T(8,128)S(1)}, f32[1,1,256,257]{2,3,1,0:T(8,128)S(1)}, u32[]{:S(2)}, u32[]{:S(2)}) %collective-permute-start.3) | collective-permute-done | bytes 263200 | tf_op jit(solution)/shard_map/ppermute | solution.py:19
  165.2 3.1 %collective-permute-done.5 = f32[8,1,32,33]{2,3,0,1:T(8,128)S(1)} collective-permute-done((f32[8,1,32,33]{2,3,0,1:T(8,128)S(1)}, f32[8,1,32,33]{2,3,0,1:T(8,128)S(1)}, u32[]{:S(2)}, u32[]{:S(2)}) %collective-permute-start.5) | collective-permute-done | bytes 33824 | tf_op jit(solution)/shard_map/ppermute | solution.py:19
  169.4 33.9 %all-to-all-done.2 = f32[2,4,8,64,256]{4,3,2,0,1:T(8,128)} async-done(((f32[2,4,8,64,256]{4,3,2,0,1:T(8,128)}), f32[2,4,8,64,256]{4,3,2,0,1:T(8,128)}, u32[]{:S(2)}, u32[]{:S(2)}) %all-to-all-start.2) | async-done | bytes 4194336 | tf_op jit(solution)/shard_map/all_to_all | solution.py:35
  203.3 2.7 reduce_sum.56
  206.0 0.9 reshape.279
  206.9 5.5 %all-to-all-start.7 = ((f32[16,1,3072]{2,1,0:T(1,128)}), f32[16,1,3072]{2,1,0:T(1,128)S(1)}, u32[]{:S(2)}, u32[]{:S(2)}) async-start(f32[16,1,3072]{2,1,0:T(1,128)} %reshape.279), calls=%async_computation.7 | async-start | bytes 393216 | tf_op jit(solution)/shard_map/all_to_all | solution.py:96
  212.4 1.1 copy.83
  213.5 13.6 %all-to-all-done.7 = f32[16,1,3072]{2,1,0:T(1,128)S(1)} async-done(((f32[16,1,3072]{2,1,0:T(1,128)}), f32[16,1,3072]{2,1,0:T(1,128)S(1)}, u32[]{:S(2)}, u32[]{:S(2)}) %all-to-all-start.7) | async-done | bytes 196640 | tf_op jit(solution)/shard_map/all_to_all | solution.py:96
  227.1 3.6 %all-to-all-start.5 = ((f32[2,8,64,256]{3,2,0,1:T(8,128)}), f32[2,8,64,256]{3,2,0,1:T(8,128)S(1)}, u32[]{:S(2)}, u32[]{:S(2)}) async-start(f32[2,8,64,256]{3,2,0,1:T(8,128)} %copy.83), calls=%async_computation.5 | async-start | bytes 2097152 | tf_op jit(solution)/shard_map/all_to_all | solution.py:39
  230.6 1.1 reduce.9
  232.3 1.0 fusion.2
  233.3 1.0 fusion.3
  234.4 24.7 %all-to-all-done.5 = f32[2,8,64,256]{3,2,0,1:T(8,128)S(1)} async-done(((f32[2,8,64,256]{3,2,0,1:T(8,128)}), f32[2,8,64,256]{3,2,0,1:T(8,128)S(1)}, u32[]{:S(2)}, u32[]{:S(2)}) %all-to-all-start.5) | async-done | bytes 1048608 | tf_op jit(solution)/shard_map/all_to_all | solution.py:39
  259.2 11.6 %collective-permute-start.4 = (f32[64,256]{1,0:T(8,128)S(1)}, f32[64,256]{1,0:T(8,128)S(1)}, u32[]{:S(2)}, u32[]{:S(2)}) collective-permute-start(f32[64,256]{1,0:T(8,128)S(1)} %dynamic-slice_bitcast_fusion), channel_id=1, source_target_pairs={{0,32},{32,0},{1,33},{33,1},{2,34},{34,2},{3,35},{35,3},{4,36},{36... | collective-permute-start | bytes 196616 | tf_op jit(solution)/shard_map/ppermute | solution.py:19
  271.4 1.6 collective-permute-done.4
  (80 shorter events, 13.6 us)
Async XLA Ops:
  0.6 31.1 %copy-start.4 = (f32[256,64]{0,1:T(8,128)S(1)}, f32[256,64]{0,1:T(8,128)}, u32[]{:S(2)}) copy-start(f32[256,64]{0,1:T(8,128)} %param.8) | copy-start | bytes 196612
  0.6 31.2 %copy-start.6 = (f32[256,64]{0,1:T(8,128)S(1)}, f32[256,64]{0,1:T(8,128)}, u32[]{:S(2)}) copy-start(f32[256,64]{0,1:T(8,128)} %param.7) | copy-start | bytes 196612
  0.7 21.7 %collective-permute-start.2 = (bf16[256,64]{0,1:T(8,128)(2,1)}, bf16[256,64]{0,1:T(8,128)(2,1)S(1)}, u32[]{:S(2)}, u32[]{:S(2)}) collective-permute-start(bf16[256,64]{0,1:T(8,128)(2,1)} %param.13), channel_id=1, source_target_pairs={{0,32},{32,0},{1,33},{33,1},{2,34},{34,2},{3,35},{35,3},{4,36},{36... | collective-permute-start | bytes 98312 | tf_op jit(solution)/shard_map/ppermute | solution.py:19
  24.0 20.0 %all-to-all-start.3 = ((bf16[8,2,256,64]{2,3,1,0:T(8,128)(2,1)}), bf16[8,2,256,64]{2,3,1,0:T(8,128)(2,1)S(1)}, u32[]{:S(2)}, u32[]{:S(2)}) async-start(bf16[8,2,256,64]{2,3,1,0:T(8,128)(2,1)} %broadcast_in_dim.56), calls=%async_computation.3 | async-start | bytes 1048576 | tf_op jit(solution)/shard_map/all_to_all | solution.py:54
  43.9 14.3 %copy-start = (bf16[8,2,256,64]{2,3,1,0:T(8,128)(2,1)}, bf16[8,2,256,64]{2,3,1,0:T(8,128)(2,1)S(1)}, u32[]{:S(2)}) copy-start(bf16[8,2,256,64]{2,3,1,0:T(8,128)(2,1)S(1)} %all-to-all-done.3) | copy-start | bytes 1572868
  43.9 28.5 %all-to-all-start = ((f32[16,1,3072]{2,1,0:T(1,128)}), f32[16,1,3072]{2,1,0:T(1,128)S(1)}, u32[]{:S(2)}, u32[]{:S(2)}) async-start(f32[16,1,3072]{2,1,0:T(1,128)} %reshape.273), calls=%async_computation | async-start | bytes 393216 | tf_op jit(solution)/shard_map/all_to_all | solution.py:88
  58.2 22.2 %collective-permute-start = (f32[1,1,256,256]{2,3,1,0:T(8,128)S(1)}, f32[1,1,256,256]{2,3,1,0:T(8,128)S(1)}, u32[]{:S(2)}, u32[]{:S(2)}) collective-permute-start(f32[1,1,256,256]{2,3,1,0:T(8,128)S(1)} %convolution_bitcast_fusion.1), channel_id=1, source_target_pairs={{0,1},{1,0},{2,3},{3,2},{4,5},{5,4},{6,7},{7,6},{8,9},{9,8},{10,11... | collective-permute-start | bytes 786440 | tf_op jit(solution)/shard_map/ppermute | solution.py:19
  60.5 1.4 copy-start.1
  74.0 30.4 %all-to-all-start.4 = ((bf16[4,8,2,256,64]{3,4,1,2,0:T(8,128)(2,1)}), bf16[4,8,2,256,64]{3,4,1,2,0:T(8,128)(2,1)}, u32[]{:S(2)}, u32[]{:S(2)}) async-start(bf16[4,8,2,256,64]{3,4,1,2,0:T(8,128)(2,1)} %broadcast_in_dim.57), calls=%async_computation.4 | async-start | bytes 4194304 | tf_op jit(solution)/shard_map/all_to_all | solution.py:54
  78.5 1.3 copy-start.8
  85.7 6.8 %collective-permute-start.1 = (f32[8,1,32,32]{2,3,0,1:T(8,128)S(1)}, f32[8,1,32,32]{2,3,0,1:T(8,128)S(1)}, u32[]{:S(2)}, u32[]{:S(2)}) collective-permute-start(f32[8,1,32,32]{2,3,0,1:T(8,128)S(1)} %convolution_bitcast_fusion.4), channel_id=1, source_target_pairs={{0,1},{1,0},{2,3},{3,2},{4,5},{5,4},{6,7},{7,6},{8,9},{9,8},{10,11... | collective-permute-start | bytes 98312 | tf_op jit(solution)/shard_map/ppermute | solution.py:19
  108.5 16.1 %all-to-all-start.6 = ((f32[16,1,1024]{2,1,0:T(1,128)}), f32[16,1,1024]{2,1,0:T(1,128)S(1)}, u32[]{:S(2)}, u32[]{:S(2)}) async-start(f32[16,1,1024]{2,1,0:T(1,128)} %reshape.277), calls=%async_computation.6 | async-start | bytes 131072 | tf_op jit(solution)/shard_map/all_to_all | solution.py:88
  127.6 15.1 %all-to-all-start.1 = ((f32[16,1,1024]{2,1,0:T(1,128)}), f32[16,1,1024]{2,1,0:T(1,128)}, u32[]{:S(2)}, u32[]{:S(2)}) async-start(f32[16,1,1024]{2,1,0:T(1,128)} %reshape.275), calls=%async_computation.1 | async-start | bytes 131072 | tf_op jit(solution)/shard_map/all_to_all | solution.py:96
  150.4 5.0 %copy-start.3 = (f32[256,64]{0,1:T(8,128)S(1)}, f32[256,64]{0,1:T(8,128)}, u32[]{:S(2)}) copy-start(f32[256,64]{0,1:T(8,128)} %param.9) | copy-start | bytes 196612
  150.4 7.7 %copy-start.2 = (f32[32,8,1,64]{3,1,0,2:T(8,128)S(1)}, f32[32,8,1,64]{3,1,0,2:T(8,128)}, u32[]{:S(2)}) copy-start(f32[32,8,1,64]{3,1,0,2:T(8,128)} %get-tuple-element.15) | copy-start | bytes 196612
  150.4 52.9 %all-to-all-start.2 = ((f32[2,4,8,64,256]{4,3,2,0,1:T(8,128)}), f32[2,4,8,64,256]{4,3,2,0,1:T(8,128)}, u32[]{:S(2)}, u32[]{:S(2)}) async-start(f32[2,4,8,64,256]{4,3,2,0,1:T(8,128)} %copy.80), calls=%async_computation.2 | async-start | bytes 8388608 | tf_op jit(solution)/shard_map/all_to_all | solution.py:35
  155.4 9.5 %copy-start.5 = (f32[256,64]{0,1:T(8,128)S(1)}, f32[256,64]{0,1:T(8,128)}, u32[]{:S(2)}) copy-start(f32[256,64]{0,1:T(8,128)} %param.8) | copy-start | bytes 196612
  155.9 9.0 %collective-permute-start.3 = (f32[1,1,256,257]{2,3,1,0:T(8,128)S(1)}, f32[1,1,256,257]{2,3,1,0:T(8,128)S(1)}, u32[]{:S(2)}, u32[]{:S(2)}) collective-permute-start(f32[1,1,256,257]{2,3,1,0:T(8,128)S(1)} %pad_maximum_fusion.2), channel_id=1, source_target_pairs={{0,1},{1,0},{2,3},{3,2},{4,5},{5,4},{6,7},{7,6},{8,9},{9,8},{10,11... | collective-permute-start | bytes 789512 | tf_op jit(solution)/shard_map/ppermute | solution.py:19
  158.4 9.9 %collective-permute-start.5 = (f32[8,1,32,33]{2,3,0,1:T(8,128)S(1)}, f32[8,1,32,33]{2,3,0,1:T(8,128)S(1)}, u32[]{:S(2)}, u32[]{:S(2)}) collective-permute-start(f32[8,1,32,33]{2,3,0,1:T(8,128)S(1)} %pad_maximum_fusion.3), channel_id=1, source_target_pairs={{0,1},{1,0},{2,3},{3,2},{4,5},{5,4},{6,7},{7,6},{8,9},{9,8},{10,11... | collective-permute-start | bytes 101384 | tf_op jit(solution)/shard_map/ppermute | solution.py:19
  206.9 20.2 %all-to-all-start.7 = ((f32[16,1,3072]{2,1,0:T(1,128)}), f32[16,1,3072]{2,1,0:T(1,128)S(1)}, u32[]{:S(2)}, u32[]{:S(2)}) async-start(f32[16,1,3072]{2,1,0:T(1,128)} %reshape.279), calls=%async_computation.7 | async-start | bytes 393216 | tf_op jit(solution)/shard_map/all_to_all | solution.py:96
  227.1 32.0 %all-to-all-start.5 = ((f32[2,8,64,256]{3,2,0,1:T(8,128)}), f32[2,8,64,256]{3,2,0,1:T(8,128)S(1)}, u32[]{:S(2)}, u32[]{:S(2)}) async-start(f32[2,8,64,256]{3,2,0,1:T(8,128)} %copy.83), calls=%async_computation.5 | async-start | bytes 2097152 | tf_op jit(solution)/shard_map/all_to_all | solution.py:39
  231.7 1.6 copy-start.7
  259.2 13.8 %collective-permute-start.4 = (f32[64,256]{1,0:T(8,128)S(1)}, f32[64,256]{1,0:T(8,128)S(1)}, u32[]{:S(2)}, u32[]{:S(2)}) collective-permute-start(f32[64,256]{1,0:T(8,128)S(1)} %dynamic-slice_bitcast_fusion), channel_id=1, source_target_pairs={{0,32},{32,0},{1,33},{33,1},{2,34},{34,2},{3,35},{35,3},{4,36},{36... | collective-permute-start | bytes 196616 | tf_op jit(solution)/shard_map/ppermute | solution.py:19

commit v11 on v9

--- a/solution.py
+++ b/solution.py
@@ -38,9 +38,7 @@
 def finish_scatter(parts):
     parts = lax.all_to_all(parts, "y", 1, 1, tiled=True).sum(1)
     own = lax.axis_index("zh")
-    kept = lax.dynamic_index_in_dim(parts, own, 0, keepdims=False)
-    sent = lax.dynamic_index_in_dim(parts, 1 - own, 0, keepdims=False)
-    return kept + swapped(sent, "zh", 0)
+    return lax.dynamic_index_in_dim(parts + swapped(parts, "zh", 0), own, 0, keepdims=False)
 
 
 def gather_head(piece):

time: 272 us -> 275 us (1.011)
  no operation moved by 1% of the time
where the time goes in v11:
time: 275 us; the launch traced here: 272 us
  waiting for transfers between devices  135 us (49%)
  starting transfers between devices  90.8 us (33%)
  local copies, waits for them, and re-layouts  19 us (7%)
  other arithmetic  14 us (5%)
  matrix products  12.1 us (4%)
    ppermute x6, starting transfers between devices, swapped(): lax.ppermute(x, axis, [(i, i ^ 1 << distance) for i in range(lax.axis_siz...  40.6 us
    all_to_all x1, waiting for transfers between devices, scatter_head(): return (lax.all_to_all(parts, 'x', 1, 1, tiled=True).sum(1), companion)  38.5 us
    all_to_all x1, waiting for transfers between devices, finish_scatter(): parts = lax.all_to_all(parts, 'y', 1, 1, tiled=True).sum(1)  25.4 us
    all_to_all x2, waiting for transfers between devices, gather_head(): stacked = lax.all_to_all(copies, axis, 0, 0, tiled=True)  22.8 us
    all_to_all x2, waiting for transfers between devices, to_strided(): lax.all_to_all(layout, 'seq', split_axis=1, concat_axis=0, tiled=True)  20.5 us
    all_to_all x2, starting transfers between devices, to_strided(): lax.all_to_all(layout, 'seq', split_axis=1, concat_axis=0, tiled=True)  19.9 us
    ppermute x6, waiting for transfers between devices, swapped(): lax.ppermute(x, axis, [(i, i ^ 1 << distance) for i in range(lax.axis_siz...  19.6 us
    all_to_all x2, starting transfers between devices, gather_head(): stacked = lax.all_to_all(copies, axis, 0, 0, tiled=True)  11.4 us
  transfers between devices with their start and end apart: 14, of which 13 were waited for; matrix products, arithmetic and copies ran while one was open for 10% of the time, Pallas kernels for 0%

profile of v11, /device:TPU:1, one launch (start us, length us, event | category | flops | bytes accessed | tf_op | source)
XLA Modules:
  0.0 272.2 jit_solution(18050122988116646144)
XLA Ops:
  0.7 20.0 %collective-permute-start.2 = (bf16[256,64]{0,1:T(8,128)(2,1)}, bf16[256,64]{0,1:T(8,128)(2,1)S(1)}, u32[]{:S(2)}, u32[]{:S(2)}) collective-permute-start(bf16[256,64]{0,1:T(8,128)(2,1)} %param.13), channel_id=1, source_target_pairs={{0,32},{32,0},{1,33},{33,1},{2,34},{34,2},{3,35},{35,3},{4,36},{36... | collective-permute-start | bytes 98312 | tf_op jit(solution)/shard_map/ppermute | solution.py:19
  20.7 1.6 collective-permute-done.2
  24.0 7.0 %all-to-all-start.3 = ((bf16[8,2,256,64]{2,3,1,0:T(8,128)(2,1)}), bf16[8,2,256,64]{2,3,1,0:T(8,128)(2,1)S(1)}, u32[]{:S(2)}, u32[]{:S(2)}) async-start(bf16[8,2,256,64]{2,3,1,0:T(8,128)(2,1)} %broadcast_in_dim.56), calls=%async_computation.3 | async-start | bytes 1048576 | tf_op jit(solution)/shard_map/all_to_all | solution.py:52
  30.9 0.9 copy.67
  32.2 0.9 reshape.276
  33.1 10.9 %all-to-all-done.3 = bf16[8,2,256,64]{2,3,1,0:T(8,128)(2,1)S(1)} async-done(((bf16[8,2,256,64]{2,3,1,0:T(8,128)(2,1)}), bf16[8,2,256,64]{2,3,1,0:T(8,128)(2,1)S(1)}, u32[]{:S(2)}, u32[]{:S(2)}) %all-to-all-start.3) | async-done | bytes 524320 | tf_op jit(solution)/shard_map/all_to_all | solution.py:52
  44.1 13.9 %all-to-all-start = ((f32[16,1,3072]{2,1,0:T(1,128)}), f32[16,1,3072]{2,1,0:T(1,128)S(1)}, u32[]{:S(2)}, u32[]{:S(2)}) async-start(f32[16,1,3072]{2,1,0:T(1,128)} %reshape.276), calls=%async_computation | async-start | bytes 393216 | tf_op jit(solution)/shard_map/all_to_all | solution.py:86
  58.4 2.2 collective-permute-start
  60.6 1.4 constant_dynamic-update-slice_fusion.1
  62.0 10.6 %all-to-all-done = f32[16,1,3072]{2,1,0:T(1,128)S(1)} async-done(((f32[16,1,3072]{2,1,0:T(1,128)}), f32[16,1,3072]{2,1,0:T(1,128)S(1)}, u32[]{:S(2)}, u32[]{:S(2)}) %all-to-all-start) | async-done | bytes 196640 | tf_op jit(solution)/shard_map/all_to_all | solution.py:86
  72.6 1.6 broadcast_in_dim.57
  74.2 4.4 %all-to-all-start.4 = ((bf16[4,8,2,256,64]{3,4,1,2,0:T(8,128)(2,1)}), bf16[4,8,2,256,64]{3,4,1,2,0:T(8,128)(2,1)}, u32[]{:S(2)}, u32[]{:S(2)}) async-start(bf16[4,8,2,256,64]{3,4,1,2,0:T(8,128)(2,1)} %broadcast_in_dim.57), calls=%async_computation.4 | async-start | bytes 4194304 | tf_op jit(solution)/shard_map/all_to_all | solution.py:52
  78.6 1.3 constant_dynamic-update-slice_fusion
  81.9 1.8 reduce.7
  83.7 1.0 reshape.277
  85.8 2.2 collective-permute-start.1
  88.0 1.3 fusion.12
  89.4 3.3 %collective-permute-done.1 = f32[8,1,32,32]{2,3,0,1:T(8,128)S(1)} collective-permute-done((f32[8,1,32,32]{2,3,0,1:T(8,128)S(1)}, f32[8,1,32,32]{2,3,0,1:T(8,128)S(1)}, u32[]{:S(2)}, u32[]{:S(2)}) %collective-permute-start.1) | collective-permute-done | bytes 32800 | tf_op jit(solution)/shard_map/ppermute | solution.py:19
  92.7 11.9 %all-to-all-done.4 = bf16[4,8,2,256,64]{3,4,1,2,0:T(8,128)(2,1)} async-done(((bf16[4,8,2,256,64]{3,4,1,2,0:T(8,128)(2,1)}), bf16[4,8,2,256,64]{3,4,1,2,0:T(8,128)(2,1)}, u32[]{:S(2)}, u32[]{:S(2)}) %all-to-all-start.4) | async-done | bytes 2097184 | tf_op jit(solution)/shard_map/all_to_all | solution.py:52
  104.6 1.7 copy.82
  106.3 1.3 fusion.53
  108.6 6.0 %all-to-all-start.6 = ((f32[16,1,1024]{2,1,0:T(1,128)}), f32[16,1,1024]{2,1,0:T(1,128)S(1)}, u32[]{:S(2)}, u32[]{:S(2)}) async-start(f32[16,1,1024]{2,1,0:T(1,128)} %reshape.280), calls=%async_computation.6 | async-start | bytes 131072 | tf_op jit(solution)/shard_map/all_to_all | solution.py:86
  114.7 10.0 %all-to-all-done.6 = f32[16,1,1024]{2,1,0:T(1,128)S(1)} async-done(((f32[16,1,1024]{2,1,0:T(1,128)}), f32[16,1,1024]{2,1,0:T(1,128)S(1)}, u32[]{:S(2)}, u32[]{:S(2)}) %all-to-all-start.6) | async-done | bytes 65568 | tf_op jit(solution)/shard_map/all_to_all | solution.py:86
  125.6 1.4 fusion.19
  127.8 4.9 %all-to-all-start.1 = ((f32[16,1,1024]{2,1,0:T(1,128)}), f32[16,1,1024]{2,1,0:T(1,128)}, u32[]{:S(2)}, u32[]{:S(2)}) async-start(f32[16,1,1024]{2,1,0:T(1,128)} %reshape.278), calls=%async_computation.1 | async-start | bytes 131072 | tf_op jit(solution)/shard_map/all_to_all | solution.py:94
  132.7 1.4 fusion.11
  134.1 1.1 fusion.44
  135.2 7.7 %all-to-all-done.1 = f32[16,1,1024]{2,1,0:T(1,128)} async-done(((f32[16,1,1024]{2,1,0:T(1,128)}), f32[16,1,1024]{2,1,0:T(1,128)}, u32[]{:S(2)}, u32[]{:S(2)}) %all-to-all-start.1) | async-done | bytes 65568 | tf_op jit(solution)/shard_map/all_to_all | solution.py:94
  142.9 1.6 reduce.8
  144.8 3.5 %fusion.15 = f32[4096,256]{1,0:T(8,128)S(1)} fusion(f32[128,4096]{1,0:T(8,128)S(1)} %constant_dynamic-update-slice_fusion, f32[256,64]{0,1:T(8,128)S(1)} %copy.79, f32[256,64]{0,1:T(8,128)S(1)} %get-tuple-element.17), kind=kOutput, calls=%fused_computation.39 | convolution fusion | flops 1610645504 | bytes 6422528 | tf_op jit(solution)/shard_map/dot_general | solution.py:135
  148.3 2.3 copy.80
  150.5 5.0 %all-to-all-start.2 = ((f32[2,4,8,64,256]{4,3,2,0,1:T(8,128)}), f32[2,4,8,64,256]{4,3,2,0,1:T(8,128)}, u32[]{:S(2)}, u32[]{:S(2)}) async-start(f32[2,4,8,64,256]{4,3,2,0,1:T(8,128)} %copy.80), calls=%async_computation.2 | async-start | bytes 8388608 | tf_op jit(solution)/shard_map/all_to_all | solution.py:35
  156.3 2.4 collective-permute-start.5
  159.1 4.0 %collective-permute-done.5 = f32[8,1,32,33]{2,3,0,1:T(8,128)S(1)} collective-permute-done((f32[8,1,32,33]{2,3,0,1:T(8,128)S(1)}, f32[8,1,32,33]{2,3,0,1:T(8,128)S(1)}, u32[]{:S(2)}, u32[]{:S(2)}) %collective-permute-start.5) | collective-permute-done | bytes 33824 | tf_op jit(solution)/shard_map/ppermute | solution.py:19
  164.0 0.9 reshape.282
  164.9 38.5 %all-to-all-done.2 = f32[2,4,8,64,256]{4,3,2,0,1:T(8,128)} async-done(((f32[2,4,8,64,256]{4,3,2,0,1:T(8,128)}), f32[2,4,8,64,256]{4,3,2,0,1:T(8,128)}, u32[]{:S(2)}, u32[]{:S(2)}) %all-to-all-start.2) | async-done | bytes 4194336 | tf_op jit(solution)/shard_map/all_to_all | solution.py:35
  203.4 5.5 %all-to-all-start.7 = ((f32[16,1,3072]{2,1,0:T(1,128)}), f32[16,1,3072]{2,1,0:T(1,128)S(1)}, u32[]{:S(2)}, u32[]{:S(2)}) async-start(f32[16,1,3072]{2,1,0:T(1,128)} %reshape.282), calls=%async_computation.7 | async-start | bytes 393216 | tf_op jit(solution)/shard_map/all_to_all | solution.py:94
  208.9 2.2 collective-permute-start.3
  211.2 7.7 %collective-permute-done.3 = f32[1,1,256,257]{2,3,1,0:T(8,128)S(1)} collective-permute-done((f32[1,1,256,257]{2,3,1,0:T(8,128)S(1)}, f32[1,1,256,257]{2,3,1,0:T(8,128)S(1)}, u32[]{:S(2)}, u32[]{:S(2)}) %collective-permute-start.3) | collective-permute-done | bytes 263200 | tf_op jit(solution)/shard_map/ppermute | solution.py:19
  219.3 2.7 reduce_sum.56
  221.9 1.1 copy.83
  223.6 3.6 %all-to-all-start.5 = ((f32[2,8,64,256]{3,2,0,1:T(8,128)}), f32[2,8,64,256]{3,2,0,1:T(8,128)S(1)}, u32[]{:S(2)}, u32[]{:S(2)}) async-start(f32[2,8,64,256]{3,2,0,1:T(8,128)} %copy.83), calls=%async_computation.5 | async-start | bytes 2097152 | tf_op jit(solution)/shard_map/all_to_all | solution.py:39
  227.1 1.1 reduce.9
  228.8 1.0 fusion.2
  229.9 1.0 fusion.3
  230.9 25.4 %all-to-all-done.5 = f32[2,8,64,256]{3,2,0,1:T(8,128)S(1)} async-done(((f32[2,8,64,256]{3,2,0,1:T(8,128)}), f32[2,8,64,256]{3,2,0,1:T(8,128)S(1)}, u32[]{:S(2)}, u32[]{:S(2)}) %all-to-all-start.5) | async-done | bytes 1048608 | tf_op jit(solution)/shard_map/all_to_all | solution.py:39
  256.4 11.6 %collective-permute-start.4 = (f32[2,64,256]{2,1,0:T(8,128)S(1)}, f32[2,64,256]{2,1,0:T(8,128)S(1)}, u32[]{:S(2)}, u32[]{:S(2)}) collective-permute-start(f32[2,64,256]{2,1,0:T(8,128)S(1)} %reduce_sum.58), channel_id=1, source_target_pairs={{0,32},{32,0},{1,33},{33,1},{2,34},{34,2},{3,35},{35,3},{4,36},{36... | collective-permute-start | bytes 393224 | tf_op jit(solution)/shard_map/ppermute | solution.py:19
  268.6 3.0 %collective-permute-done.4 = f32[2,64,256]{2,1,0:T(8,128)S(1)} collective-permute-done((f32[2,64,256]{2,1,0:T(8,128)S(1)}, f32[2,64,256]{2,1,0:T(8,128)S(1)}, u32[]{:S(2)}, u32[]{:S(2)}) %collective-permute-start.4) | collective-permute-done | bytes 131104 | tf_op jit(solution)/shard_map/ppermute | solution.py:19
  (81 shorter events, 13.3 us)
Async XLA Ops:
  0.6 31.2 %copy-start.5 = (f32[256,64]{0,1:T(8,128)S(1)}, f32[256,64]{0,1:T(8,128)}, u32[]{:S(2)}) copy-start(f32[256,64]{0,1:T(8,128)} %param.8) | copy-start | bytes 196612
  0.6 31.3 %copy-start.3 = (f32[256,64]{0,1:T(8,128)S(1)}, f32[256,64]{0,1:T(8,128)}, u32[]{:S(2)}) copy-start(f32[256,64]{0,1:T(8,128)} %param.9) | copy-start | bytes 196612
  0.7 21.7 %collective-permute-start.2 = (bf16[256,64]{0,1:T(8,128)(2,1)}, bf16[256,64]{0,1:T(8,128)(2,1)S(1)}, u32[]{:S(2)}, u32[]{:S(2)}) collective-permute-start(bf16[256,64]{0,1:T(8,128)(2,1)} %param.13), channel_id=1, source_target_pairs={{0,32},{32,0},{1,33},{33,1},{2,34},{34,2},{3,35},{35,3},{4,36},{36... | collective-permute-start | bytes 98312 | tf_op jit(solution)/shard_map/ppermute | solution.py:19
  24.0 34.0 %copy-start.7 = (f32[256,64]{0,1:T(8,128)S(1)}, f32[256,64]{0,1:T(8,128)}, u32[]{:S(2)}) copy-start(f32[256,64]{0,1:T(8,128)} %param.7) | copy-start | bytes 196612
  24.0 20.1 %all-to-all-start.3 = ((bf16[8,2,256,64]{2,3,1,0:T(8,128)(2,1)}), bf16[8,2,256,64]{2,3,1,0:T(8,128)(2,1)S(1)}, u32[]{:S(2)}, u32[]{:S(2)}) async-start(bf16[8,2,256,64]{2,3,1,0:T(8,128)(2,1)} %broadcast_in_dim.56), calls=%async_computation.3 | async-start | bytes 1048576 | tf_op jit(solution)/shard_map/all_to_all | solution.py:52
  44.1 14.3 %copy-start = (bf16[8,2,256,64]{2,3,1,0:T(8,128)(2,1)}, bf16[8,2,256,64]{2,3,1,0:T(8,128)(2,1)S(1)}, u32[]{:S(2)}) copy-start(bf16[8,2,256,64]{2,3,1,0:T(8,128)(2,1)S(1)} %all-to-all-done.3) | copy-start | bytes 1572868
  44.1 28.5 %all-to-all-start = ((f32[16,1,3072]{2,1,0:T(1,128)}), f32[16,1,3072]{2,1,0:T(1,128)S(1)}, u32[]{:S(2)}, u32[]{:S(2)}) async-start(f32[16,1,3072]{2,1,0:T(1,128)} %reshape.276), calls=%async_computation | async-start | bytes 393216 | tf_op jit(solution)/shard_map/all_to_all | solution.py:86
  58.4 22.2 %collective-permute-start = (f32[1,1,256,256]{2,3,1,0:T(8,128)S(1)}, f32[1,1,256,256]{2,3,1,0:T(8,128)S(1)}, u32[]{:S(2)}, u32[]{:S(2)}) collective-permute-start(f32[1,1,256,256]{2,3,1,0:T(8,128)S(1)} %convolution_bitcast_fusion.1), channel_id=1, source_target_pairs={{0,1},{1,0},{2,3},{3,2},{4,5},{5,4},{6,7},{7,6},{8,9},{9,8},{10,11... | collective-permute-start | bytes 786440 | tf_op jit(solution)/shard_map/ppermute | solution.py:19
  60.6 1.4 copy-start.1
  74.2 30.4 %all-to-all-start.4 = ((bf16[4,8,2,256,64]{3,4,1,2,0:T(8,128)(2,1)}), bf16[4,8,2,256,64]{3,4,1,2,0:T(8,128)(2,1)}, u32[]{:S(2)}, u32[]{:S(2)}) async-start(bf16[4,8,2,256,64]{3,4,1,2,0:T(8,128)(2,1)} %broadcast_in_dim.57), calls=%async_computation.4 | async-start | bytes 4194304 | tf_op jit(solution)/shard_map/all_to_all | solution.py:52
  78.6 1.3 copy-start.9
  85.8 6.8 %collective-permute-start.1 = (f32[8,1,32,32]{2,3,0,1:T(8,128)S(1)}, f32[8,1,32,32]{2,3,0,1:T(8,128)S(1)}, u32[]{:S(2)}, u32[]{:S(2)}) collective-permute-start(f32[8,1,32,32]{2,3,0,1:T(8,128)S(1)} %convolution_bitcast_fusion.4), channel_id=1, source_target_pairs={{0,1},{1,0},{2,3},{3,2},{4,5},{5,4},{6,7},{7,6},{8,9},{9,8},{10,11... | collective-permute-start | bytes 98312 | tf_op jit(solution)/shard_map/ppermute | solution.py:19
  108.6 16.1 %all-to-all-start.6 = ((f32[16,1,1024]{2,1,0:T(1,128)}), f32[16,1,1024]{2,1,0:T(1,128)S(1)}, u32[]{:S(2)}, u32[]{:S(2)}) async-start(f32[16,1,1024]{2,1,0:T(1,128)} %reshape.280), calls=%async_computation.6 | async-start | bytes 131072 | tf_op jit(solution)/shard_map/all_to_all | solution.py:86
  127.8 15.1 %all-to-all-start.1 = ((f32[16,1,1024]{2,1,0:T(1,128)}), f32[16,1,1024]{2,1,0:T(1,128)}, u32[]{:S(2)}, u32[]{:S(2)}) async-start(f32[16,1,1024]{2,1,0:T(1,128)} %reshape.278), calls=%async_computation.1 | async-start | bytes 131072 | tf_op jit(solution)/shard_map/all_to_all | solution.py:94
  150.5 5.0 %copy-start.4 = (f32[256,64]{0,1:T(8,128)S(1)}, f32[256,64]{0,1:T(8,128)}, u32[]{:S(2)}) copy-start(f32[256,64]{0,1:T(8,128)} %param.9) | copy-start | bytes 196612
  150.5 5.4 %copy-start.2 = (f32[32,8,1,64]{3,1,0,2:T(8,128)S(1)}, f32[32,8,1,64]{3,1,0,2:T(8,128)}, u32[]{:S(2)}) copy-start(f32[32,8,1,64]{3,1,0,2:T(8,128)} %get-tuple-element.11) | copy-start | bytes 196612
  150.5 52.9 %all-to-all-start.2 = ((f32[2,4,8,64,256]{4,3,2,0,1:T(8,128)}), f32[2,4,8,64,256]{4,3,2,0,1:T(8,128)}, u32[]{:S(2)}, u32[]{:S(2)}) async-start(f32[2,4,8,64,256]{4,3,2,0,1:T(8,128)} %copy.80), calls=%async_computation.2 | async-start | bytes 8388608 | tf_op jit(solution)/shard_map/all_to_all | solution.py:35
  156.3 6.7 %collective-permute-start.5 = (f32[8,1,32,33]{2,3,0,1:T(8,128)S(1)}, f32[8,1,32,33]{2,3,0,1:T(8,128)S(1)}, u32[]{:S(2)}, u32[]{:S(2)}) collective-permute-start(f32[8,1,32,33]{2,3,0,1:T(8,128)S(1)} %pad_maximum_fusion.3), channel_id=1, source_target_pairs={{0,1},{1,0},{2,3},{3,2},{4,5},{5,4},{6,7},{7,6},{8,9},{9,8},{10,11... | collective-permute-start | bytes 101384 | tf_op jit(solution)/shard_map/ppermute | solution.py:19
  163.5 55.5 %copy-start.6 = (f32[256,64]{0,1:T(8,128)S(1)}, f32[256,64]{0,1:T(8,128)}, u32[]{:S(2)}) copy-start(f32[256,64]{0,1:T(8,128)} %param.8) | copy-start | bytes 196612
  203.4 20.2 %all-to-all-start.7 = ((f32[16,1,3072]{2,1,0:T(1,128)}), f32[16,1,3072]{2,1,0:T(1,128)S(1)}, u32[]{:S(2)}, u32[]{:S(2)}) async-start(f32[16,1,3072]{2,1,0:T(1,128)} %reshape.282), calls=%async_computation.7 | async-start | bytes 393216 | tf_op jit(solution)/shard_map/all_to_all | solution.py:94
  208.9 9.9 %collective-permute-start.3 = (f32[1,1,256,257]{2,3,1,0:T(8,128)S(1)}, f32[1,1,256,257]{2,3,1,0:T(8,128)S(1)}, u32[]{:S(2)}, u32[]{:S(2)}) collective-permute-start(f32[1,1,256,257]{2,3,1,0:T(8,128)S(1)} %pad_maximum_fusion.2), channel_id=1, source_target_pairs={{0,1},{1,0},{2,3},{3,2},{4,5},{5,4},{6,7},{7,6},{8,9},{9,8},{10,11... | collective-permute-start | bytes 789512 | tf_op jit(solution)/shard_map/ppermute | solution.py:19
  223.6 32.7 %all-to-all-start.5 = ((f32[2,8,64,256]{3,2,0,1:T(8,128)}), f32[2,8,64,256]{3,2,0,1:T(8,128)S(1)}, u32[]{:S(2)}, u32[]{:S(2)}) async-start(f32[2,8,64,256]{3,2,0,1:T(8,128)} %copy.83), calls=%async_computation.5 | async-start | bytes 2097152 | tf_op jit(solution)/shard_map/all_to_all | solution.py:39
  228.3 1.6 copy-start.8
  256.4 15.2 %collective-permute-start.4 = (f32[2,64,256]{2,1,0:T(8,128)S(1)}, f32[2,64,256]{2,1,0:T(8,128)S(1)}, u32[]{:S(2)}, u32[]{:S(2)}) collective-permute-start(f32[2,64,256]{2,1,0:T(8,128)S(1)} %reduce_sum.58), channel_id=1, source_target_pairs={{0,32},{32,0},{1,33},{33,1},{2,34},{34,2},{3,35},{35,3},{4,36},{36... | collective-permute-start | bytes 393224 | tf_op jit(solution)/shard_map/ppermute | solution.py:19
